TPU v7x, 256 devices: a whole 4x4x8 slice. The times are simulated.
256 devices in a mesh: pipe: 8 (over y, core), ctx: 32 (over x, z).
Axes of the slice: x: 4, y: 4, z: 8, core: 2. Of those that a mesh axis runs over, the one named last changes fastest.
Arguments:
- queries: bfloat16 [8, 4096, 4096], P('pipe', 'ctx'), may hold values from -240 to 240
- keys: bfloat16 [8, 4096, 4096], P('pipe', 'ctx'), may hold values from -6 to 6
- values: bfloat16 [8, 4096, 4096], P('pipe', 'ctx'), may hold values from -6 to 6
- attn_out: bfloat16 [8, 4096, 4096], P('pipe', 'ctx'), may hold values from -3 to 3
- out_grad: bfloat16 [8, 4096, 4096], P('pipe', 'ctx'), may hold values from -24 to 24
- random_blocks: int32 [8, 32, 64, 3], P('pipe', 'ctx'), may hold values from 0 to 63
- global_blocks: int32 [8, 2], P('pipe'), may hold values from 0 to 63, as said below
- radius: int32 [8, 32], P('pipe', 'ctx'), may hold values from 1 to 2, as said below
Outputs:
- grad_queries: bfloat16 [8, 4096, 4096], P('pipe', 'ctx')
- grad_keys: bfloat16 [8, 4096, 4096], P('pipe', 'ctx')
- grad_values: bfloat16 [8, 4096, 4096], P('pipe', 'ctx')
Inputs may be any that keep to these rules, and one draw needn't show every extreme that they name: `global_blocks`: the 2 entries of a section differ. In every section some head has radius 2 and some head has radius 1.
All inputs are finite; a program needn't handle non-finite values.
Results may differ from a plain program's by a relative error of at most 0.0049.
Values may be sent and summed in bfloat16 or wider, within the bound.
No kernel may reach another device: no remote copies, remote signals or barrier semaphores. Data moves between devices by JAX's collectives and lax.ppermute only.
A program may use at most 64 MiB of HBM per device.

v0:
```python
import jax
import jax.numpy as jnp
from jax import lax
from jax.sharding import PartitionSpec as P

HD = 128
BLK = 64
RMAX = 2
NR = 3
QG = 8
KB = 10


def passed_along(value, axis, steps):
    count = lax.axis_size(axis)
    pairs = [(source, (source + steps) % count) for source in range(count)]
    return lax.ppermute(value, axis, pairs)


def slot_table(random_list, global_list, head_radius, block_count):
    blocks = jnp.arange(block_count, dtype=jnp.int32)[:, None]
    offsets = jnp.arange(-RMAX, RMAX + 1, dtype=jnp.int32)[None, :]
    window = blocks + offsets
    window_ok = (jnp.abs(offsets) <= head_radius) & (window >= 0) & (window < block_count)
    window = jnp.clip(window, 0, block_count - 1)
    global_slots = jnp.broadcast_to(global_list[None, :], (block_count, global_list.shape[0]))
    global_ok = jnp.abs(global_slots - blocks) > head_radius
    random_ok = jnp.abs(random_list - blocks) > head_radius
    random_ok = random_ok & jnp.all(random_list[:, :, None] != global_list[None, None, :], axis=2)
    earlier = jnp.arange(NR)[None, :] < jnp.arange(NR)[:, None]
    repeated = jnp.any((random_list[:, :, None] == random_list[:, None, :]) & earlier[None], axis=2)
    random_ok = random_ok & jnp.logical_not(repeated)
    slot_index = jnp.concatenate([window, global_slots, random_list], axis=1)
    slot_valid = jnp.concatenate([window_ok, global_ok, random_ok], axis=1)
    return (slot_index, slot_valid)


def lane_sums(first, second):
    product = first.astype(jnp.float32) * second.astype(jnp.float32)
    flat = product.reshape(-1, product.shape[-1])
    ones_column = jnp.ones((product.shape[-1],), jnp.float32)
    summed = jnp.dot(
        flat, ones_column, precision=lax.Precision.HIGHEST, preferred_element_type=jnp.float32
    )
    return summed.reshape(product.shape[:-1])


def head_grads(
    query_rows,
    key_rows,
    value_rows,
    grad_rows,
    correction_rows,
    random_list,
    global_list,
    head_radius,
):
    block_count = query_rows.shape[0] // BLK
    score_scale = HD ** (-0.5)
    slot_index, slot_valid = slot_table(random_list, global_list, head_radius, block_count)
    query_blocks = query_rows.reshape(block_count, BLK, HD)
    key_blocks = key_rows.reshape(block_count, BLK, HD)
    value_blocks = value_rows.reshape(block_count, BLK, HD)
    grad_blocks = grad_rows.reshape(block_count, BLK, HD)
    correction = correction_rows.reshape(block_count, BLK)
    block_ids = jnp.arange(block_count, dtype=jnp.int32)[:, None]

    def one_group(totals, first_block):
        key_total, value_total = totals
        group_index = lax.dynamic_slice_in_dim(slot_index, first_block, QG, 0)
        group_valid = lax.dynamic_slice_in_dim(slot_valid, first_block, QG, 0)
        group_query = lax.dynamic_slice_in_dim(query_blocks, first_block, QG, 0)
        group_grad = lax.dynamic_slice_in_dim(grad_blocks, first_block, QG, 0)
        group_corr = lax.dynamic_slice_in_dim(correction, first_block, QG, 0)
        key_tiles = key_blocks[group_index].reshape(QG, KB * BLK, HD)
        value_tiles = value_blocks[group_index].reshape(QG, KB * BLK, HD)
        key_live = jnp.repeat(group_valid, BLK, axis=1)
        scores = (
            jnp.einsum("bid,bjd->bij", group_query, key_tiles, preferred_element_type=jnp.float32)
            * score_scale
        )
        scores = jnp.where(key_live[:, None, :], scores, -jnp.inf)
        row_max = jnp.max(scores, axis=-1, keepdims=True)
        weights = jnp.exp(scores - row_max)
        attention = weights / jnp.sum(weights, axis=-1, keepdims=True)
        attention_low = attention.astype(jnp.bfloat16)
        dprobs = jnp.einsum(
            "bid,bjd->bij", group_grad, value_tiles, preferred_element_type=jnp.float32
        )
        dscores_low = (attention * (dprobs - group_corr[:, :, None])).astype(jnp.bfloat16)
        query_grad = (
            jnp.einsum("bij,bjd->bid", dscores_low, key_tiles, preferred_element_type=jnp.float32)
            * score_scale
        ).astype(jnp.bfloat16)
        key_part = jnp.einsum(
            "bij,bid->bjd", dscores_low, group_query, preferred_element_type=jnp.float32
        ).reshape(QG * KB, BLK * HD)
        value_part = jnp.einsum(
            "bij,bid->bjd", attention_low, group_grad, preferred_element_type=jnp.float32
        ).reshape(QG * KB, BLK * HD)
        flat_index = group_index.reshape(1, -1)
        placing = (block_ids == flat_index).astype(jnp.float32)
        key_total = key_total + jnp.dot(
            placing, key_part, precision=lax.Precision.HIGHEST, preferred_element_type=jnp.float32
        )
        value_total = value_total + jnp.dot(
            placing, value_part, precision=lax.Precision.HIGHEST, preferred_element_type=jnp.float32
        )
        return ((key_total, value_total), query_grad)

    starts = jnp.arange(block_count // QG) * QG
    empty = jnp.zeros((block_count, BLK * HD), jnp.float32)
    (key_total, value_total), query_grad = lax.scan(one_group, (empty, empty), starts)
    query_grad = query_grad.reshape(block_count * BLK, HD)
    key_grad = (key_total * score_scale).astype(jnp.bfloat16).reshape(block_count * BLK, HD)
    value_grad = value_total.astype(jnp.bfloat16).reshape(block_count * BLK, HD)
    return (query_grad, key_grad, value_grad)


def body(queries, keys, values, attn_out, out_grad, random_blocks, global_blocks, radius):
    head_query, head_key, head_value, head_output, head_grad = (
        lax.all_to_all(queries, "ctx", split_axis=2, concat_axis=1, tiled=True),
        lax.all_to_all(keys, "ctx", split_axis=2, concat_axis=1, tiled=True),
        lax.all_to_all(values, "ctx", split_axis=2, concat_axis=1, tiled=True),
        lax.all_to_all(attn_out, "ctx", split_axis=2, concat_axis=1, tiled=True),
        lax.all_to_all(out_grad, "ctx", split_axis=2, concat_axis=1, tiled=True),
    )
    length = head_query.shape[1]
    local_heads = head_query.shape[2] // HD
    correction = lane_sums(
        head_output.reshape(1, length, local_heads, HD),
        head_grad.reshape(1, length, local_heads, HD),
    )
    local_heads = head_query.shape[2] // HD
    columns = slice(0, HD)
    query_grad, key_grad, value_grad = head_grads(
        head_query[0, :, columns],
        head_key[0, :, columns],
        head_value[0, :, columns],
        head_grad[0, :, columns],
        correction[0, :, 0],
        random_blocks[0, 0],
        global_blocks[0],
        radius[0, 0],
    )
    gradients = jnp.stack([query_grad, key_grad, value_grad], axis=0)[:, None]
    returned = lax.all_to_all(gradients, "ctx", split_axis=2, concat_axis=3, tiled=True)
    arrived = passed_along(returned, "pipe", -1)
    return (arrived[0], arrived[1], arrived[2])


def solution(mesh):
    return jax.shard_map(
        body,
        mesh=mesh,
        in_specs=(
            P("pipe", "ctx", None),
            P("pipe", "ctx", None),
            P("pipe", "ctx", None),
            P("pipe", "ctx", None),
            P("pipe", "ctx", None),
            P("pipe", "ctx", None, None),
            P("pipe", None),
            P("pipe", "ctx"),
        ),
        out_specs=(P("pipe", "ctx", None), P("pipe", "ctx", None), P("pipe", "ctx", None)),
        check_vma=False,
    )
```

profile of v0, /device:TPU:1, one launch (start us, length us, event | category | flops | bytes accessed | tf_op | source)
XLA Modules:
  0.0 691.4 jit_solution(3119696237251115099)
XLA Ops:
  0.6 5.0 copy.91
  6.2 22.3 %reduce = bf16[4096,128]{1,0:T(8,128)(2,1)S(1)} reduce(bf16[4096,1,128]{2,1,0:T(2,128)(2,1)S(1)} %bitcast.108, bf16[]{:T(256)} %broadcast.74), dimensions={1}, to_apply=%bitcast.48.reduce_sub_computation | reduce | bytes 2097154
  29.6 11.9 %all-to-all-start = ((bf16[32,2,8192]{2,1,0:T(2,128)(2,1)}), bf16[32,2,8192]{2,1,0:T(2,128)(2,1)S(1)}, u32[]{:S(2)}, u32[]{:S(2)}) async-start(bf16[32,2,8192]{2,1,0:T(2,128)(2,1)} %reshape.110), calls=%async_computation | async-start | bytes 2097152 | tf_op jit(solution)/shard_map/all_to_all | solution.py:122
  41.5 5.0 copy.93
  46.5 23.3 %reduce.1 = bf16[4096,128]{1,0:T(8,128)(2,1)} reduce(bf16[4096,1,128]{2,1,0:T(2,128)(2,1)S(1)} %bitcast.111, bf16[]{:T(256)} %broadcast.74), dimensions={1}, to_apply=%bitcast.50.reduce_sub_computation | reduce | bytes 2097154
  72.0 9.8 %all-to-all-start.1 = ((bf16[32,2,8192]{2,1,0:T(2,128)(2,1)}), bf16[32,2,8192]{2,1,0:T(2,128)(2,1)}, u32[]{:S(2)}, u32[]{:S(2)}) async-start(bf16[32,2,8192]{2,1,0:T(2,128)(2,1)} %reshape.112), calls=%async_computation.1 | async-start | bytes 2097152 | tf_op jit(solution)/shard_map/all_to_all | solution.py:123
  81.8 5.0 copy.97
  86.8 23.3 %reduce.3 = bf16[4096,128]{1,0:T(8,128)(2,1)} reduce(bf16[4096,1,128]{2,1,0:T(2,128)(2,1)S(1)} %bitcast.112, bf16[]{:T(256)} %broadcast.74), dimensions={1}, to_apply=%bitcast.54.reduce_sub_computation | reduce | bytes 2097154
  112.2 9.5 %all-to-all-start.3 = ((bf16[32,2,8192]{2,1,0:T(2,128)(2,1)}), bf16[32,2,8192]{2,1,0:T(2,128)(2,1)}, u32[]{:S(2)}, u32[]{:S(2)}) async-start(bf16[32,2,8192]{2,1,0:T(2,128)(2,1)} %reshape.116), calls=%async_computation.3 | async-start | bytes 2097152 | tf_op jit(solution)/shard_map/all_to_all | solution.py:124
  121.7 5.0 copy.99
  126.8 23.3 %reduce.4 = bf16[4096,128]{1,0:T(8,128)(2,1)} reduce(bf16[4096,1,128]{2,1,0:T(2,128)(2,1)S(1)} %bitcast.113, bf16[]{:T(256)} %broadcast.74), dimensions={1}, to_apply=%bitcast.56.reduce_sub_computation | reduce | bytes 2097154
  152.2 9.5 %all-to-all-start.4 = ((bf16[32,2,8192]{2,1,0:T(2,128)(2,1)}), bf16[32,2,8192]{2,1,0:T(2,128)(2,1)}, u32[]{:S(2)}, u32[]{:S(2)}) async-start(bf16[32,2,8192]{2,1,0:T(2,128)(2,1)} %reshape.118), calls=%async_computation.4 | async-start | bytes 2097152 | tf_op jit(solution)/shard_map/all_to_all | solution.py:125
  162.4 5.0 copy.95
  167.4 23.3 %reduce.2 = bf16[4096,128]{1,0:T(8,128)(2,1)} reduce(bf16[4096,1,128]{2,1,0:T(2,128)(2,1)S(1)} %bitcast.109, bf16[]{:T(256)} %broadcast.74), dimensions={1}, to_apply=%bitcast.52.reduce_sub_computation | reduce | bytes 2097154
  193.1 9.5 %all-to-all-start.2 = ((bf16[32,2,8192]{2,1,0:T(2,128)(2,1)}), bf16[32,2,8192]{2,1,0:T(2,128)(2,1)}, u32[]{:S(2)}, u32[]{:S(2)}) async-start(bf16[32,2,8192]{2,1,0:T(2,128)(2,1)} %reshape.114), calls=%async_computation.2 | async-start | bytes 2097152 | tf_op jit(solution)/shard_map/all_to_all | solution.py:126
  234.2 6.2 fusion.25
  240.4 274.9 %while.15 = (s32[]{:T(128)}, f32[64,8192]{1,0:T(8,128)}, f32[64,8192]{1,0:T(8,128)}, bf16[8,8,64,128]{3,2,1,0:T(8,128)(2,1)}, s32[8]{0:T(128)S(1)}, /*index=5*/s...) while((s32[]{:T(128)}, f32[64,8192]{1,0:T(8,128)}, ...), condition=%wide.region_5.6_spmd.clone, body=%wide.region_2.5_spmd.clone.sunk | while | flops 1431909376 | bytes 54307064 | solution.py:113
  292.4 4.4 convolution_add_fusion.5
  302.5 4.4 convolution_add_fusion.4
  327.1 4.4 convolution_add_fusion.5
  337.2 4.4 convolution_add_fusion.4
  361.9 4.4 convolution_add_fusion.5
  371.9 4.4 convolution_add_fusion.4
  396.6 4.4 convolution_add_fusion.5
  431.3 4.4 convolution_add_fusion.5
  466.1 4.4 convolution_add_fusion.5
  500.8 4.4 convolution_add_fusion.5
  510.9 4.4 convolution_add_fusion.4
  521.4 20.0 %copy.103 = bf16[3,1,4096,128]{3,0,1,2:T(4,128)(2,1)S(1)} copy(bf16[3,1,4096,128]{3,2,0,1:T(8,128)(2,1)S(1)} %maximum_bitcast_fusion) | data formatting | bytes 6291456 | tf_op jit(solution)/shard_map/broadcast_in_dim | solution.py:146
  541.4 98.1 %all_to_all.87 = bf16[3,1,4096,128]{3,0,1,2:T(4,128)(2,1)S(1)} all-to-all(bf16[3,1,4096,128]{3,0,1,2:T(4,128)(2,1)S(1)} %copy.103), channel_id=1, replica_groups=mesh['pipe'=8,'ctx'=32] {'ctx'}, dimensions={2} | all-to-all | bytes 6291456 | tf_op jit(solution)/shard_map/all_to_all | solution.py:147
  642.8 7.9 %collective-permute-start = (bf16[3,1,128,4096]{2,3,0,1:T(8,128)(2,1)}, bf16[3,1,128,4096]{2,3,0,1:T(8,128)(2,1)S(1)}, u32[]{:S(2)}, u32[]{:S(2)}) collective-permute-start(bf16[3,1,128,4096]{2,3,0,1:T(8,128)(2,1)} %bitcast.119), channel_id=1, source_target_pairs={{0,224},{32,0},{64,32},{96,64},{128,96},{160,128},{192,160},{224,1... | collective-permute-start | bytes 9437192 | tf_op jit(solution)/shard_map/ppermute | solution.py:17
  650.7 36.4 %collective-permute-done = bf16[3,1,128,4096]{2,3,0,1:T(8,128)(2,1)S(1)} collective-permute-done((bf16[3,1,128,4096]{2,3,0,1:T(8,128)(2,1)}, bf16[3,1,128,4096]{2,3,0,1:T(8,128)(2,1)S(1)}, u32[]{:S(2)}, u32[]{:S(2)}) %collective-permute-start) | collective-permute-done | bytes 3145760 | tf_op jit(solution)/shard_map/ppermute | solution.py:17
  (239 shorter events, 265.5 us)
Async XLA Ops:
  29.6 42.3 %all-to-all-start = ((bf16[32,2,8192]{2,1,0:T(2,128)(2,1)}), bf16[32,2,8192]{2,1,0:T(2,128)(2,1)S(1)}, u32[]{:S(2)}, u32[]{:S(2)}) async-start(bf16[32,2,8192]{2,1,0:T(2,128)(2,1)} %reshape.110), calls=%async_computation | async-start | bytes 2097152 | tf_op jit(solution)/shard_map/all_to_all | solution.py:122
  72.0 40.3 %all-to-all-start.1 = ((bf16[32,2,8192]{2,1,0:T(2,128)(2,1)}), bf16[32,2,8192]{2,1,0:T(2,128)(2,1)}, u32[]{:S(2)}, u32[]{:S(2)}) async-start(bf16[32,2,8192]{2,1,0:T(2,128)(2,1)} %reshape.112), calls=%async_computation.1 | async-start | bytes 2097152 | tf_op jit(solution)/shard_map/all_to_all | solution.py:123
  112.2 40.0 %all-to-all-start.3 = ((bf16[32,2,8192]{2,1,0:T(2,128)(2,1)}), bf16[32,2,8192]{2,1,0:T(2,128)(2,1)}, u32[]{:S(2)}, u32[]{:S(2)}) async-start(bf16[32,2,8192]{2,1,0:T(2,128)(2,1)} %reshape.116), calls=%async_computation.3 | async-start | bytes 2097152 | tf_op jit(solution)/shard_map/all_to_all | solution.py:124
  150.1 12.3 %copy-start.4 = (s32[1,1,64,3]{2,1,3,0:T(1,128)S(1)}, s32[1,1,64,3]{2,1,3,0:T(1,128)}, u32[]{:S(2)}) copy-start(s32[1,1,64,3]{2,1,3,0:T(1,128)} %param.15) | copy-start | bytes 2308
  152.2 40.8 %all-to-all-start.4 = ((bf16[32,2,8192]{2,1,0:T(2,128)(2,1)}), bf16[32,2,8192]{2,1,0:T(2,128)(2,1)}, u32[]{:S(2)}, u32[]{:S(2)}) async-start(bf16[32,2,8192]{2,1,0:T(2,128)(2,1)} %reshape.118), calls=%async_computation.4 | async-start | bytes 2097152 | tf_op jit(solution)/shard_map/all_to_all | solution.py:125
  167.4 25.6 %copy-start.5 = (s32[1,2]{1,0:T(1,128)S(1)}, s32[1,2]{1,0:T(1,128)}, u32[]{:S(2)}) copy-start(s32[1,2]{1,0:T(1,128)} %param.16) | copy-start | bytes 28
  193.1 34.7 %all-to-all-start.2 = ((bf16[32,2,8192]{2,1,0:T(2,128)(2,1)}), bf16[32,2,8192]{2,1,0:T(2,128)(2,1)}, u32[]{:S(2)}, u32[]{:S(2)}) async-start(bf16[32,2,8192]{2,1,0:T(2,128)(2,1)} %reshape.114), calls=%async_computation.2 | async-start | bytes 2097152 | tf_op jit(solution)/shard_map/all_to_all | solution.py:126
  232.2 2.0 copy-start.2
  250.2 1.5 copy-start.1
  281.8 1.5 copy-start.1
  316.5 1.5 copy-start.1
  351.2 1.5 copy-start.1
  386.0 1.5 copy-start.1
  420.7 1.5 copy-start.1
  455.4 1.5 copy-start.1
  490.2 1.5 copy-start.1
  515.3 3.2 copy-start
  518.6 1.2 copy-start.3
  642.8 44.3 %collective-permute-start = (bf16[3,1,128,4096]{2,3,0,1:T(8,128)(2,1)}, bf16[3,1,128,4096]{2,3,0,1:T(8,128)(2,1)S(1)}, u32[]{:S(2)}, u32[]{:S(2)}) collective-permute-start(bf16[3,1,128,4096]{2,3,0,1:T(8,128)(2,1)} %bitcast.119), channel_id=1, source_target_pairs={{0,224},{32,0},{64,32},{96,64},{128,96},{160,128},{192,160},{224,1... | collective-permute-start | bytes 9437192 | tf_op jit(solution)/shard_map/ppermute | solution.py:17
where the time goes:
time: 704 us; the launch traced here: 691 us
  local copies, waits for them, and re-layouts  184 us (26%)
  matrix products  162 us (23%)
  other arithmetic  135 us (19%)
  blocking collectives  98.1 us (14%)
  starting transfers between devices  58 us (8%)
  waiting for transfers between devices  36.4 us (5%)
  loops' own time  16.2 us (2%)
    unnamed x7, other arithmetic  116 us
    all_to_all x1, blocking collectives, body(): lax.all_to_all(gradients, 'ctx', split_axis=2, concat_axis=3, tiled=True)  98.1 us
    unnamed x36, local copies, waits for them, and re-layouts  59.7 us
    ppermute x1, waiting for transfers between devices, passed_along(): return lax.ppermute(value, axis, pairs)  36.4 us
    dot_general x8, matrix products, one_group(): jnp.dot(placing, value_part, precision=lax.Precision.HIGHEST, preferred_e...  34 us
    dot_general x8, matrix products, one_group(): jnp.dot(placing, key_part, precision=lax.Precision.HIGHEST, preferred_ele...  33.5 us
    dot_general x8, matrix products, one_group(): jnp.einsum('bij,bid->bjd', attention_low, group_grad, preferred_element_t...  31.2 us
    gather x8, local copies, waits for them, and re-layouts, one_group(): value_tiles = value_blocks[group_index].reshape(QG, KB * BLK, HD)  24.8 us
  transfers between devices with their start and end apart: 6, of which 1 were waited for; matrix products, arithmetic and copies ran while one was open for 21% of the time, Pallas kernels for 0%

commit v1 on v0

v1 whole, which is shorter than its diff:
```python
import functools

import jax
import jax.numpy as jnp
from jax import lax
from jax.experimental import pallas as pl
from jax.experimental.pallas import tpu as pltpu
from jax.sharding import PartitionSpec as P

HD = 128
BLK = 64
RMAX = 2
NR = 3
KB = 10


def passed_along(value, axis, steps):
    count = lax.axis_size(axis)
    pairs = [(source, (source + steps) % count) for source in range(count)]
    return lax.ppermute(value, axis, pairs)


def slot_table(random_list, global_list, head_radius, block_count):
    blocks = jnp.arange(block_count, dtype=jnp.int32)[:, None]
    offsets = jnp.arange(-RMAX, RMAX + 1, dtype=jnp.int32)[None, :]
    window = blocks + offsets
    window_ok = (jnp.abs(offsets) <= head_radius) & (window >= 0) & (window < block_count)
    window = jnp.clip(window, 0, block_count - 1)
    global_slots = jnp.broadcast_to(global_list[None, :], (block_count, global_list.shape[0]))
    global_ok = jnp.abs(global_slots - blocks) > head_radius
    random_ok = jnp.abs(random_list - blocks) > head_radius
    random_ok = random_ok & jnp.all(random_list[:, :, None] != global_list[None, None, :], axis=2)
    earlier = jnp.arange(NR)[None, :] < jnp.arange(NR)[:, None]
    repeated = jnp.any((random_list[:, :, None] == random_list[:, None, :]) & earlier[None], axis=2)
    random_ok = random_ok & jnp.logical_not(repeated)
    slot_index = jnp.concatenate([window, global_slots, random_list], axis=1)
    slot_valid = jnp.concatenate([window_ok, global_ok, random_ok], axis=1)
    slot_index = jnp.clip(slot_index, 0, block_count - 1)
    return (slot_index.astype(jnp.int32), slot_valid.astype(jnp.int32))


def head_kernel(slot_ref, valid_ref, x_ref, corr_ref, dq_ref, dk_ref, dv_ref,
                kt_ref, vt_ref, dk_acc, dv_acc, *, block_count, chunk_rows):
    score_scale = HD ** (-0.5)
    per_chunk = chunk_rows // BLK
    dk_acc[...] = jnp.zeros_like(dk_acc)
    dv_acc[...] = jnp.zeros_like(dv_acc)
    lane_slot = lax.broadcasted_iota(jnp.int32, (1, KB * BLK), 1) // BLK

    def one_block(i, carry):
        chunk = i // per_chunk
        row = pl.multiple_of((i % per_chunk) * BLK, BLK)
        query = x_ref[chunk, 0, pl.ds(row, BLK), :]
        grad = x_ref[chunk, 3, pl.ds(row, BLK), :]
        live = jnp.zeros((1, KB * BLK), jnp.bool_)
        for j in range(KB):
            kb = slot_ref[i * KB + j]
            kc = kb // per_chunk
            kr = pl.multiple_of((kb % per_chunk) * BLK, BLK)
            kt_ref[pl.ds(j * BLK, BLK), :] = x_ref[kc, 1, pl.ds(kr, BLK), :]
            vt_ref[pl.ds(j * BLK, BLK), :] = x_ref[kc, 2, pl.ds(kr, BLK), :]
            live = live | ((lane_slot == j) & (valid_ref[i * KB + j] != 0))
        key_tiles = kt_ref[...]
        value_tiles = vt_ref[...]
        scores = lax.dot_general(
            query, key_tiles, (((1,), (1,)), ((), ())), preferred_element_type=jnp.float32
        ) * score_scale
        scores = jnp.where(live, scores, -jnp.inf)
        row_max = jnp.max(scores, axis=-1, keepdims=True)
        weights = jnp.exp(scores - row_max)
        attention = weights / jnp.sum(weights, axis=-1, keepdims=True)
        dprobs = lax.dot_general(
            grad, value_tiles, (((1,), (1,)), ((), ())), preferred_element_type=jnp.float32
        )
        corr = corr_ref[pl.ds(pl.multiple_of(i * BLK, BLK), BLK), :]
        dscores = (attention * (dprobs - corr)).astype(jnp.bfloat16)
        query_grad = jnp.dot(dscores, key_tiles, preferred_element_type=jnp.float32) * score_scale
        dq_ref[chunk, pl.ds(row, BLK), :] = query_grad.astype(jnp.bfloat16)
        key_part = lax.dot_general(
            dscores, query, (((0,), (0,)), ((), ())), preferred_element_type=jnp.float32
        )
        value_part = lax.dot_general(
            attention.astype(jnp.bfloat16), grad, (((0,), (0,)), ((), ())),
            preferred_element_type=jnp.float32,
        )
        for j in range(KB):
            kb = slot_ref[i * KB + j]
            dk_acc[kb] = dk_acc[kb] + key_part[j * BLK:(j + 1) * BLK]
            dv_acc[kb] = dv_acc[kb] + value_part[j * BLK:(j + 1) * BLK]
        return carry

    lax.fori_loop(0, block_count, one_block, 0)

    def one_chunk(c, carry):
        for p in range(per_chunk):
            b = c * per_chunk + p
            dk_ref[c, p * BLK:(p + 1) * BLK, :] = (dk_acc[b] * score_scale).astype(jnp.bfloat16)
            dv_ref[c, p * BLK:(p + 1) * BLK, :] = dv_acc[b].astype(jnp.bfloat16)
        return carry

    lax.fori_loop(0, block_count // per_chunk, one_chunk, 0)


def head_grads(x, corr, slot_index, slot_valid, block_count, chunks, chunk_rows):
    vmem = pltpu.MemorySpace.VMEM
    smem = pltpu.MemorySpace.SMEM
    out_shape = jax.ShapeDtypeStruct((chunks, chunk_rows, HD), jnp.bfloat16)
    kernel = functools.partial(head_kernel, block_count=block_count, chunk_rows=chunk_rows)
    return pl.pallas_call(
        kernel,
        out_shape=(out_shape, out_shape, out_shape),
        in_specs=[
            pl.BlockSpec(memory_space=smem),
            pl.BlockSpec(memory_space=smem),
            pl.BlockSpec(memory_space=vmem),
            pl.BlockSpec(memory_space=vmem),
        ],
        out_specs=(
            pl.BlockSpec(memory_space=vmem),
            pl.BlockSpec(memory_space=vmem),
            pl.BlockSpec(memory_space=vmem),
        ),
        scratch_shapes=[
            pltpu.VMEM((KB * BLK, HD), jnp.bfloat16),
            pltpu.VMEM((KB * BLK, HD), jnp.bfloat16),
            pltpu.VMEM((block_count, BLK, HD), jnp.float32),
            pltpu.VMEM((block_count, BLK, HD), jnp.float32),
        ],
        compiler_params=pltpu.CompilerParams(vmem_limit_bytes=48 * 1024 * 1024),
    )(slot_index.reshape(-1), slot_valid.reshape(-1), x, corr)


def body(queries, keys, values, attn_out, out_grad, random_blocks, global_blocks, radius):
    chunks = lax.axis_size("ctx")
    local = queries.shape[1]
    width = queries.shape[2]
    heads = width // HD
    length = local * chunks
    block_count = length // BLK
    correction = jnp.sum(
        (attn_out[0].astype(jnp.float32) * out_grad[0].astype(jnp.float32)).reshape(
            local, heads, HD
        ),
        axis=-1,
    )
    correction = lax.all_to_all(correction.T, "ctx", split_axis=0, concat_axis=0, tiled=True)
    correction = correction.reshape(length, 1)
    stacked = jnp.stack([queries[0], keys[0], values[0], out_grad[0]], axis=0)
    stacked = stacked.reshape(4, local, chunks, HD).transpose(2, 0, 1, 3)
    received = lax.all_to_all(stacked, "ctx", split_axis=0, concat_axis=0, tiled=True)
    slot_index, slot_valid = slot_table(
        random_blocks[0, 0], global_blocks[0], radius[0, 0], block_count
    )
    grads = head_grads(received, correction, slot_index, slot_valid, block_count, chunks, local)
    outs = []
    for g in grads:
        back = lax.all_to_all(g, "ctx", split_axis=0, concat_axis=0, tiled=True)
        back = passed_along(back, "pipe", -1)
        outs.append(back.transpose(1, 0, 2).reshape(1, local, chunks * HD))
    return tuple(outs)


def solution(mesh):
    return jax.shard_map(
        body,
        mesh=mesh,
        in_specs=(
            P("pipe", "ctx", None),
            P("pipe", "ctx", None),
            P("pipe", "ctx", None),
            P("pipe", "ctx", None),
            P("pipe", "ctx", None),
            P("pipe", "ctx", None, None),
            P("pipe", None),
            P("pipe", "ctx"),
        ),
        out_specs=(P("pipe", "ctx", None), P("pipe", "ctx", None), P("pipe", "ctx", None)),
        check_vma=False,
    )
```

time: 704 us -> 309 us (0.44); the launches traced: 691 us -> 309 us
  matrix products: 162 us -> 0 us
  local copies, waits for them, and re-layouts: 184 us -> 23.6 us
  other arithmetic: 135 us -> 6.15 us
  waiting for transfers between devices: 36.4 us -> 123 us
  Pallas kernels: 0 us -> 52.7 us
  blocking collectives: 98.1 us -> 65.1 us
  starting transfers between devices: 58 us -> 37.1 us
  loops' own time: 16.2 us -> 0 us
    dot_general x57 -> x0, matrix products: 162 us -> none  [the longest x8 34 us: one_group(): jnp.dot(placing, value_part, precision=lax.Precision.HIGHEST, preferred_e...]
    all_to_all x5 -> x3, waiting for transfers between devices: 0.01 us -> 115 us  [the longest x1 92.6 us: body(): lax.all_to_all(stacked, 'ctx', split_axis=0, concat_axis=0, tiled=True)]
    unnamed x7 -> x1, other arithmetic: 116 us -> 1.8 us
    pallas_call x0 -> x1, Pallas kernels: none -> 52.7 us  [head_grads(): pl.pallas_call(kernel, out_shape=(out_shape, out_shape, out_shape), in_sp...]
    unnamed x36 -> x15, local copies, waits for them, and re-layouts: 59.7 us -> 10.5 us
    gather x16 -> x0, local copies, waits for them, and re-layouts: 41 us -> none  [the longest x8 24.8 us: one_group(): value_tiles = value_blocks[group_index].reshape(QG, KB * BLK, HD)]
    reshape x16 -> x2, local copies, waits for them, and re-layouts: 41.8 us -> 7.07 us  [the longest x1 6.43 us: body(): stacked = stacked.reshape(4, local, chunks, HD).transpose(2, 0, 1, 3)]
    all_to_all x1 -> x2, blocking collectives: 98.1 us -> 65.1 us  [body(): back = lax.all_to_all(g, 'ctx', split_axis=0, concat_axis=0, tiled=True)]
  transfers between devices with their start and end apart: 6 -> 6, of which waited for: 1 -> 3; matrix products, arithmetic and copies ran while one was open for 21% -> 8% of each run, Pallas kernels for 0% -> 0%
where the time goes in v1:
time: 309 us
  waiting for transfers between devices  123 us (40%)
  blocking collectives  65.1 us (21%)
  Pallas kernels  52.7 us (17%)
  starting transfers between devices  37.1 us (12%)
  local copies, waits for them, and re-layouts  23.6 us (8%)
  other arithmetic  6.15 us (2%)
    all_to_all x1, waiting for transfers between devices, body(): lax.all_to_all(stacked, 'ctx', split_axis=0, concat_axis=0, tiled=True)  92.6 us
    all_to_all x2, blocking collectives, body(): back = lax.all_to_all(g, 'ctx', split_axis=0, concat_axis=0, tiled=True)  65.1 us
    pallas_call x1, Pallas kernels, head_grads(): pl.pallas_call(kernel, out_shape=(out_shape, out_shape, out_shape), in_sp...  52.7 us
    all_to_all x1, waiting for transfers between devices, body(): back = lax.all_to_all(g, 'ctx', split_axis=0, concat_axis=0, tiled=True)  22 us
    all_to_all x1, starting transfers between devices, body(): lax.all_to_all(correction.T, 'ctx', split_axis=0, concat_axis=0, tiled=True)  11.9 us
    unnamed x15, local copies, waits for them, and re-layouts  10.5 us
    all_to_all x1, starting transfers between devices, body(): lax.all_to_all(stacked, 'ctx', split_axis=0, concat_axis=0, tiled=True)  9.5 us
    all_to_all x1, starting transfers between devices, body(): back = lax.all_to_all(g, 'ctx', split_axis=0, concat_axis=0, tiled=True)  8.03 us
  transfers between devices with their start and end apart: 6, of which 3 were waited for; matrix products, arithmetic and copies ran while one was open for 8% of the time, Pallas kernels for 0%

profile of v1, /device:TPU:1, one launch (start us, length us, event | category | flops | bytes accessed | tf_op | source)
XLA Modules:
  0.0 308.7 jit_solution(11257848461812453040)
XLA Ops:
  0.6 1.8 multiply_bitcast_fusion
  2.4 0.4 copy.67
  2.8 0.6 reduce_sum.9
  3.4 0.7 copy.58
  4.1 11.9 %all-to-all-start.1 = ((f32[32,1,128]{2,1,0:T(1,128)}), f32[32,1,128]{2,1,0:T(1,128)S(1)}, u32[]{:S(2)}, u32[]{:S(2)}) async-start(f32[32,1,128]{2,1,0:T(1,128)} %copy.58), calls=%async_computation.1 | async-start | bytes 32768 | tf_op jit(solution)/shard_map/all_to_all | solution.py:146
  16.0 0.7 copy.56
  16.7 1.6 copy.53
  18.3 1.6 copy.54
  19.9 2.3 copy.55
  22.2 3.3 %pad_maximum_fusion = bf16[4,128,4096]{1,2,0:T(8,128)(2,1)} fusion(bf16[1,128,4096]{1,2,0:T(8,128)(2,1)S(1)} %copy.56, bf16[1,128,4096]{1,2,0:T(8,128)(2,1)} %copy.55, bf16[1,128,4096]{1,2,0:T(8,128)(2,1)S(1)} %copy.54, bf16[1,128,4096]{1,2,0:T(8,128)(2,1)S(1)} %copy.53), kind=kLoop, calls=%fused_computation | loop fusion | flops 6291456 | bytes 8388608 | tf_op jit(solution)/shard_map/stack | solution.py:148
  25.5 6.4 %copy.57 = bf16[4,128,32,128]{3,1,0,2:T(8,128)(2,1)} copy(bf16[4,128,32,128]{1,3,2,0:T(8,128)(2,1)} %bitcast.27) | data formatting | bytes 8388608 | tf_op jit(solution)/shard_map/reshape | solution.py:149
  31.9 9.5 %all-to-all-start = ((bf16[32,4,128,128]{3,2,1,0:T(8,128)(2,1)}), bf16[32,4,128,128]{3,2,1,0:T(8,128)(2,1)}, u32[]{:S(2)}, u32[]{:S(2)}) async-start(bf16[32,4,128,128]{3,2,1,0:T(8,128)(2,1)} %bitcast.26), calls=%async_computation | async-start | bytes 8388608 | tf_op jit(solution)/shard_map/all_to_all | solution.py:150
  42.6 0.1 reshape.69.valid_ref
  42.9 0.1 copy.51
  43.0 0.1 min.22.slot_ref
  43.1 0.6 copy.59.corr_ref
  43.8 92.6 %all-to-all-done.x_ref = bf16[32,4,128,128]{3,2,1,0:T(8,128)(2,1)} async-done(((bf16[32,4,128,128]{3,2,1,0:T(8,128)(2,1)}), bf16[32,4,128,128]{3,2,1,0:T(8,128)(2,1)}, u32[]{:S(2)}, u32[]{:S(2)}) %all-to-all-start) | async-done | bytes 4194336 | tf_op jit(solution)/shard_map/all_to_all | solution.py:150
  136.4 52.7 %shard_map.103 = (bf16[32,128,128]{2,1,0:T(8,128)(2,1)}, bf16[32,128,128]{2,1,0:T(8,128)(2,1)S(1)}, bf16[32,128,128]{2,1,0:T(8,128)(2,1)S(1)}) custom-call(s32[640]{0:T(1024)S(1)} %min.22.slot_ref, s32[640]{0:T(1024)S(1)} %reshape.69.valid_ref, bf16[32,4,128,128]{3,2,1,0:T(8,128)(2,1)} %all-to-all-done.x_ref, f32[4096,1]{1,0:T(8,128)S(1)} %copy.59.corr_ref), custom_call_target="tpu_custom_call" | custom-call | tf_op jit(solution)/shard_map/pallas_call | solution.py:109
  189.1 32.3 %all_to_all.29 = bf16[32,128,128]{2,1,0:T(8,128)(2,1)S(1)} all-to-all(bf16[32,128,128]{2,1,0:T(8,128)(2,1)S(1)} %get-tuple-element.7), channel_id=1, replica_groups=mesh['pipe'=8,'ctx'=32] {'ctx'}, dimensions={0} | all-to-all | bytes 2097152 | tf_op jit(solution)/shard_map/all_to_all | solution.py:157
  221.4 32.9 %all_to_all.30 = bf16[32,128,128]{2,1,0:T(8,128)(2,1)S(1)} all-to-all(bf16[32,128,128]{2,1,0:T(8,128)(2,1)S(1)} %get-tuple-element.8), channel_id=1, replica_groups=mesh['pipe'=8,'ctx'=32] {'ctx'}, dimensions={0} | all-to-all | bytes 2097152 | tf_op jit(solution)/shard_map/all_to_all | solution.py:157
  254.2 8.0 %all-to-all-start.2 = ((bf16[32,128,128]{2,1,0:T(8,128)(2,1)}), bf16[32,128,128]{2,1,0:T(8,128)(2,1)S(1)}, u32[]{:S(2)}, u32[]{:S(2)}) async-start(bf16[32,128,128]{2,1,0:T(8,128)(2,1)} %get-tuple-element.6), calls=%async_computation.2 | async-start | bytes 2097152 | tf_op jit(solution)/shard_map/all_to_all | solution.py:157
  262.3 1.5 collective-permute-start.2
  263.7 1.7 collective-permute-start.1
  265.4 22.0 %all-to-all-done.2 = bf16[32,128,128]{2,1,0:T(8,128)(2,1)S(1)} async-done(((bf16[32,128,128]{2,1,0:T(8,128)(2,1)}), bf16[32,128,128]{2,1,0:T(8,128)(2,1)S(1)}, u32[]{:S(2)}, u32[]{:S(2)}) %all-to-all-start.2) | async-done | bytes 1048608 | tf_op jit(solution)/shard_map/all_to_all | solution.py:157
  287.4 4.6 %collective-permute-start = (bf16[32,128,128]{2,1,0:T(8,128)(2,1)S(1)}, bf16[32,128,128]{2,1,0:T(8,128)(2,1)}, u32[]{:S(2)}, u32[]{:S(2)}) collective-permute-start(bf16[32,128,128]{2,1,0:T(8,128)(2,1)S(1)} %all-to-all-done.2), channel_id=1, source_target_pairs={{0,224},{32,0},{64,32},{96,64},{128,96},{160,128},{192,160},{224,1... | collective-permute-start | bytes 3145736 | tf_op jit(solution)/shard_map/ppermute | solution.py:20
  292.0 1.6 copy.62
  293.6 1.3 copy.65
  294.9 1.6 copy.61
  296.6 1.3 copy.64
  297.9 7.9 %collective-permute-done = bf16[32,128,128]{2,1,0:T(8,128)(2,1)} collective-permute-done((bf16[32,128,128]{2,1,0:T(8,128)(2,1)S(1)}, bf16[32,128,128]{2,1,0:T(8,128)(2,1)}, u32[]{:S(2)}, u32[]{:S(2)}) %collective-permute-start) | collective-permute-done | bytes 1048608 | tf_op jit(solution)/shard_map/ppermute | solution.py:20
  305.8 1.6 copy.60
  307.4 1.3 copy.63
  (23 shorter events, 0.6 us)
Async XLA Ops:
  2.4 13.5 %copy-start = (bf16[1,128,4096]{2,1,0:T(8,128)(2,1)S(1)}, bf16[1,128,4096]{2,1,0:T(8,128)(2,1)}, u32[]{:S(2)}) copy-start(bf16[1,128,4096]{2,1,0:T(8,128)(2,1)} %param.12) | copy-start | bytes 3145732
  4.1 27.8 %all-to-all-start.1 = ((f32[32,1,128]{2,1,0:T(1,128)}), f32[32,1,128]{2,1,0:T(1,128)S(1)}, u32[]{:S(2)}, u32[]{:S(2)}) async-start(f32[32,1,128]{2,1,0:T(1,128)} %copy.58), calls=%async_computation.1 | async-start | bytes 32768 | tf_op jit(solution)/shard_map/all_to_all | solution.py:146
  31.9 10.2 %copy-start.1 = (s32[1,1,64,3]{2,1,3,0:T(1,128)S(1)}, s32[1,1,64,3]{2,1,3,0:T(1,128)}, u32[]{:S(2)}) copy-start(s32[1,1,64,3]{2,1,3,0:T(1,128)} %param.13) | copy-start | bytes 2308
  31.9 10.2 %copy-start.2 = (s32[1,2]{1,0:T(1,128)S(1)}, s32[1,2]{1,0:T(1,128)}, u32[]{:S(2)}) copy-start(s32[1,2]{1,0:T(1,128)} %param.14) | copy-start | bytes 28
  31.9 104.5 %all-to-all-start = ((bf16[32,4,128,128]{3,2,1,0:T(8,128)(2,1)}), bf16[32,4,128,128]{3,2,1,0:T(8,128)(2,1)}, u32[]{:S(2)}, u32[]{:S(2)}) async-start(bf16[32,4,128,128]{3,2,1,0:T(8,128)(2,1)} %bitcast.26), calls=%async_computation | async-start | bytes 8388608 | tf_op jit(solution)/shard_map/all_to_all | solution.py:150
  254.2 33.2 %all-to-all-start.2 = ((bf16[32,128,128]{2,1,0:T(8,128)(2,1)}), bf16[32,128,128]{2,1,0:T(8,128)(2,1)S(1)}, u32[]{:S(2)}, u32[]{:S(2)}) async-start(bf16[32,128,128]{2,1,0:T(8,128)(2,1)} %get-tuple-element.6), calls=%async_computation.2 | async-start | bytes 2097152 | tf_op jit(solution)/shard_map/all_to_all | solution.py:157
  262.3 29.7 %collective-permute-start.2 = (bf16[32,128,128]{2,1,0:T(8,128)(2,1)S(1)}, bf16[32,128,128]{2,1,0:T(8,128)(2,1)}, u32[]{:S(2)}, u32[]{:S(2)}) collective-permute-start(bf16[32,128,128]{2,1,0:T(8,128)(2,1)S(1)} %all_to_all.30), channel_id=1, source_target_pairs={{0,224},{32,0},{64,32},{96,64},{128,96},{160,128},{192,160},{224,1... | collective-permute-start | bytes 3145736 | tf_op jit(solution)/shard_map/ppermute | solution.py:20
  263.7 31.2 %collective-permute-start.1 = (bf16[32,128,128]{2,1,0:T(8,128)(2,1)S(1)}, bf16[32,128,128]{2,1,0:T(8,128)(2,1)}, u32[]{:S(2)}, u32[]{:S(2)}) collective-permute-start(bf16[32,128,128]{2,1,0:T(8,128)(2,1)S(1)} %all_to_all.29), channel_id=1, source_target_pairs={{0,224},{32,0},{64,32},{96,64},{128,96},{160,128},{192,160},{224,1... | collective-permute-start | bytes 3145736 | tf_op jit(solution)/shard_map/ppermute | solution.py:20
  287.4 18.3 %collective-permute-start = (bf16[32,128,128]{2,1,0:T(8,128)(2,1)S(1)}, bf16[32,128,128]{2,1,0:T(8,128)(2,1)}, u32[]{:S(2)}, u32[]{:S(2)}) collective-permute-start(bf16[32,128,128]{2,1,0:T(8,128)(2,1)S(1)} %all-to-all-done.2), channel_id=1, source_target_pairs={{0,224},{32,0},{64,32},{96,64},{128,96},{160,128},{192,160},{224,1... | collective-permute-start | bytes 3145736 | tf_op jit(solution)/shard_map/ppermute | solution.py:20

commit v2 on v1

--- a/solution.py
+++ b/solution.py
@@ -39,26 +39,29 @@
     return (slot_index.astype(jnp.int32), slot_valid.astype(jnp.int32))
 
 
-def head_kernel(slot_ref, valid_ref, x_ref, corr_ref, dq_ref, dk_ref, dv_ref,
-                kt_ref, vt_ref, dk_acc, dv_acc, *, block_count, chunk_rows):
+def head_kernel(slot_ref, valid_ref, kv_ref, qd_ref, corr_ref, *rest, block_count,
+                chunk_rows, parity, final):
+    if final:
+        (dk_prev, dv_prev, dq_ref, dk_ref, dv_ref, kt_ref, vt_ref, dk_acc, dv_acc) = rest
+    else:
+        (dq_ref, dk_acc, dv_acc, kt_ref, vt_ref) = rest
     score_scale = HD ** (-0.5)
     per_chunk = chunk_rows // BLK
     dk_acc[...] = jnp.zeros_like(dk_acc)
     dv_acc[...] = jnp.zeros_like(dv_acc)
     lane_slot = lax.broadcasted_iota(jnp.int32, (1, KB * BLK), 1) // BLK
 
-    def one_block(i, carry):
-        chunk = i // per_chunk
-        row = pl.multiple_of((i % per_chunk) * BLK, BLK)
-        query = x_ref[chunk, 0, pl.ds(row, BLK), :]
-        grad = x_ref[chunk, 3, pl.ds(row, BLK), :]
+    def one_block(t, carry):
+        i = t * per_chunk + parity
+        query = qd_ref[t, 0]
+        grad = qd_ref[t, 1]
         live = jnp.zeros((1, KB * BLK), jnp.bool_)
         for j in range(KB):
             kb = slot_ref[i * KB + j]
             kc = kb // per_chunk
             kr = pl.multiple_of((kb % per_chunk) * BLK, BLK)
-            kt_ref[pl.ds(j * BLK, BLK), :] = x_ref[kc, 1, pl.ds(kr, BLK), :]
-            vt_ref[pl.ds(j * BLK, BLK), :] = x_ref[kc, 2, pl.ds(kr, BLK), :]
+            kt_ref[pl.ds(j * BLK, BLK), :] = kv_ref[kc, 0, pl.ds(kr, BLK), :]
+            vt_ref[pl.ds(j * BLK, BLK), :] = kv_ref[kc, 1, pl.ds(kr, BLK), :]
             live = live | ((lane_slot == j) & (valid_ref[i * KB + j] != 0))
         key_tiles = kt_ref[...]
         value_tiles = vt_ref[...]
@@ -75,7 +78,7 @@
         corr = corr_ref[pl.ds(pl.multiple_of(i * BLK, BLK), BLK), :]
         dscores = (attention * (dprobs - corr)).astype(jnp.bfloat16)
         query_grad = jnp.dot(dscores, key_tiles, preferred_element_type=jnp.float32) * score_scale
-        dq_ref[chunk, pl.ds(row, BLK), :] = query_grad.astype(jnp.bfloat16)
+        dq_ref[t] = query_grad.astype(jnp.bfloat16)
         key_part = lax.dot_general(
             dscores, query, (((0,), (0,)), ((), ())), preferred_element_type=jnp.float32
         )
@@ -89,45 +92,58 @@
             dv_acc[kb] = dv_acc[kb] + value_part[j * BLK:(j + 1) * BLK]
         return carry
 
-    lax.fori_loop(0, block_count, one_block, 0)
-
-    def one_chunk(c, carry):
-        for p in range(per_chunk):
-            b = c * per_chunk + p
-            dk_ref[c, p * BLK:(p + 1) * BLK, :] = (dk_acc[b] * score_scale).astype(jnp.bfloat16)
-            dv_ref[c, p * BLK:(p + 1) * BLK, :] = dv_acc[b].astype(jnp.bfloat16)
-        return carry
-
-    lax.fori_loop(0, block_count // per_chunk, one_chunk, 0)
-
-
-def head_grads(x, corr, slot_index, slot_valid, block_count, chunks, chunk_rows):
+    lax.fori_loop(0, block_count // per_chunk, one_block, 0)
+
+    if final:
+        def one_chunk(c, carry):
+            for p in range(per_chunk):
+                b = c * per_chunk + p
+                dk_ref[c, p * BLK:(p + 1) * BLK, :] = (
+                    (dk_acc[b] + dk_prev[b]) * score_scale
+                ).astype(jnp.bfloat16)
+                dv_ref[c, p * BLK:(p + 1) * BLK, :] = (dv_acc[b] + dv_prev[b]).astype(
+                    jnp.bfloat16
+                )
+            return carry
+
+        lax.fori_loop(0, block_count // per_chunk, one_chunk, 0)
+
+
+def head_part(kv, qd, corr, slot_index, slot_valid, previous, block_count, chunks, chunk_rows,
+              parity):
     vmem = pltpu.MemorySpace.VMEM
     smem = pltpu.MemorySpace.SMEM
-    out_shape = jax.ShapeDtypeStruct((chunks, chunk_rows, HD), jnp.bfloat16)
-    kernel = functools.partial(head_kernel, block_count=block_count, chunk_rows=chunk_rows)
+    final = previous is not None
+    dq_shape = jax.ShapeDtypeStruct((chunks, BLK, HD), jnp.bfloat16)
+    acc_shape = jax.ShapeDtypeStruct((block_count, BLK, HD), jnp.float32)
+    grad_shape = jax.ShapeDtypeStruct((chunks, chunk_rows, HD), jnp.bfloat16)
+    kernel = functools.partial(
+        head_kernel, block_count=block_count, chunk_rows=chunk_rows, parity=parity, final=final
+    )
+    operands = [slot_index.reshape(-1), slot_valid.reshape(-1), kv, qd, corr]
+    scratch = [pltpu.VMEM((KB * BLK, HD), jnp.bfloat16), pltpu.VMEM((KB * BLK, HD), jnp.bfloat16)]
+    if final:
+        operands += list(previous)
+        out_shape = (dq_shape, grad_shape, grad_shape)
+        scratch += [pltpu.VMEM((block_count, BLK, HD), jnp.float32)] * 2
+    else:
+        out_shape = (dq_shape, acc_shape, acc_shape)
+    in_specs = [pl.BlockSpec(memory_space=smem)] * 2 + [pl.BlockSpec(memory_space=vmem)] * (
+        len(operands) - 2
+    )
     return pl.pallas_call(
         kernel,
-        out_shape=(out_shape, out_shape, out_shape),
-        in_specs=[
-            pl.BlockSpec(memory_space=smem),
-            pl.BlockSpec(memory_space=smem),
-            pl.BlockSpec(memory_space=vmem),
-            pl.BlockSpec(memory_space=vmem),
-        ],
-        out_specs=(
-            pl.BlockSpec(memory_space=vmem),
-            pl.BlockSpec(memory_space=vmem),
-            pl.BlockSpec(memory_space=vmem),
-        ),
-        scratch_shapes=[
-            pltpu.VMEM((KB * BLK, HD), jnp.bfloat16),
-            pltpu.VMEM((KB * BLK, HD), jnp.bfloat16),
-            pltpu.VMEM((block_count, BLK, HD), jnp.float32),
-            pltpu.VMEM((block_count, BLK, HD), jnp.float32),
-        ],
+        out_shape=out_shape,
+        in_specs=in_specs,
+        out_specs=tuple(pl.BlockSpec(memory_space=vmem) for _ in out_shape),
+        scratch_shapes=scratch,
         compiler_params=pltpu.CompilerParams(vmem_limit_bytes=48 * 1024 * 1024),
-    )(slot_index.reshape(-1), slot_valid.reshape(-1), x, corr)
+    )(*operands)
+
+
+def to_chunks(rows, chunks):
+    count, local, width = rows.shape
+    return rows.reshape(count, local, chunks, width // chunks).transpose(2, 0, 1, 3)
 
 
 def body(queries, keys, values, attn_out, out_grad, random_blocks, global_blocks, radius):
@@ -137,6 +153,7 @@
     heads = width // HD
     length = local * chunks
     block_count = length // BLK
+    per_chunk = local // BLK
     correction = jnp.sum(
         (attn_out[0].astype(jnp.float32) * out_grad[0].astype(jnp.float32)).reshape(
             local, heads, HD
@@ -145,19 +162,34 @@
     )
     correction = lax.all_to_all(correction.T, "ctx", split_axis=0, concat_axis=0, tiled=True)
     correction = correction.reshape(length, 1)
-    stacked = jnp.stack([queries[0], keys[0], values[0], out_grad[0]], axis=0)
-    stacked = stacked.reshape(4, local, chunks, HD).transpose(2, 0, 1, 3)
-    received = lax.all_to_all(stacked, "ctx", split_axis=0, concat_axis=0, tiled=True)
+    kv = to_chunks(jnp.stack([keys[0], values[0]], axis=0), chunks)
+    kv = lax.all_to_all(kv, "ctx", split_axis=0, concat_axis=0, tiled=True)
     slot_index, slot_valid = slot_table(
         random_blocks[0, 0], global_blocks[0], radius[0, 0], block_count
     )
-    grads = head_grads(received, correction, slot_index, slot_valid, block_count, chunks, local)
-    outs = []
-    for g in grads:
+    previous = None
+    after = kv
+    dq_parts = []
+    returned = []
+    for parity in range(per_chunk):
+        rows = slice(parity * BLK, (parity + 1) * BLK)
+        qd = to_chunks(jnp.stack([queries[0, rows], out_grad[0, rows]], axis=0), chunks)
+        qd, _ = lax.optimization_barrier((qd, after))
+        qd = lax.all_to_all(qd, "ctx", split_axis=0, concat_axis=0, tiled=True)
+        after = qd
+        dq, dk, dv = head_part(
+            kv, qd, correction, slot_index, slot_valid, previous, block_count, chunks, local,
+            parity,
+        )
+        previous = (dk, dv)
+        back = lax.all_to_all(dq, "ctx", split_axis=0, concat_axis=0, tiled=True)
+        dq_parts.append(passed_along(back, "pipe", -1))
+    for g in previous:
         back = lax.all_to_all(g, "ctx", split_axis=0, concat_axis=0, tiled=True)
-        back = passed_along(back, "pipe", -1)
-        outs.append(back.transpose(1, 0, 2).reshape(1, local, chunks * HD))
-    return tuple(outs)
+        returned.append(passed_along(back, "pipe", -1))
+    dq_all = jnp.concatenate(dq_parts, axis=1)
+    outs = [dq_all] + returned
+    return tuple(o.transpose(1, 0, 2).reshape(1, local, chunks * HD) for o in outs)
 
 
 def solution(mesh):

time: 309 us -> 315 us (1.019)
  starting transfers between devices: 37.1 us -> 67 us
  waiting for transfers between devices: 123 us -> 96 us
  blocking collectives: 65.1 us -> 59.7 us
    all_to_all x2 -> x5, waiting for transfers between devices: 115 us -> 67 us  [the longest x1 45.3 us: body(): kv = lax.all_to_all(kv, 'ctx', split_axis=0, concat_axis=0, tiled=True)]
    all_to_all x2 -> x5, starting transfers between devices: 17.5 us -> 42.1 us  [the longest x2 18.4 us: body(): back = lax.all_to_all(dq, 'ctx', split_axis=0, concat_axis=0, tiled=True)]
    ppermute x3 -> x4, waiting for transfers between devices: 7.9 us -> 21.6 us  [passed_along(): return lax.ppermute(value, axis, pairs)]
    ppermute x3 -> x4, starting transfers between devices: 7.7 us -> 16.6 us  [passed_along(): return lax.ppermute(value, axis, pairs)]
    all_to_all x1, waiting for transfers between devices: 0.01 us -> 7.35 us  [body(): lax.all_to_all(correction.T, 'ctx', split_axis=0, concat_axis=0, tiled=True)]
    all_to_all x2, blocking collectives: 65.1 us -> 59.7 us  [body(): back = lax.all_to_all(g, 'ctx', split_axis=0, concat_axis=0, tiled=True)]
    reshape x1, local copies, waits for them, and re-layouts: 6.43 us -> 2.76 us  [to_chunks(): rows.reshape(count, local, chunks, width // chunks).transpose(2, 0, 1, 3)]
    all_to_all x1, starting transfers between devices: 11.9 us -> 8.33 us  [body(): lax.all_to_all(correction.T, 'ctx', split_axis=0, concat_axis=0, tiled=True)]
  transfers between devices with their start and end apart: 6 -> 10, of which waited for: 3 -> 6; matrix products, arithmetic and copies ran while one was open for 8% -> 6% of each run, Pallas kernels for 0% -> 18%
where the time goes in v2:
time: 315 us; the launch traced here: 314 us
  waiting for transfers between devices  96 us (30%)
  starting transfers between devices  67 us (21%)
  blocking collectives  59.7 us (19%)
  Pallas kernels  55.6 us (18%)
  local copies, waits for them, and re-layouts  25.2 us (8%)
  other arithmetic  8.57 us (3%)
    all_to_all x2, blocking collectives, body(): back = lax.all_to_all(g, 'ctx', split_axis=0, concat_axis=0, tiled=True)  59.7 us
    pallas_call x2, Pallas kernels, head_part(): pl.pallas_call(kernel, out_shape=out_shape, in_specs=in_specs, out_specs=...  55.6 us
    all_to_all x1, waiting for transfers between devices, body(): kv = lax.all_to_all(kv, 'ctx', split_axis=0, concat_axis=0, tiled=True)  45.3 us
    ppermute x4, waiting for transfers between devices, passed_along(): return lax.ppermute(value, axis, pairs)  21.6 us
    all_to_all x2, waiting for transfers between devices, body(): qd = lax.all_to_all(qd, 'ctx', split_axis=0, concat_axis=0, tiled=True)  18.4 us
    all_to_all x2, starting transfers between devices, body(): back = lax.all_to_all(dq, 'ctx', split_axis=0, concat_axis=0, tiled=True)  18.4 us
    ppermute x4, starting transfers between devices, passed_along(): return lax.ppermute(value, axis, pairs)  16.6 us
    unnamed x31, local copies, waits for them, and re-layouts  13.1 us
  transfers between devices with their start and end apart: 10, of which 6 were waited for; matrix products, arithmetic and copies ran while one was open for 6% of the time, Pallas kernels for 18%

profile of v2, /device:TPU:1, one launch (start us, length us, event | category | flops | bytes accessed | tf_op | source)
XLA Modules:
  0.0 313.6 jit_solution(7291061260193811107)
XLA Ops:
  0.6 1.7 copy.55
  3.7 1.4 pad_maximum_fusion
  5.1 2.8 copy.57
  7.8 12.0 %all-to-all-start = ((bf16[32,2,128,128]{3,2,1,0:T(8,128)(2,1)}), bf16[32,2,128,128]{3,2,1,0:T(8,128)(2,1)S(1)}, u32[]{:S(2)}, u32[]{:S(2)}) async-start(bf16[32,2,128,128]{3,2,1,0:T(8,128)(2,1)} %bitcast.41), calls=%async_computation | async-start | bytes 4194304 | tf_op jit(solution)/shard_map/all_to_all | solution.py:166
  19.8 2.3 fusion.6
  23.4 45.3 %all-to-all-done.kv_ref = bf16[32,2,128,128]{3,2,1,0:T(8,128)(2,1)S(1)} async-done(((bf16[32,2,128,128]{3,2,1,0:T(8,128)(2,1)}), bf16[32,2,128,128]{3,2,1,0:T(8,128)(2,1)S(1)}, u32[]{:S(2)}, u32[]{:S(2)}) %all-to-all-start) | async-done | bytes 2097184 | tf_op jit(solution)/shard_map/all_to_all | solution.py:166
  68.7 7.0 %all-to-all-start.1 = ((bf16[32,2,64,128]{3,2,1,0:T(8,128)(2,1)}), bf16[32,2,64,128]{3,2,1,0:T(8,128)(2,1)S(1)}, u32[]{:S(2)}, u32[]{:S(2)}) async-start(bf16[32,2,64,128]{3,2,1,0:T(8,128)(2,1)} %bitcast_bitcast_fusion.1), calls=%async_computation.1 | async-start | bytes 2097152 | tf_op jit(solution)/shard_map/all_to_all | solution.py:178
  75.8 1.8 multiply_bitcast_fusion
  77.6 1.7 copy.72
  79.3 2.3 reduce_sum.9
  82.2 18.4 %all-to-all-done.1.qd_ref = bf16[32,2,64,128]{3,2,1,0:T(8,128)(2,1)S(1)} async-done(((bf16[32,2,64,128]{3,2,1,0:T(8,128)(2,1)}), bf16[32,2,64,128]{3,2,1,0:T(8,128)(2,1)S(1)}, u32[]{:S(2)}, u32[]{:S(2)}) %all-to-all-start.1) | async-done | bytes 1048608 | tf_op jit(solution)/shard_map/all_to_all | solution.py:178
  100.7 8.3 %all-to-all-start.2 = ((f32[32,1,128]{2,1,0:T(1,128)}), f32[32,1,128]{2,1,0:T(1,128)S(1)}, u32[]{:S(2)}, u32[]{:S(2)}) async-start(f32[32,1,128]{2,1,0:T(1,128)} %copy.59), calls=%async_computation.2 | async-start | bytes 32768 | tf_op jit(solution)/shard_map/all_to_all | solution.py:163
  110.3 7.3 %all-to-all-done.2 = f32[32,1,128]{2,1,0:T(1,128)S(1)} async-done(((f32[32,1,128]{2,1,0:T(1,128)}), f32[32,1,128]{2,1,0:T(1,128)S(1)}, u32[]{:S(2)}, u32[]{:S(2)}) %all-to-all-start.2) | async-done | bytes 16416 | tf_op jit(solution)/shard_map/all_to_all | solution.py:163
  117.6 4.7 %all-to-all-start.4 = ((bf16[32,2,64,128]{3,2,1,0:T(8,128)(2,1)}), bf16[32,2,64,128]{3,2,1,0:T(8,128)(2,1)}, u32[]{:S(2)}, u32[]{:S(2)}) async-start(bf16[32,2,64,128]{3,2,1,0:T(8,128)(2,1)} %bitcast_bitcast_fusion), calls=%async_computation.4 | async-start | bytes 2097152 | tf_op jit(solution)/shard_map/all_to_all | solution.py:178
  124.0 2.0 copy.60.corr_ref
  126.0 26.6 %shard_map.103 = (bf16[32,64,128]{2,1,0:T(8,128)(2,1)S(1)}, f32[64,64,128]{2,1,0:T(8,128)S(1)}, f32[64,64,128]{2,1,0:T(8,128)S(1)}) custom-call(s32[640]{0:T(1024)S(1)} %min.22.slot_ref, s32[640]{0:T(1024)S(1)} %reshape.79.valid_ref, bf16[32,2,128,128]{3,2,1,0:T(8,128)(2,1)} %copy-done, bf16[32,2,64,128]{3,2,1,0:T(8,128)(2,1)S(1)} %all-to-all-done.1.qd_ref, ...), custom_call_target="tpu_custom_call" | custom-call | tf_op jit(solution)/shard_map/pallas_call | solution.py:134
  152.6 1.3 copy-done.2
  154.0 1.4 copy-done.3
  156.1 9.3 %all-to-all-start.3 = ((bf16[32,64,128]{2,1,0:T(8,128)(2,1)}), bf16[32,64,128]{2,1,0:T(8,128)(2,1)}, u32[]{:S(2)}, u32[]{:S(2)}) async-start(bf16[32,64,128]{2,1,0:T(8,128)(2,1)} %copy-done.5), calls=%async_computation.3 | async-start | bytes 1048576 | tf_op jit(solution)/shard_map/all_to_all | solution.py:185
  165.4 29.0 %shard_map.104 = (bf16[32,64,128]{2,1,0:T(8,128)(2,1)}, bf16[32,128,128]{2,1,0:T(8,128)(2,1)S(1)}, bf16[32,128,128]{2,1,0:T(8,128)(2,1)S(1)}) custom-call(s32[640]{0:T(1024)S(1)} %min.22.slot_ref, s32[640]{0:T(1024)S(1)} %reshape.79.valid_ref, bf16[32,2,128,128]{3,2,1,0:T(8,128)(2,1)S(1)} %copy-done.1, bf16[32,2,64,128]{3,2,1,0:T(8,128)(2,1)} %all-to-all-done.4.qd_ref, ...), custom_call_target="tpu_custom_call" | custom-call | tf_op jit(solution)/shard_map/pallas_call | solution.py:134
  195.4 30.8 %all_to_all.44 = bf16[32,128,128]{2,1,0:T(8,128)(2,1)S(1)} all-to-all(bf16[32,128,128]{2,1,0:T(8,128)(2,1)} %copy-done.4), channel_id=1, replica_groups=mesh['pipe'=8,'ctx'=32] {'ctx'}, dimensions={0} | all-to-all | bytes 2097152 | tf_op jit(solution)/shard_map/all_to_all | solution.py:188
  226.2 28.9 %all_to_all.45 = bf16[32,128,128]{2,1,0:T(8,128)(2,1)} all-to-all(bf16[32,128,128]{2,1,0:T(8,128)(2,1)S(1)} %get-tuple-element.18), channel_id=1, replica_groups=mesh['pipe'=8,'ctx'=32] {'ctx'}, dimensions={0} | all-to-all | bytes 2097152 | tf_op jit(solution)/shard_map/all_to_all | solution.py:188
  255.1 9.1 %all-to-all-start.5 = ((bf16[32,64,128]{2,1,0:T(8,128)(2,1)}), bf16[32,64,128]{2,1,0:T(8,128)(2,1)S(1)}, u32[]{:S(2)}, u32[]{:S(2)}) async-start(bf16[32,64,128]{2,1,0:T(8,128)(2,1)} %get-tuple-element.16), calls=%async_computation.5 | async-start | bytes 1048576 | tf_op jit(solution)/shard_map/all_to_all | solution.py:185
  264.2 5.1 %collective-permute-start.3 = (bf16[32,128,128]{2,1,0:T(8,128)(2,1)}, bf16[32,128,128]{2,1,0:T(8,128)(2,1)}, u32[]{:S(2)}, u32[]{:S(2)}) collective-permute-start(bf16[32,128,128]{2,1,0:T(8,128)(2,1)} %all_to_all.45), channel_id=1, source_target_pairs={{0,224},{32,0},{64,32},{96,64},{128,96},{160,128},{192,160},{224,1... | collective-permute-start | bytes 3145736 | tf_op jit(solution)/shard_map/ppermute | solution.py:20
  269.4 3.1 collective-permute-start
  272.5 3.2 %all-to-all-done.5 = bf16[32,64,128]{2,1,0:T(8,128)(2,1)S(1)} async-done(((bf16[32,64,128]{2,1,0:T(8,128)(2,1)}), bf16[32,64,128]{2,1,0:T(8,128)(2,1)S(1)}, u32[]{:S(2)}, u32[]{:S(2)}) %all-to-all-start.5) | async-done | bytes 524320 | tf_op jit(solution)/shard_map/all_to_all | solution.py:185
  275.7 8.3 %collective-permute-start.1 = (bf16[32,64,128]{2,1,0:T(8,128)(2,1)S(1)}, bf16[32,64,128]{2,1,0:T(8,128)(2,1)S(1)}, u32[]{:S(2)}, u32[]{:S(2)}) collective-permute-start(bf16[32,64,128]{2,1,0:T(8,128)(2,1)S(1)} %all-to-all-done.5), channel_id=1, source_target_pairs={{0,224},{32,0},{64,32},{96,64},{128,96},{160,128},{192,160},{224,1... | collective-permute-start | bytes 1572872 | tf_op jit(solution)/shard_map/ppermute | solution.py:20
  284.1 16.0 %collective-permute-done = bf16[32,64,128]{2,1,0:T(8,128)(2,1)S(1)} collective-permute-done((bf16[32,64,128]{2,1,0:T(8,128)(2,1)}, bf16[32,64,128]{2,1,0:T(8,128)(2,1)S(1)}, u32[]{:S(2)}, u32[]{:S(2)}) %collective-permute-start) | collective-permute-done | bytes 524320 | tf_op jit(solution)/shard_map/ppermute | solution.py:20
  300.1 5.6 %collective-permute-done.1 = bf16[32,64,128]{2,1,0:T(8,128)(2,1)S(1)} collective-permute-done((bf16[32,64,128]{2,1,0:T(8,128)(2,1)S(1)}, bf16[32,64,128]{2,1,0:T(8,128)(2,1)S(1)}, u32[]{:S(2)}, u32[]{:S(2)}) %collective-permute-start.1) | collective-permute-done | bytes 524320 | tf_op jit(solution)/shard_map/ppermute | solution.py:20
  306.5 1.3 copy.66
  307.8 1.6 copy.65
  310.7 1.6 copy.64
  (52 shorter events, 10.7 us)
Async XLA Ops:
  0.6 1.7 copy-start.9
  7.8 12.0 %copy-start.6 = (bf16[1,128,4096]{2,1,0:T(8,128)(2,1)S(1)}, bf16[1,128,4096]{2,1,0:T(8,128)(2,1)}, u32[]{:S(2)}) copy-start(bf16[1,128,4096]{2,1,0:T(8,128)(2,1)} %param.12) | copy-start | bytes 3145732
  7.8 60.9 %all-to-all-start = ((bf16[32,2,128,128]{3,2,1,0:T(8,128)(2,1)}), bf16[32,2,128,128]{3,2,1,0:T(8,128)(2,1)S(1)}, u32[]{:S(2)}, u32[]{:S(2)}) async-start(bf16[32,2,128,128]{3,2,1,0:T(8,128)(2,1)} %bitcast.41), calls=%async_computation | async-start | bytes 4194304 | tf_op jit(solution)/shard_map/all_to_all | solution.py:166
  68.7 8.8 %copy-start = (bf16[32,2,128,128]{3,2,1,0:T(8,128)(2,1)}, bf16[32,2,128,128]{3,2,1,0:T(8,128)(2,1)S(1)}, u32[]{:S(2)}) copy-start(bf16[32,2,128,128]{3,2,1,0:T(8,128)(2,1)S(1)} %all-to-all-done.kv_ref) | copy-start | bytes 6291460
  68.7 31.9 %all-to-all-start.1 = ((bf16[32,2,64,128]{3,2,1,0:T(8,128)(2,1)}), bf16[32,2,64,128]{3,2,1,0:T(8,128)(2,1)S(1)}, u32[]{:S(2)}, u32[]{:S(2)}) async-start(bf16[32,2,64,128]{3,2,1,0:T(8,128)(2,1)} %bitcast_bitcast_fusion.1), calls=%async_computation.1 | async-start | bytes 2097152 | tf_op jit(solution)/shard_map/all_to_all | solution.py:178
  79.3 29.7 %copy-start.7 = (bf16[1,64,4096]{2,1,0:T(8,128)(2,1)S(1)}, bf16[1,64,4096]{2,1,0:T(8,128)(2,1)}, u32[]{:S(2)}) copy-start(bf16[1,64,4096]{2,1,0:T(8,128)(2,1)} %get-tuple-element.29) | copy-start | bytes 1572868
  79.3 29.7 %copy-start.8 = (bf16[1,64,4096]{2,1,0:T(8,128)(2,1)S(1)}, bf16[1,64,4096]{2,1,0:T(8,128)(2,1)}, u32[]{:S(2)}) copy-start(bf16[1,64,4096]{2,1,0:T(8,128)(2,1)} %get-tuple-element.32) | copy-start | bytes 1572868
  100.7 17.0 %all-to-all-start.2 = ((f32[32,1,128]{2,1,0:T(1,128)}), f32[32,1,128]{2,1,0:T(1,128)S(1)}, u32[]{:S(2)}, u32[]{:S(2)}) async-start(f32[32,1,128]{2,1,0:T(1,128)} %copy.59), calls=%async_computation.2 | async-start | bytes 32768 | tf_op jit(solution)/shard_map/all_to_all | solution.py:163
  109.0 14.0 %copy-start.10 = (s32[1,1,64,3]{2,1,3,0:T(1,128)S(1)}, s32[1,1,64,3]{2,1,3,0:T(1,128)}, u32[]{:S(2)}) copy-start(s32[1,1,64,3]{2,1,3,0:T(1,128)} %param.13) | copy-start | bytes 2308
  109.0 14.0 %copy-start.11 = (s32[1,2]{1,0:T(1,128)S(1)}, s32[1,2]{1,0:T(1,128)}, u32[]{:S(2)}) copy-start(s32[1,2]{1,0:T(1,128)} %param.14) | copy-start | bytes 28
  117.6 38.5 %all-to-all-start.4 = ((bf16[32,2,64,128]{3,2,1,0:T(8,128)(2,1)}), bf16[32,2,64,128]{3,2,1,0:T(8,128)(2,1)}, u32[]{:S(2)}, u32[]{:S(2)}) async-start(bf16[32,2,64,128]{3,2,1,0:T(8,128)(2,1)} %bitcast_bitcast_fusion), calls=%async_computation.4 | async-start | bytes 2097152 | tf_op jit(solution)/shard_map/all_to_all | solution.py:178
  126.0 39.4 %copy-start.1 = (bf16[32,2,128,128]{3,2,1,0:T(8,128)(2,1)S(1)}, bf16[32,2,128,128]{3,2,1,0:T(8,128)(2,1)}, u32[]{:S(2)}) copy-start(bf16[32,2,128,128]{3,2,1,0:T(8,128)(2,1)} %copy-done) | copy-start | bytes 6291460
  152.6 1.3 copy-start.2
  154.0 1.4 copy-start.3
  155.3 0.8 copy-start.5
  156.1 39.2 %all-to-all-start.3 = ((bf16[32,64,128]{2,1,0:T(8,128)(2,1)}), bf16[32,64,128]{2,1,0:T(8,128)(2,1)}, u32[]{:S(2)}, u32[]{:S(2)}) async-start(bf16[32,64,128]{2,1,0:T(8,128)(2,1)} %copy-done.5), calls=%async_computation.3 | async-start | bytes 1048576 | tf_op jit(solution)/shard_map/all_to_all | solution.py:185
  194.4 1.0 copy-start.4
  255.1 20.6 %all-to-all-start.5 = ((bf16[32,64,128]{2,1,0:T(8,128)(2,1)}), bf16[32,64,128]{2,1,0:T(8,128)(2,1)S(1)}, u32[]{:S(2)}, u32[]{:S(2)}) async-start(bf16[32,64,128]{2,1,0:T(8,128)(2,1)} %get-tuple-element.16), calls=%async_computation.5 | async-start | bytes 1048576 | tf_op jit(solution)/shard_map/all_to_all | solution.py:185
  264.2 43.6 %collective-permute-start.3 = (bf16[32,128,128]{2,1,0:T(8,128)(2,1)}, bf16[32,128,128]{2,1,0:T(8,128)(2,1)}, u32[]{:S(2)}, u32[]{:S(2)}) collective-permute-start(bf16[32,128,128]{2,1,0:T(8,128)(2,1)} %all_to_all.45), channel_id=1, source_target_pairs={{0,224},{32,0},{64,32},{96,64},{128,96},{160,128},{192,160},{224,1... | collective-permute-start | bytes 3145736 | tf_op jit(solution)/shard_map/ppermute | solution.py:20
  269.3 41.4 %collective-permute-start.2 = (bf16[32,128,128]{2,1,0:T(8,128)(2,1)S(1)}, bf16[32,128,128]{2,1,0:T(8,128)(2,1)}, u32[]{:S(2)}, u32[]{:S(2)}) collective-permute-start(bf16[32,128,128]{2,1,0:T(8,128)(2,1)S(1)} %all_to_all.44), channel_id=1, source_target_pairs={{0,224},{32,0},{64,32},{96,64},{128,96},{160,128},{192,160},{224,1... | collective-permute-start | bytes 3145736 | tf_op jit(solution)/shard_map/ppermute | solution.py:20
  269.4 30.7 %collective-permute-start = (bf16[32,64,128]{2,1,0:T(8,128)(2,1)}, bf16[32,64,128]{2,1,0:T(8,128)(2,1)S(1)}, u32[]{:S(2)}, u32[]{:S(2)}) collective-permute-start(bf16[32,64,128]{2,1,0:T(8,128)(2,1)} %all-to-all-done.3), channel_id=1, source_target_pairs={{0,224},{32,0},{64,32},{96,64},{128,96},{160,128},{192,160},{224,1... | collective-permute-start | bytes 1572872 | tf_op jit(solution)/shard_map/ppermute | solution.py:20
  275.7 30.0 %collective-permute-start.1 = (bf16[32,64,128]{2,1,0:T(8,128)(2,1)S(1)}, bf16[32,64,128]{2,1,0:T(8,128)(2,1)S(1)}, u32[]{:S(2)}, u32[]{:S(2)}) collective-permute-start(bf16[32,64,128]{2,1,0:T(8,128)(2,1)S(1)} %all-to-all-done.5), channel_id=1, source_target_pairs={{0,224},{32,0},{64,32},{96,64},{128,96},{160,128},{192,160},{224,1... | collective-permute-start | bytes 1572872 | tf_op jit(solution)/shard_map/ppermute | solution.py:20

commit v3 on v2

--- a/solution.py
+++ b/solution.py
@@ -42,7 +42,11 @@
 def head_kernel(slot_ref, valid_ref, kv_ref, qd_ref, corr_ref, *rest, block_count,
                 chunk_rows, parity, final):
     if final:
-        (dk_prev, dv_prev, dq_ref, dk_ref, dv_ref, kt_ref, vt_ref, dk_acc, dv_acc) = rest
+        (dq_prev, dk_prev, dv_prev, out_ref, kt_ref, vt_ref, dk_acc, dv_acc) = rest
+        out_ref[:, 0:parity * BLK, :] = dq_prev[...]
+        dq_ref = out_ref.at[:, parity * BLK:(parity + 1) * BLK, :]
+        dk_ref = out_ref.at[:, chunk_rows:2 * chunk_rows, :]
+        dv_ref = out_ref.at[:, 2 * chunk_rows:3 * chunk_rows, :]
     else:
         (dq_ref, dk_acc, dv_acc, kt_ref, vt_ref) = rest
     score_scale = HD ** (-0.5)
@@ -60,8 +64,8 @@
             kb = slot_ref[i * KB + j]
             kc = kb // per_chunk
             kr = pl.multiple_of((kb % per_chunk) * BLK, BLK)
-            kt_ref[pl.ds(j * BLK, BLK), :] = kv_ref[kc, 0, pl.ds(kr, BLK), :]
-            vt_ref[pl.ds(j * BLK, BLK), :] = kv_ref[kc, 1, pl.ds(kr, BLK), :]
+            kt_ref[pl.ds(j * BLK, BLK), :] = kv_ref[kc, pl.ds(kr, BLK), :]
+            vt_ref[pl.ds(j * BLK, BLK), :] = kv_ref[kc, pl.ds(chunk_rows + kr, BLK), :]
             live = live | ((lane_slot == j) & (valid_ref[i * KB + j] != 0))
         key_tiles = kt_ref[...]
         value_tiles = vt_ref[...]
@@ -116,7 +120,6 @@
     final = previous is not None
     dq_shape = jax.ShapeDtypeStruct((chunks, BLK, HD), jnp.bfloat16)
     acc_shape = jax.ShapeDtypeStruct((block_count, BLK, HD), jnp.float32)
-    grad_shape = jax.ShapeDtypeStruct((chunks, chunk_rows, HD), jnp.bfloat16)
     kernel = functools.partial(
         head_kernel, block_count=block_count, chunk_rows=chunk_rows, parity=parity, final=final
     )
@@ -124,7 +127,7 @@
     scratch = [pltpu.VMEM((KB * BLK, HD), jnp.bfloat16), pltpu.VMEM((KB * BLK, HD), jnp.bfloat16)]
     if final:
         operands += list(previous)
-        out_shape = (dq_shape, grad_shape, grad_shape)
+        out_shape = (jax.ShapeDtypeStruct((chunks, 3 * chunk_rows, HD), jnp.bfloat16),)
         scratch += [pltpu.VMEM((block_count, BLK, HD), jnp.float32)] * 2
     else:
         out_shape = (dq_shape, acc_shape, acc_shape)
@@ -144,6 +147,16 @@
 def to_chunks(rows, chunks):
     count, local, width = rows.shape
     return rows.reshape(count, local, chunks, width // chunks).transpose(2, 0, 1, 3)
+
+
+def split_pieces(value, count):
+    pieces = []
+    rest = value
+    for _ in range(count):
+        piece = lax.optimization_barrier(rest.astype(jnp.bfloat16))
+        pieces.append(piece)
+        rest = rest - piece.astype(jnp.float32)
+    return pieces
 
 
 def body(queries, keys, values, attn_out, out_grad, random_blocks, global_blocks, radius):
@@ -160,35 +173,32 @@
         ),
         axis=-1,
     )
-    correction = lax.all_to_all(correction.T, "ctx", split_axis=0, concat_axis=0, tiled=True)
-    correction = correction.reshape(length, 1)
-    kv = to_chunks(jnp.stack([keys[0], values[0]], axis=0), chunks)
+    pieces = jnp.stack(split_pieces(correction.T, 3), axis=1)
+    pieces = jnp.pad(pieces, ((0, 0), (0, 8 - pieces.shape[1]), (0, 0)))
+    kv = to_chunks(jnp.stack([keys[0], values[0]], axis=0), chunks).reshape(chunks, 2 * local, HD)
+    kv = jnp.concatenate([kv, pieces], axis=1)
     kv = lax.all_to_all(kv, "ctx", split_axis=0, concat_axis=0, tiled=True)
+    got = kv[:, 2 * local:2 * local + 3, :].astype(jnp.float32)
+    correction = ((got[:, 0] + got[:, 1]) + got[:, 2]).reshape(length, 1)
     slot_index, slot_valid = slot_table(
         random_blocks[0, 0], global_blocks[0], radius[0, 0], block_count
     )
     previous = None
     after = kv
-    dq_parts = []
-    returned = []
     for parity in range(per_chunk):
         rows = slice(parity * BLK, (parity + 1) * BLK)
         qd = to_chunks(jnp.stack([queries[0, rows], out_grad[0, rows]], axis=0), chunks)
         qd, _ = lax.optimization_barrier((qd, after))
         qd = lax.all_to_all(qd, "ctx", split_axis=0, concat_axis=0, tiled=True)
         after = qd
-        dq, dk, dv = head_part(
+        result = head_part(
             kv, qd, correction, slot_index, slot_valid, previous, block_count, chunks, local,
             parity,
         )
-        previous = (dk, dv)
-        back = lax.all_to_all(dq, "ctx", split_axis=0, concat_axis=0, tiled=True)
-        dq_parts.append(passed_along(back, "pipe", -1))
-    for g in previous:
-        back = lax.all_to_all(g, "ctx", split_axis=0, concat_axis=0, tiled=True)
-        returned.append(passed_along(back, "pipe", -1))
-    dq_all = jnp.concatenate(dq_parts, axis=1)
-    outs = [dq_all] + returned
+        previous = result
+    back = lax.all_to_all(result[0], "ctx", split_axis=0, concat_axis=0, tiled=True)
+    back = passed_along(back, "pipe", -1)
+    outs = [back[:, k * local:(k + 1) * local] for k in range(3)]
     return tuple(o.transpose(1, 0, 2).reshape(1, local, chunks * HD) for o in outs)
 
 

time: 315 us -> 306 us (0.971)
  starting transfers between devices: 67 us -> 32.7 us
  blocking collectives: 59.7 us -> 78.8 us
  waiting for transfers between devices: 96 us -> 107 us
  local copies, waits for them, and re-layouts: 25.2 us -> 19.1 us
    all_to_all x3 -> x0, starting transfers between devices: 26.7 us -> none  [the longest x2 18.4 us: body(): back = lax.all_to_all(dq, 'ctx', split_axis=0, concat_axis=0, tiled=True)]
    all_to_all x2 -> x1, blocking collectives: 59.7 us -> 78.8 us  [body(): lax.all_to_all(result[0], 'ctx', split_axis=0, concat_axis=0, tiled=True)]
    ppermute x4 -> x1, waiting for transfers between devices: 21.6 us -> 36.1 us  [passed_along(): return lax.ppermute(value, axis, pairs)]
    ppermute x4 -> x1, starting transfers between devices: 16.6 us -> 5.07 us  [passed_along(): return lax.ppermute(value, axis, pairs)]
    all_to_all x3 -> x0, waiting for transfers between devices: 10.6 us -> none  [the longest x1 7.35 us: body(): lax.all_to_all(correction.T, 'ctx', split_axis=0, concat_axis=0, tiled=True)]
    reshape x2 -> x0, local copies, waits for them, and re-layouts: 4.71 us -> none  [the longest x1 2.76 us: to_chunks(): rows.reshape(count, local, chunks, width // chunks).transpose(2, 0, 1, 3)]
    all_to_all x2, waiting for transfers between devices: 18.4 us -> 22.7 us  [body(): qd = lax.all_to_all(qd, 'ctx', split_axis=0, concat_axis=0, tiled=True)]
    all_to_all x2, starting transfers between devices: 11.7 us -> 15.5 us  [body(): qd = lax.all_to_all(qd, 'ctx', split_axis=0, concat_axis=0, tiled=True)]
  transfers between devices with their start and end apart: 10 -> 4, of which waited for: 6 -> 3; matrix products, arithmetic and copies ran while one was open for 6% -> 2% of each run, Pallas kernels for 18% -> 9%
where the time goes in v3:
time: 306 us; the launch traced here: 305 us
  waiting for transfers between devices  107 us (35%)
  blocking collectives  78.8 us (26%)
  Pallas kernels  56 us (18%)
  starting transfers between devices  32.7 us (11%)
  local copies, waits for them, and re-layouts  19.1 us (6%)
  other arithmetic  9.68 us (3%)
    all_to_all x1, blocking collectives, body(): lax.all_to_all(result[0], 'ctx', split_axis=0, concat_axis=0, tiled=True)  78.8 us
    pallas_call x2, Pallas kernels, head_part(): pl.pallas_call(kernel, out_shape=out_shape, in_specs=in_specs, out_specs=...  56 us
    all_to_all x1, waiting for transfers between devices, body(): kv = lax.all_to_all(kv, 'ctx', split_axis=0, concat_axis=0, tiled=True)  48.6 us
    ppermute x1, waiting for transfers between devices, passed_along(): return lax.ppermute(value, axis, pairs)  36.1 us
    all_to_all x2, waiting for transfers between devices, body(): qd = lax.all_to_all(qd, 'ctx', split_axis=0, concat_axis=0, tiled=True)  22.7 us
    all_to_all x2, starting transfers between devices, body(): qd = lax.all_to_all(qd, 'ctx', split_axis=0, concat_axis=0, tiled=True)  15.5 us
    all_to_all x1, starting transfers between devices, body(): kv = lax.all_to_all(kv, 'ctx', split_axis=0, concat_axis=0, tiled=True)  12.1 us
    unnamed x31, local copies, waits for them, and re-layouts  11.9 us
  transfers between devices with their start and end apart: 4, of which 3 were waited for; matrix products, arithmetic and copies ran while one was open for 2% of the time, Pallas kernels for 9%

profile of v3, /device:TPU:1, one launch (start us, length us, event | category | flops | bytes accessed | tf_op | source)
XLA Modules:
  0.0 305.2 jit_solution(13111741193315126242)
XLA Ops:
  0.6 1.8 multiply_bitcast_fusion
  2.4 0.4 copy.125
  2.8 0.6 reduce_sum.9
  4.0 1.8 copy_bitcast_fusion
  5.9 1.5 pad_maximum_fusion
  7.4 12.1 %all-to-all-start = ((bf16[32,264,128]{2,1,0:T(8,128)(2,1)}), bf16[32,264,128]{2,1,0:T(8,128)(2,1)}, u32[]{:S(2)}, u32[]{:S(2)}) async-start(bf16[32,264,128]{2,1,0:T(8,128)(2,1)} %pad_maximum_fusion), calls=%async_computation | async-start | bytes 4325376 | tf_op jit(solution)/shard_map/all_to_all | solution.py:180
  19.8 1.3 bitcast_bitcast_fusion
  21.1 48.6 %all-to-all-done.kv_ref = bf16[32,264,128]{2,1,0:T(8,128)(2,1)} async-done(((bf16[32,264,128]{2,1,0:T(8,128)(2,1)}), bf16[32,264,128]{2,1,0:T(8,128)(2,1)}, u32[]{:S(2)}, u32[]{:S(2)}) %all-to-all-start) | async-done | bytes 2162720 | tf_op jit(solution)/shard_map/all_to_all | solution.py:180
  69.6 7.2 %all-to-all-start.1 = ((bf16[32,2,64,128]{3,2,1,0:T(8,128)(2,1)}), bf16[32,2,64,128]{3,2,1,0:T(8,128)(2,1)S(1)}, u32[]{:S(2)}, u32[]{:S(2)}) async-start(bf16[32,2,64,128]{3,2,1,0:T(8,128)(2,1)} %bitcast_bitcast_fusion), calls=%async_computation.1 | async-start | bytes 2097152 | tf_op jit(solution)/shard_map/all_to_all | solution.py:192
  77.7 1.3 bitcast_bitcast_fusion.1
  79.1 22.7 %all-to-all-done.1.qd_ref = bf16[32,2,64,128]{3,2,1,0:T(8,128)(2,1)S(1)} async-done(((bf16[32,2,64,128]{3,2,1,0:T(8,128)(2,1)}), bf16[32,2,64,128]{3,2,1,0:T(8,128)(2,1)S(1)}, u32[]{:S(2)}, u32[]{:S(2)}) %all-to-all-start.1) | async-done | bytes 1048608 | tf_op jit(solution)/shard_map/all_to_all | solution.py:192
  101.8 8.3 %all-to-all-start.2 = ((bf16[32,2,64,128]{3,2,1,0:T(8,128)(2,1)}), bf16[32,2,64,128]{3,2,1,0:T(8,128)(2,1)S(1)}, u32[]{:S(2)}, u32[]{:S(2)}) async-start(bf16[32,2,64,128]{3,2,1,0:T(8,128)(2,1)} %bitcast_bitcast_fusion.1), calls=%async_computation.2 | async-start | bytes 2097152 | tf_op jit(solution)/shard_map/all_to_all | solution.py:192
  110.8 0.8 slice_convert_fusion
  111.7 2.0 copy.108.corr_ref
  113.8 1.2 copy-done.2
  115.0 26.8 %shard_map.103 = (bf16[32,64,128]{2,1,0:T(8,128)(2,1)S(1)}, f32[64,64,128]{2,1,0:T(8,128)S(1)}, f32[64,64,128]{2,1,0:T(8,128)S(1)}) custom-call(s32[640]{0:T(1024)S(1)} %min.22.slot_ref, s32[640]{0:T(1024)S(1)} %reshape.106.valid_ref, bf16[32,264,128]{2,1,0:T(8,128)(2,1)} %all-to-all-done.kv_ref, bf16[32,2,64,128]{3,2,1,0:T(8,128)(2,1)S(1)} %copy-done.2, ...), custom_call_target="tpu_custom_call" | custom-call | tf_op jit(solution)/shard_map/pallas_call | solution.py:137
  141.8 1.4 copy-done.3
  143.2 1.3 copy-done.5
  144.5 0.8 copy-done.6
  145.3 1.6 copy-done.4
  146.9 1.0 copy-done.7
  147.9 29.2 %shard_map.104 = bf16[32,384,128]{2,1,0:T(8,128)(2,1)} custom-call(s32[640]{0:T(1024)S(1)} %min.22.slot_ref, s32[640]{0:T(1024)S(1)} %reshape.106.valid_ref, bf16[32,264,128]{2,1,0:T(8,128)(2,1)} %all-to-all-done.kv_ref, bf16[32,2,64,128]{3,2,1,0:T(8,128)(2,1)S(1)} %all-to-all-done.2.qd_ref, f32[4096,1]{1,0:T(8,128)S(1)} %copy-done, ...), custom_call_target="tpu_custom_call" | custom-call | tf_op jit(solution)/shard_map/pallas_call | solution.py:137
  177.1 78.8 %all_to_all.20 = bf16[32,384,128]{2,1,0:T(8,128)(2,1)S(1)} all-to-all(bf16[32,384,128]{2,1,0:T(8,128)(2,1)} %shard_map.104), channel_id=1, replica_groups=mesh['pipe'=8,'ctx'=32] {'ctx'}, dimensions={0} | all-to-all | bytes 6291456 | tf_op jit(solution)/shard_map/all_to_all | solution.py:199
  255.9 5.1 %collective-permute-start = (bf16[32,384,128]{2,1,0:T(8,128)(2,1)S(1)}, bf16[32,384,128]{2,1,0:T(8,128)(2,1)S(1)}, u32[]{:S(2)}, u32[]{:S(2)}) collective-permute-start(bf16[32,384,128]{2,1,0:T(8,128)(2,1)S(1)} %all_to_all.20), channel_id=1, source_target_pairs={{0,224},{32,0},{64,32},{96,64},{128,96},{160,128},{192,160},{224,1... | collective-permute-start | bytes 9437192 | tf_op jit(solution)/shard_map/ppermute | solution.py:20
  261.0 36.1 %collective-permute-done = bf16[32,384,128]{2,1,0:T(8,128)(2,1)S(1)} collective-permute-done((bf16[32,384,128]{2,1,0:T(8,128)(2,1)S(1)}, bf16[32,384,128]{2,1,0:T(8,128)(2,1)S(1)}, u32[]{:S(2)}, u32[]{:S(2)}) %collective-permute-start) | collective-permute-done | bytes 3145760 | tf_op jit(solution)/shard_map/ppermute | solution.py:20
  297.1 1.2 slice_bitcast_fusion
  298.4 1.6 copy.111
  300.0 1.3 copy.114
  301.3 0.7 copy.110
  302.0 1.3 copy.113
  303.3 0.7 copy.109
  303.9 1.3 copy.112
  (47 shorter events, 1.9 us)
Async XLA Ops:
  2.8 1.2 copy-start.9
  7.4 12.1 %copy-start.8 = (bf16[1,128,4096]{2,1,0:T(8,128)(2,1)S(1)}, bf16[1,128,4096]{2,1,0:T(8,128)(2,1)}, u32[]{:S(2)}) copy-start(bf16[1,128,4096]{2,1,0:T(8,128)(2,1)} %param.12) | copy-start | bytes 3145732
  7.4 12.1 %copy-start.10 = (bf16[1,128,4096]{2,1,0:T(8,128)(2,1)S(1)}, bf16[1,128,4096]{2,1,0:T(8,128)(2,1)}, u32[]{:S(2)}) copy-start(bf16[1,128,4096]{2,1,0:T(8,128)(2,1)} %param.8) | copy-start | bytes 3145732
  7.4 62.2 %all-to-all-start = ((bf16[32,264,128]{2,1,0:T(8,128)(2,1)}), bf16[32,264,128]{2,1,0:T(8,128)(2,1)}, u32[]{:S(2)}, u32[]{:S(2)}) async-start(bf16[32,264,128]{2,1,0:T(8,128)(2,1)} %pad_maximum_fusion), calls=%async_computation | async-start | bytes 4325376 | tf_op jit(solution)/shard_map/all_to_all | solution.py:180
  19.8 57.7 %copy-start.11 = (s32[1,1,64,3]{2,1,3,0:T(1,128)S(1)}, s32[1,1,64,3]{2,1,3,0:T(1,128)}, u32[]{:S(2)}) copy-start(s32[1,1,64,3]{2,1,3,0:T(1,128)} %param.13) | copy-start | bytes 2308
  19.8 57.8 %copy-start.12 = (s32[1,2]{1,0:T(1,128)S(1)}, s32[1,2]{1,0:T(1,128)}, u32[]{:S(2)}) copy-start(s32[1,2]{1,0:T(1,128)} %param.14) | copy-start | bytes 28
  69.6 32.1 %all-to-all-start.1 = ((bf16[32,2,64,128]{3,2,1,0:T(8,128)(2,1)}), bf16[32,2,64,128]{3,2,1,0:T(8,128)(2,1)S(1)}, u32[]{:S(2)}, u32[]{:S(2)}) async-start(bf16[32,2,64,128]{3,2,1,0:T(8,128)(2,1)} %bitcast_bitcast_fusion), calls=%async_computation.1 | async-start | bytes 2097152 | tf_op jit(solution)/shard_map/all_to_all | solution.py:192
  101.8 10.0 %copy-start.1 = (bf16[32,2,64,128]{3,2,1,0:T(8,128)(2,1)}, bf16[32,2,64,128]{3,2,1,0:T(8,128)(2,1)S(1)}, u32[]{:S(2)}) copy-start(bf16[32,2,64,128]{3,2,1,0:T(8,128)(2,1)S(1)} %all-to-all-done.1.qd_ref) | copy-start | bytes 3145732
  101.8 43.5 %all-to-all-start.2 = ((bf16[32,2,64,128]{3,2,1,0:T(8,128)(2,1)}), bf16[32,2,64,128]{3,2,1,0:T(8,128)(2,1)S(1)}, u32[]{:S(2)}, u32[]{:S(2)}) async-start(bf16[32,2,64,128]{3,2,1,0:T(8,128)(2,1)} %bitcast_bitcast_fusion.1), calls=%async_computation.2 | async-start | bytes 2097152 | tf_op jit(solution)/shard_map/all_to_all | solution.py:192
  113.8 1.2 copy-start.2
  115.0 30.3 %copy-start = (f32[4096,1]{1,0:T(8,128)S(1)}, f32[4096,1]{1,0:T(8,128)}, u32[]{:S(2)}) copy-start(f32[4096,1]{1,0:T(8,128)} %copy.108.corr_ref) | copy-start | bytes 49156
  141.8 1.4 copy-start.3
  143.2 1.3 copy-start.5
  144.5 0.8 copy-start.6
  145.3 1.6 copy-start.4
  146.9 1.0 copy-start.7
  255.9 41.2 %collective-permute-start = (bf16[32,384,128]{2,1,0:T(8,128)(2,1)S(1)}, bf16[32,384,128]{2,1,0:T(8,128)(2,1)S(1)}, u32[]{:S(2)}, u32[]{:S(2)}) collective-permute-start(bf16[32,384,128]{2,1,0:T(8,128)(2,1)S(1)} %all_to_all.20), channel_id=1, source_target_pairs={{0,224},{32,0},{64,32},{96,64},{128,96},{160,128},{192,160},{224,1... | collective-permute-start | bytes 9437192 | tf_op jit(solution)/shard_map/ppermute | solution.py:20

commit v4 on v3

--- a/solution.py
+++ b/solution.py
@@ -6,6 +6,7 @@
 from jax.experimental import pallas as pl
 from jax.experimental.pallas import tpu as pltpu
 from jax.sharding import PartitionSpec as P
+
 
 HD = 128
 BLK = 64
@@ -178,26 +179,28 @@
     kv = to_chunks(jnp.stack([keys[0], values[0]], axis=0), chunks).reshape(chunks, 2 * local, HD)
     kv = jnp.concatenate([kv, pieces], axis=1)
     kv = lax.all_to_all(kv, "ctx", split_axis=0, concat_axis=0, tiled=True)
+    after = kv
+    kv = passed_along(kv, "pipe", -1)
     got = kv[:, 2 * local:2 * local + 3, :].astype(jnp.float32)
     correction = ((got[:, 0] + got[:, 1]) + got[:, 2]).reshape(length, 1)
-    slot_index, slot_valid = slot_table(
-        random_blocks[0, 0], global_blocks[0], radius[0, 0], block_count
-    )
+    random_list = passed_along(random_blocks[0, 0], "pipe", -1)
+    global_list = passed_along(global_blocks[0], "pipe", -1)
+    head_radius = passed_along(radius[0, 0], "pipe", -1)
+    slot_index, slot_valid = slot_table(random_list, global_list, head_radius, block_count)
     previous = None
-    after = kv
     for parity in range(per_chunk):
         rows = slice(parity * BLK, (parity + 1) * BLK)
         qd = to_chunks(jnp.stack([queries[0, rows], out_grad[0, rows]], axis=0), chunks)
         qd, _ = lax.optimization_barrier((qd, after))
         qd = lax.all_to_all(qd, "ctx", split_axis=0, concat_axis=0, tiled=True)
         after = qd
+        qd = passed_along(qd, "pipe", -1)
         result = head_part(
             kv, qd, correction, slot_index, slot_valid, previous, block_count, chunks, local,
             parity,
         )
         previous = result
     back = lax.all_to_all(result[0], "ctx", split_axis=0, concat_axis=0, tiled=True)
-    back = passed_along(back, "pipe", -1)
     outs = [back[:, k * local:(k + 1) * local] for k in range(3)]
     return tuple(o.transpose(1, 0, 2).reshape(1, local, chunks * HD) for o in outs)
 

time: 306 us -> 287 us (0.938); the launches traced: 305 us -> 282 us
  waiting for transfers between devices: 107 us -> 87.8 us
  starting transfers between devices: 32.7 us -> 39 us
  local copies, waits for them, and re-layouts: 19.1 us -> 13.1 us
  blocking collectives: 78.8 us -> 73.9 us
    ppermute x1 -> x6, waiting for transfers between devices: 36.1 us -> 0.46 us  [passed_along(): return lax.ppermute(value, axis, pairs)]
    all_to_all x2, waiting for transfers between devices: 22.7 us -> 38.7 us  [body(): qd = lax.all_to_all(qd, 'ctx', split_axis=0, concat_axis=0, tiled=True)]
    ppermute x1 -> x6, starting transfers between devices: 5.07 us -> 11.3 us  [passed_along(): return lax.ppermute(value, axis, pairs)]
    unnamed x31 -> x19, local copies, waits for them, and re-layouts: 11.9 us -> 5.91 us
    all_to_all x1, blocking collectives: 78.8 us -> 73.9 us  [body(): lax.all_to_all(result[0], 'ctx', split_axis=0, concat_axis=0, tiled=True)]
  transfers between devices with their start and end apart: 4 -> 9, of which waited for: 3 -> 5; matrix products, arithmetic and copies ran while one was open for 2% -> 3% of each run, Pallas kernels for 9% -> 10%
where the time goes in v4:
time: 287 us; the launch traced here: 282 us
  waiting for transfers between devices  87.8 us (31%)
  blocking collectives  73.9 us (26%)
  Pallas kernels  56.1 us (20%)
  starting transfers between devices  39 us (14%)
  local copies, waits for them, and re-layouts  13.1 us (5%)
  other arithmetic  11.6 us (4%)
    all_to_all x1, blocking collectives, body(): lax.all_to_all(result[0], 'ctx', split_axis=0, concat_axis=0, tiled=True)  73.9 us
    pallas_call x2, Pallas kernels, head_part(): pl.pallas_call(kernel, out_shape=out_shape, in_specs=in_specs, out_specs=...  56.1 us
    all_to_all x1, waiting for transfers between devices, body(): kv = lax.all_to_all(kv, 'ctx', split_axis=0, concat_axis=0, tiled=True)  48.6 us
    all_to_all x2, waiting for transfers between devices, body(): qd = lax.all_to_all(qd, 'ctx', split_axis=0, concat_axis=0, tiled=True)  38.7 us
    all_to_all x2, starting transfers between devices, body(): qd = lax.all_to_all(qd, 'ctx', split_axis=0, concat_axis=0, tiled=True)  15.7 us
    all_to_all x1, starting transfers between devices, body(): kv = lax.all_to_all(kv, 'ctx', split_axis=0, concat_axis=0, tiled=True)  12.1 us
    ppermute x6, starting transfers between devices, passed_along(): return lax.ppermute(value, axis, pairs)  11.3 us
    unnamed x19, local copies, waits for them, and re-layouts  5.91 us
  transfers between devices with their start and end apart: 9, of which 5 were waited for; matrix products, arithmetic and copies ran while one was open for 3% of the time, Pallas kernels for 10%

profile of v4, /device:TPU:1, one launch (start us, length us, event | category | flops | bytes accessed | tf_op | source)
XLA Modules:
  0.0 282.3 jit_solution(6276541121536084286)
XLA Ops:
  0.6 1.8 multiply_bitcast_fusion
  4.0 1.8 copy_bitcast_fusion
  5.9 1.5 pad_maximum_fusion
  7.5 12.1 %all-to-all-start = ((bf16[32,264,128]{2,1,0:T(8,128)(2,1)}), bf16[32,264,128]{2,1,0:T(8,128)(2,1)}, u32[]{:S(2)}, u32[]{:S(2)}) async-start(bf16[32,264,128]{2,1,0:T(8,128)(2,1)} %pad_maximum_fusion), calls=%async_computation | async-start | bytes 4325376 | tf_op jit(solution)/shard_map/all_to_all | solution.py:181
  19.8 1.3 bitcast_bitcast_fusion
  21.1 48.6 %all-to-all-done = bf16[32,264,128]{2,1,0:T(8,128)(2,1)} async-done(((bf16[32,264,128]{2,1,0:T(8,128)(2,1)}), bf16[32,264,128]{2,1,0:T(8,128)(2,1)}, u32[]{:S(2)}, u32[]{:S(2)}) %all-to-all-start) | async-done | bytes 2162720 | tf_op jit(solution)/shard_map/all_to_all | solution.py:181
  69.7 7.2 %all-to-all-start.1 = ((bf16[32,2,64,128]{3,2,1,0:T(8,128)(2,1)}), bf16[32,2,64,128]{3,2,1,0:T(8,128)(2,1)S(1)}, u32[]{:S(2)}, u32[]{:S(2)}) async-start(bf16[32,2,64,128]{3,2,1,0:T(8,128)(2,1)} %bitcast_bitcast_fusion), calls=%async_computation.1 | async-start | bytes 2097152 | tf_op jit(solution)/shard_map/all_to_all | solution.py:195
  76.9 1.2 collective-permute-start.3
  78.1 1.3 bitcast_bitcast_fusion.1
  79.4 22.4 %all-to-all-done.1 = bf16[32,2,64,128]{3,2,1,0:T(8,128)(2,1)S(1)} async-done(((bf16[32,2,64,128]{3,2,1,0:T(8,128)(2,1)}), bf16[32,2,64,128]{3,2,1,0:T(8,128)(2,1)S(1)}, u32[]{:S(2)}, u32[]{:S(2)}) %all-to-all-start.1) | async-done | bytes 1048608 | tf_op jit(solution)/shard_map/all_to_all | solution.py:195
  101.8 8.4 %all-to-all-start.2 = ((bf16[32,2,64,128]{3,2,1,0:T(8,128)(2,1)}), bf16[32,2,64,128]{3,2,1,0:T(8,128)(2,1)}, u32[]{:S(2)}, u32[]{:S(2)}) async-start(bf16[32,2,64,128]{3,2,1,0:T(8,128)(2,1)} %bitcast_bitcast_fusion.1), calls=%async_computation.2 | async-start | bytes 2097152 | tf_op jit(solution)/shard_map/all_to_all | solution.py:195
  110.3 1.5 collective-permute-start
  111.7 1.7 collective-permute-start.2
  113.4 1.5 collective-permute-start.1
  115.8 0.7 abs_compare_fusion.1
  117.0 0.6 not_and_fusion
  118.2 0.9 collective-permute-start.5
  119.1 16.3 %all-to-all-done.2 = bf16[32,2,64,128]{3,2,1,0:T(8,128)(2,1)} async-done(((bf16[32,2,64,128]{3,2,1,0:T(8,128)(2,1)}), bf16[32,2,64,128]{3,2,1,0:T(8,128)(2,1)}, u32[]{:S(2)}, u32[]{:S(2)}) %all-to-all-start.2) | async-done | bytes 1048608 | tf_op jit(solution)/shard_map/all_to_all | solution.py:195
  135.4 4.6 %collective-permute-start.4 = (bf16[32,2,64,128]{3,2,1,0:T(8,128)(2,1)}, bf16[32,2,64,128]{3,2,1,0:T(8,128)(2,1)S(1)}, u32[]{:S(2)}, u32[]{:S(2)}) collective-permute-start(bf16[32,2,64,128]{3,2,1,0:T(8,128)(2,1)} %all-to-all-done.2), channel_id=1, source_target_pairs={{0,224},{32,0},{64,32},{96,64},{128,96},{160,128},{192,160},{224,1... | collective-permute-start | bytes 3145736 | tf_op jit(solution)/shard_map/ppermute | solution.py:21
  140.0 0.8 slice_convert_fusion
  140.9 2.0 copy.108.corr_ref
  142.9 26.8 %shard_map.103 = (bf16[32,64,128]{2,1,0:T(8,128)(2,1)S(1)}, f32[64,64,128]{2,1,0:T(8,128)S(1)}, f32[64,64,128]{2,1,0:T(8,128)S(1)}) custom-call(s32[640]{0:T(1024)S(1)} %min.22.slot_ref, s32[640]{0:T(1024)S(1)} %reshape.107.valid_ref, bf16[32,264,128]{2,1,0:T(8,128)(2,1)} %collective-permute-done.3.kv_ref, ...), custom_call_target="tpu_custom_call" | custom-call | tf_op jit(solution)/shard_map/pallas_call | solution.py:138
  169.7 1.3 copy-done.1
  171.0 29.2 %shard_map.104 = bf16[32,384,128]{2,1,0:T(8,128)(2,1)} custom-call(s32[640]{0:T(1024)S(1)} %min.22.slot_ref, s32[640]{0:T(1024)S(1)} %reshape.107.valid_ref, bf16[32,264,128]{2,1,0:T(8,128)(2,1)} %collective-permute-done.3.kv_ref, bf16[32,2,64,128]{3,2,1,0:T(8,128)(2,1)S(1)} %collective-permute-done.4.qd_ref, f32[4096,1]{1,0:T(8,128)S(1)} %copy-done, ...), custom_call_target="tpu_custom_call" | custom-call | tf_op jit(solution)/shard_map/pallas_call | solution.py:138
  200.3 73.9 %all_to_all.20 = bf16[32,384,128]{2,1,0:T(8,128)(2,1)S(1)} all-to-all(bf16[32,384,128]{2,1,0:T(8,128)(2,1)} %shard_map.104), channel_id=1, replica_groups=mesh['pipe'=8,'ctx'=32] {'ctx'}, dimensions={0} | all-to-all | bytes 6291456 | tf_op jit(solution)/shard_map/all_to_all | solution.py:203
  274.1 1.2 slice_bitcast_fusion
  275.4 1.6 copy.111
  277.0 1.3 copy.114
  278.3 0.7 copy.110
  279.0 1.3 copy.113
  280.3 0.7 copy.109
  280.9 1.3 copy.112
  (45 shorter events, 3.8 us)
Async XLA Ops:
  2.8 1.2 copy-start.3
  7.5 12.1 %copy-start.2 = (bf16[1,128,4096]{2,1,0:T(8,128)(2,1)S(1)}, bf16[1,128,4096]{2,1,0:T(8,128)(2,1)}, u32[]{:S(2)}) copy-start(bf16[1,128,4096]{2,1,0:T(8,128)(2,1)} %param.12) | copy-start | bytes 3145732
  7.5 12.1 %copy-start.4 = (bf16[1,128,4096]{2,1,0:T(8,128)(2,1)S(1)}, bf16[1,128,4096]{2,1,0:T(8,128)(2,1)}, u32[]{:S(2)}) copy-start(bf16[1,128,4096]{2,1,0:T(8,128)(2,1)} %param.8) | copy-start | bytes 3145732
  7.5 62.2 %all-to-all-start = ((bf16[32,264,128]{2,1,0:T(8,128)(2,1)}), bf16[32,264,128]{2,1,0:T(8,128)(2,1)}, u32[]{:S(2)}, u32[]{:S(2)}) async-start(bf16[32,264,128]{2,1,0:T(8,128)(2,1)} %pad_maximum_fusion), calls=%async_computation | async-start | bytes 4325376 | tf_op jit(solution)/shard_map/all_to_all | solution.py:181
  69.7 32.1 %all-to-all-start.1 = ((bf16[32,2,64,128]{3,2,1,0:T(8,128)(2,1)}), bf16[32,2,64,128]{3,2,1,0:T(8,128)(2,1)S(1)}, u32[]{:S(2)}, u32[]{:S(2)}) async-start(bf16[32,2,64,128]{3,2,1,0:T(8,128)(2,1)} %bitcast_bitcast_fusion), calls=%async_computation.1 | async-start | bytes 2097152 | tf_op jit(solution)/shard_map/all_to_all | solution.py:195
  76.9 63.1 %collective-permute-start.3 = (bf16[32,264,128]{2,1,0:T(8,128)(2,1)}, bf16[32,264,128]{2,1,0:T(8,128)(2,1)}, u32[]{:S(2)}, u32[]{:S(2)}) collective-permute-start(bf16[32,264,128]{2,1,0:T(8,128)(2,1)} %all-to-all-done), channel_id=1, source_target_pairs={{0,224},{32,0},{64,32},{96,64},{128,96},{160,128},{192,160},{224,1... | collective-permute-start | bytes 6488072 | tf_op jit(solution)/shard_map/ppermute | solution.py:21
  78.1 32.1 %copy-start.6 = (s32[1,2]{1,0:T(1,128)S(1)}, s32[1,2]{1,0:T(1,128)}, u32[]{:S(2)}) copy-start(s32[1,2]{1,0:T(1,128)} %param.14) | copy-start | bytes 28
  78.1 35.3 %copy-start.5 = (s32[1,1,64,3]{2,1,3,0:T(1,128)S(1)}, s32[1,1,64,3]{2,1,3,0:T(1,128)}, u32[]{:S(2)}) copy-start(s32[1,1,64,3]{2,1,3,0:T(1,128)} %param.13) | copy-start | bytes 2308
  101.8 33.6 %all-to-all-start.2 = ((bf16[32,2,64,128]{3,2,1,0:T(8,128)(2,1)}), bf16[32,2,64,128]{3,2,1,0:T(8,128)(2,1)}, u32[]{:S(2)}, u32[]{:S(2)}) async-start(bf16[32,2,64,128]{3,2,1,0:T(8,128)(2,1)} %bitcast_bitcast_fusion.1), calls=%async_computation.2 | async-start | bytes 2097152 | tf_op jit(solution)/shard_map/all_to_all | solution.py:195
  110.3 5.5 %collective-permute-start = (s32[2]{0:T(128)S(1)}, s32[2]{0:T(128)S(1)}, u32[]{:S(2)}, u32[]{:S(2)}) collective-permute-start(s32[2]{0:T(128)S(1)} %bitcast.61), channel_id=1, source_target_pairs={{0,224},{32,0},{64,32},{96,64},{128,96},{160,128},{192,160},{224,1... | collective-permute-start | bytes 32 | tf_op jit(solution)/shard_map/ppermute | solution.py:21
  111.7 3.3 %collective-permute-start.2 = (s32[]{:T(128)}, s32[]{:T(128)}, u32[]{:S(2)}, u32[]{:S(2)}) collective-permute-start(s32[]{:T(128)} %bitcast.1), channel_id=1, source_target_pairs={{0,224},{32,0},{64,32},{96,64},{128,96},{160,128},{192,160},{224,1... | collective-permute-start | bytes 20 | tf_op jit(solution)/shard_map/ppermute | solution.py:21
  113.4 3.4 %collective-permute-start.1 = (s32[64,3]{0,1:T(4,128)S(1)}, s32[64,3]{0,1:T(4,128)S(1)}, u32[]{:S(2)}, u32[]{:S(2)}) collective-permute-start(s32[64,3]{0,1:T(4,128)S(1)} %bitcast.60), channel_id=1, source_target_pairs={{0,224},{32,0},{64,32},{96,64},{128,96},{160,128},{192,160},{224,1... | collective-permute-start | bytes 2312 | tf_op jit(solution)/shard_map/ppermute | solution.py:21
  118.2 24.7 %collective-permute-start.5 = (bf16[32,2,64,128]{3,2,1,0:T(8,128)(2,1)S(1)}, bf16[32,2,64,128]{3,2,1,0:T(8,128)(2,1)S(1)}, u32[]{:S(2)}, u32[]{:S(2)}) collective-permute-start(bf16[32,2,64,128]{3,2,1,0:T(8,128)(2,1)S(1)} %all-to-all-done.1), channel_id=1, source_target_pairs={{0,224},{32,0},{64,32},{96,64},{128,96},{160,128},{192,160},{224,1... | collective-permute-start | bytes 3145736 | tf_op jit(solution)/shard_map/ppermute | solution.py:21
  135.4 35.6 %collective-permute-start.4 = (bf16[32,2,64,128]{3,2,1,0:T(8,128)(2,1)}, bf16[32,2,64,128]{3,2,1,0:T(8,128)(2,1)S(1)}, u32[]{:S(2)}, u32[]{:S(2)}) collective-permute-start(bf16[32,2,64,128]{3,2,1,0:T(8,128)(2,1)} %all-to-all-done.2), channel_id=1, source_target_pairs={{0,224},{32,0},{64,32},{96,64},{128,96},{160,128},{192,160},{224,1... | collective-permute-start | bytes 3145736 | tf_op jit(solution)/shard_map/ppermute | solution.py:21
  142.9 28.2 %copy-start = (f32[4096,1]{1,0:T(8,128)S(1)}, f32[4096,1]{1,0:T(8,128)}, u32[]{:S(2)}) copy-start(f32[4096,1]{1,0:T(8,128)} %copy.108.corr_ref) | copy-start | bytes 49156
  169.7 1.3 copy-start.1

commit v5 on v4

--- a/solution.py
+++ b/solution.py
@@ -168,6 +168,19 @@
     length = local * chunks
     block_count = length // BLK
     per_chunk = local // BLK
+    ints = jnp.concatenate(
+        [random_blocks.reshape(-1), global_blocks.reshape(-1), radius.reshape(-1)]
+    )
+    ints = passed_along(ints, "pipe", -1)
+    random_list = ints[:block_count * NR].reshape(block_count, NR)
+    global_list = ints[block_count * NR:-1]
+    head_radius = ints[-1]
+    shipped = []
+    for parity in range(per_chunk):
+        rows = slice(parity * BLK, (parity + 1) * BLK)
+        qd = to_chunks(jnp.stack([queries[0, rows], out_grad[0, rows]], axis=0), chunks)
+        qd, _ = lax.optimization_barrier((qd, ints))
+        shipped.append(passed_along(qd, "pipe", -1))
     correction = jnp.sum(
         (attn_out[0].astype(jnp.float32) * out_grad[0].astype(jnp.float32)).reshape(
             local, heads, HD
@@ -180,21 +193,16 @@
     kv = jnp.concatenate([kv, pieces], axis=1)
     kv = lax.all_to_all(kv, "ctx", split_axis=0, concat_axis=0, tiled=True)
     after = kv
+    kv, _ = lax.optimization_barrier((kv, shipped[-1]))
     kv = passed_along(kv, "pipe", -1)
     got = kv[:, 2 * local:2 * local + 3, :].astype(jnp.float32)
     correction = ((got[:, 0] + got[:, 1]) + got[:, 2]).reshape(length, 1)
-    random_list = passed_along(random_blocks[0, 0], "pipe", -1)
-    global_list = passed_along(global_blocks[0], "pipe", -1)
-    head_radius = passed_along(radius[0, 0], "pipe", -1)
     slot_index, slot_valid = slot_table(random_list, global_list, head_radius, block_count)
     previous = None
     for parity in range(per_chunk):
-        rows = slice(parity * BLK, (parity + 1) * BLK)
-        qd = to_chunks(jnp.stack([queries[0, rows], out_grad[0, rows]], axis=0), chunks)
-        qd, _ = lax.optimization_barrier((qd, after))
+        qd, _ = lax.optimization_barrier((shipped[parity], after))
         qd = lax.all_to_all(qd, "ctx", split_axis=0, concat_axis=0, tiled=True)
         after = qd
-        qd = passed_along(qd, "pipe", -1)
         result = head_part(
             kv, qd, correction, slot_index, slot_valid, previous, block_count, chunks, local,
             parity,

time: 287 us -> 270 us (0.941)
  waiting for transfers between devices: 87.8 us -> 65.5 us
  local copies, waits for them, and re-layouts: 13.1 us -> 20.8 us
  starting transfers between devices: 39 us -> 33.9 us
  blocking collectives: 73.9 us -> 78.8 us
    all_to_all x1, waiting for transfers between devices: 48.6 us -> 30.7 us  [body(): kv = lax.all_to_all(kv, 'ctx', split_axis=0, concat_axis=0, tiled=True)]
    all_to_all x2, waiting for transfers between devices: 38.7 us -> 22.5 us  [body(): qd = lax.all_to_all(qd, 'ctx', split_axis=0, concat_axis=0, tiled=True)]
    ppermute x6 -> x4, waiting for transfers between devices: 0.46 us -> 12.3 us  [passed_along(): return lax.ppermute(value, axis, pairs)]
    unnamed x19 -> x31, local copies, waits for them, and re-layouts: 5.91 us -> 12.1 us
    ppermute x6 -> x4, starting transfers between devices: 11.3 us -> 6.27 us  [passed_along(): return lax.ppermute(value, axis, pairs)]
    all_to_all x1, blocking collectives: 73.9 us -> 78.8 us  [body(): lax.all_to_all(result[0], 'ctx', split_axis=0, concat_axis=0, tiled=True)]
  transfers between devices with their start and end apart: 9 -> 7, of which waited for: 5 -> 4; matrix products, arithmetic and copies ran while one was open for 3% -> 3% of each run, Pallas kernels for 10% -> 10%
where the time goes in v5:
time: 270 us; the launch traced here: 266 us
  blocking collectives  78.8 us (29%)
  waiting for transfers between devices  65.5 us (24%)
  Pallas kernels  56 us (21%)
  starting transfers between devices  33.9 us (13%)
  local copies, waits for them, and re-layouts  20.8 us (8%)
  other arithmetic  9.37 us (3%)
    all_to_all x1, blocking collectives, body(): lax.all_to_all(result[0], 'ctx', split_axis=0, concat_axis=0, tiled=True)  78.8 us
    pallas_call x2, Pallas kernels, head_part(): pl.pallas_call(kernel, out_shape=out_shape, in_specs=in_specs, out_specs=...  56 us
    all_to_all x1, waiting for transfers between devices, body(): kv = lax.all_to_all(kv, 'ctx', split_axis=0, concat_axis=0, tiled=True)  30.7 us
    all_to_all x2, waiting for transfers between devices, body(): qd = lax.all_to_all(qd, 'ctx', split_axis=0, concat_axis=0, tiled=True)  22.5 us
    all_to_all x2, starting transfers between devices, body(): qd = lax.all_to_all(qd, 'ctx', split_axis=0, concat_axis=0, tiled=True)  15.5 us
    ppermute x4, waiting for transfers between devices, passed_along(): return lax.ppermute(value, axis, pairs)  12.3 us
    all_to_all x1, starting transfers between devices, body(): kv = lax.all_to_all(kv, 'ctx', split_axis=0, concat_axis=0, tiled=True)  12.1 us
    unnamed x31, local copies, waits for them, and re-layouts  12.1 us
  transfers between devices with their start and end apart: 7, of which 4 were waited for; matrix products, arithmetic and copies ran while one was open for 3% of the time, Pallas kernels for 10%

profile of v5, /device:TPU:1, one launch (start us, length us, event | category | flops | bytes accessed | tf_op | source)
XLA Modules:
  0.0 266.1 jit_solution(3231067482086095373)
XLA Ops:
  0.6 1.8 multiply_bitcast_fusion
  4.0 1.8 copy_bitcast_fusion
  5.9 1.5 pad_maximum_fusion
  7.5 12.1 %all-to-all-start = ((bf16[32,264,128]{2,1,0:T(8,128)(2,1)}), bf16[32,264,128]{2,1,0:T(8,128)(2,1)}, u32[]{:S(2)}, u32[]{:S(2)}) async-start(bf16[32,264,128]{2,1,0:T(8,128)(2,1)} %pad_maximum_fusion), calls=%async_computation | async-start | bytes 4325376 | tf_op jit(solution)/shard_map/all_to_all | solution.py:194
  20.6 1.0 collective-permute-start
  22.3 2.0 collective-permute-done
  24.3 0.8 collective-permute-start.3
  25.4 3.3 %collective-permute-start.1 = (bf16[32,2,64,128]{3,2,1,0:T(8,128)(2,1)S(1)}, bf16[32,2,64,128]{3,2,1,0:T(8,128)(2,1)}, u32[]{:S(2)}, u32[]{:S(2)}) collective-permute-start(bf16[32,2,64,128]{3,2,1,0:T(8,128)(2,1)S(1)} %bitcast.61), channel_id=1, source_target_pairs={{0,224},{32,0},{64,32},{96,64},{128,96},{160,128},{192,160},{224,1... | collective-permute-start | bytes 3145736 | tf_op jit(solution)/shard_map/ppermute | solution.py:21
  28.7 10.2 %collective-permute-done.3 = bf16[32,2,64,128]{3,2,1,0:T(8,128)(2,1)} collective-permute-done((bf16[32,2,64,128]{3,2,1,0:T(8,128)(2,1)S(1)}, bf16[32,2,64,128]{3,2,1,0:T(8,128)(2,1)}, u32[]{:S(2)}, u32[]{:S(2)}) %collective-permute-start.3) | collective-permute-done | bytes 1048608 | tf_op jit(solution)/shard_map/ppermute | solution.py:21
  38.9 30.7 %all-to-all-done = bf16[32,264,128]{2,1,0:T(8,128)(2,1)} async-done(((bf16[32,264,128]{2,1,0:T(8,128)(2,1)}), bf16[32,264,128]{2,1,0:T(8,128)(2,1)}, u32[]{:S(2)}, u32[]{:S(2)}) %all-to-all-start) | async-done | bytes 2162720 | tf_op jit(solution)/shard_map/all_to_all | solution.py:194
  69.7 7.2 %all-to-all-start.1 = ((bf16[32,2,64,128]{3,2,1,0:T(8,128)(2,1)}), bf16[32,2,64,128]{3,2,1,0:T(8,128)(2,1)S(1)}, u32[]{:S(2)}, u32[]{:S(2)}) async-start(bf16[32,2,64,128]{3,2,1,0:T(8,128)(2,1)} %collective-permute-done.3), calls=%async_computation.1 | async-start | bytes 2097152 | tf_op jit(solution)/shard_map/all_to_all | solution.py:204
  76.9 1.2 collective-permute-start.2
  79.3 22.5 %all-to-all-done.1.qd_ref = bf16[32,2,64,128]{3,2,1,0:T(8,128)(2,1)S(1)} async-done(((bf16[32,2,64,128]{3,2,1,0:T(8,128)(2,1)}), bf16[32,2,64,128]{3,2,1,0:T(8,128)(2,1)S(1)}, u32[]{:S(2)}, u32[]{:S(2)}) %all-to-all-start.1) | async-done | bytes 1048608 | tf_op jit(solution)/shard_map/all_to_all | solution.py:204
  101.8 8.3 %all-to-all-start.2 = ((bf16[32,2,64,128]{3,2,1,0:T(8,128)(2,1)}), bf16[32,2,64,128]{3,2,1,0:T(8,128)(2,1)S(1)}, u32[]{:S(2)}, u32[]{:S(2)}) async-start(bf16[32,2,64,128]{3,2,1,0:T(8,128)(2,1)} %collective-permute-done.1), calls=%async_computation.2 | async-start | bytes 2097152 | tf_op jit(solution)/shard_map/all_to_all | solution.py:204
  110.8 0.7 abs_compare_fusion.1
  111.6 0.7 not_and_fusion
  112.8 0.8 slice_convert_fusion
  113.7 2.0 copy.97.corr_ref
  115.7 1.2 copy-done.2
  116.9 26.8 %shard_map.103 = (bf16[32,64,128]{2,1,0:T(8,128)(2,1)S(1)}, f32[64,64,128]{2,1,0:T(8,128)S(1)}, f32[64,64,128]{2,1,0:T(8,128)S(1)}) custom-call(s32[640]{0:T(1024)S(1)} %min.22.slot_ref, s32[640]{0:T(1024)S(1)} %reshape.135.valid_ref, bf16[32,264,128]{2,1,0:T(8,128)(2,1)} %collective-permute-done.2.kv_ref, bf16[32,2,64,128]{3,2,1,0:T(8,128)(2,1)S(1)} %copy-done.2, ...), custom_call_target="tpu_custom_call" | custom-call | tf_op jit(solution)/shard_map/pallas_call | solution.py:138
  143.8 1.4 copy-done.3
  145.2 1.4 copy-done.5
  146.5 0.8 copy-done.6
  147.3 1.6 copy-done.4
  148.9 1.0 copy-done.7
  150.0 29.2 %shard_map.104 = bf16[32,384,128]{2,1,0:T(8,128)(2,1)} custom-call(s32[640]{0:T(1024)S(1)} %min.22.slot_ref, s32[640]{0:T(1024)S(1)} %reshape.135.valid_ref, bf16[32,264,128]{2,1,0:T(8,128)(2,1)} %collective-permute-done.2.kv_ref, bf16[32,2,64,128]{3,2,1,0:T(8,128)(2,1)S(1)} %all-to-all-done.2.qd_ref, f32[4096,1]{1,0:T(8,128)S(1)} %copy-done, ...), custom_call_target="tpu_custom_call" | custom-call | tf_op jit(solution)/shard_map/pallas_call | solution.py:138
  179.1 78.8 %all_to_all.20 = bf16[32,384,128]{2,1,0:T(8,128)(2,1)S(1)} all-to-all(bf16[32,384,128]{2,1,0:T(8,128)(2,1)} %shard_map.104), channel_id=1, replica_groups=mesh['pipe'=8,'ctx'=32] {'ctx'}, dimensions={0} | all-to-all | bytes 6291456 | tf_op jit(solution)/shard_map/all_to_all | solution.py:211
  257.9 1.2 slice_bitcast_fusion
  259.2 1.6 copy.100
  260.8 1.3 copy.103
  262.8 1.3 copy.102
  264.8 1.3 copy.101
  (61 shorter events, 6.6 us)
Async XLA Ops:
  2.8 1.2 copy-start.10
  7.4 12.9 %copy-start.11 = (s32[1,1,64,3]{2,1,3,0:T(1,128)S(1)}, s32[1,1,64,3]{2,1,3,0:T(1,128)}, u32[]{:S(2)}) copy-start(s32[1,1,64,3]{2,1,3,0:T(1,128)} %param.13) | copy-start | bytes 2308
  7.5 13.1 %copy-start.12 = (s32[1,2]{1,0:T(1,128)S(1)}, s32[1,2]{1,0:T(1,128)}, u32[]{:S(2)}) copy-start(s32[1,2]{1,0:T(1,128)} %param.14) | copy-start | bytes 28
  7.5 14.1 %copy-start.8 = (bf16[1,128,4096]{2,1,0:T(8,128)(2,1)S(1)}, bf16[1,128,4096]{2,1,0:T(8,128)(2,1)}, u32[]{:S(2)}) copy-start(bf16[1,128,4096]{2,1,0:T(8,128)(2,1)} %param.12) | copy-start | bytes 3145732
  7.5 62.2 %all-to-all-start = ((bf16[32,264,128]{2,1,0:T(8,128)(2,1)}), bf16[32,264,128]{2,1,0:T(8,128)(2,1)}, u32[]{:S(2)}, u32[]{:S(2)}) async-start(bf16[32,264,128]{2,1,0:T(8,128)(2,1)} %pad_maximum_fusion), calls=%async_computation | async-start | bytes 4325376 | tf_op jit(solution)/shard_map/all_to_all | solution.py:194
  19.6 2.1 copy-start.9
  20.6 3.7 %collective-permute-start = (s32[195]{0:T(256)S(1)}, s32[195]{0:T(256)S(1)}, u32[]{:S(2)}, u32[]{:S(2)}) collective-permute-start(s32[195]{0:T(256)S(1)} %pad_add_fusion), channel_id=1, source_target_pairs={{0,224},{32,0},{64,32},{96,64},{128,96},{160,128},{192,160},{224,1... | collective-permute-start | bytes 2348 | tf_op jit(solution)/shard_map/ppermute | solution.py:21
  24.3 14.6 %collective-permute-start.3 = (bf16[32,2,64,128]{3,2,1,0:T(8,128)(2,1)S(1)}, bf16[32,2,64,128]{3,2,1,0:T(8,128)(2,1)}, u32[]{:S(2)}, u32[]{:S(2)}) collective-permute-start(bf16[32,2,64,128]{3,2,1,0:T(8,128)(2,1)S(1)} %bitcast.62), channel_id=1, source_target_pairs={{0,224},{32,0},{64,32},{96,64},{128,96},{160,128},{192,160},{224,1... | collective-permute-start | bytes 3145736 | tf_op jit(solution)/shard_map/ppermute | solution.py:21
  25.4 51.5 %collective-permute-start.1 = (bf16[32,2,64,128]{3,2,1,0:T(8,128)(2,1)S(1)}, bf16[32,2,64,128]{3,2,1,0:T(8,128)(2,1)}, u32[]{:S(2)}, u32[]{:S(2)}) collective-permute-start(bf16[32,2,64,128]{3,2,1,0:T(8,128)(2,1)S(1)} %bitcast.61), channel_id=1, source_target_pairs={{0,224},{32,0},{64,32},{96,64},{128,96},{160,128},{192,160},{224,1... | collective-permute-start | bytes 3145736 | tf_op jit(solution)/shard_map/ppermute | solution.py:21
  69.7 32.1 %all-to-all-start.1 = ((bf16[32,2,64,128]{3,2,1,0:T(8,128)(2,1)}), bf16[32,2,64,128]{3,2,1,0:T(8,128)(2,1)S(1)}, u32[]{:S(2)}, u32[]{:S(2)}) async-start(bf16[32,2,64,128]{3,2,1,0:T(8,128)(2,1)} %collective-permute-done.3), calls=%async_computation.1 | async-start | bytes 2097152 | tf_op jit(solution)/shard_map/all_to_all | solution.py:204
  76.9 35.9 %collective-permute-start.2 = (bf16[32,264,128]{2,1,0:T(8,128)(2,1)}, bf16[32,264,128]{2,1,0:T(8,128)(2,1)}, u32[]{:S(2)}, u32[]{:S(2)}) collective-permute-start(bf16[32,264,128]{2,1,0:T(8,128)(2,1)} %all-to-all-done), channel_id=1, source_target_pairs={{0,224},{32,0},{64,32},{96,64},{128,96},{160,128},{192,160},{224,1... | collective-permute-start | bytes 6488072 | tf_op jit(solution)/shard_map/ppermute | solution.py:21
  101.8 11.9 %copy-start.1 = (bf16[32,2,64,128]{3,2,1,0:T(8,128)(2,1)}, bf16[32,2,64,128]{3,2,1,0:T(8,128)(2,1)S(1)}, u32[]{:S(2)}) copy-start(bf16[32,2,64,128]{3,2,1,0:T(8,128)(2,1)S(1)} %all-to-all-done.1.qd_ref) | copy-start | bytes 3145732
  101.8 45.5 %all-to-all-start.2 = ((bf16[32,2,64,128]{3,2,1,0:T(8,128)(2,1)}), bf16[32,2,64,128]{3,2,1,0:T(8,128)(2,1)S(1)}, u32[]{:S(2)}, u32[]{:S(2)}) async-start(bf16[32,2,64,128]{3,2,1,0:T(8,128)(2,1)} %collective-permute-done.1), calls=%async_computation.2 | async-start | bytes 2097152 | tf_op jit(solution)/shard_map/all_to_all | solution.py:204
  115.7 1.2 copy-start.2
  116.9 30.4 %copy-start = (f32[4096,1]{1,0:T(8,128)S(1)}, f32[4096,1]{1,0:T(8,128)}, u32[]{:S(2)}) copy-start(f32[4096,1]{1,0:T(8,128)} %copy.97.corr_ref) | copy-start | bytes 49156
  143.8 1.4 copy-start.3
  145.2 1.4 copy-start.5
  146.5 0.8 copy-start.6
  147.3 1.6 copy-start.4
  148.9 1.0 copy-start.7

commit v6 on v5

--- a/solution.py
+++ b/solution.py
@@ -43,11 +43,10 @@
 def head_kernel(slot_ref, valid_ref, kv_ref, qd_ref, corr_ref, *rest, block_count,
                 chunk_rows, parity, final):
     if final:
-        (dq_prev, dk_prev, dv_prev, out_ref, kt_ref, vt_ref, dk_acc, dv_acc) = rest
-        out_ref[:, 0:parity * BLK, :] = dq_prev[...]
-        dq_ref = out_ref.at[:, parity * BLK:(parity + 1) * BLK, :]
-        dk_ref = out_ref.at[:, chunk_rows:2 * chunk_rows, :]
-        dv_ref = out_ref.at[:, 2 * chunk_rows:3 * chunk_rows, :]
+        (dk_prev, dv_prev, out_ref, kt_ref, vt_ref, dk_acc, dv_acc) = rest
+        dq_ref = out_ref.at[:, 0:BLK, :]
+        dk_ref = out_ref.at[:, BLK:BLK + chunk_rows, :]
+        dv_ref = out_ref.at[:, BLK + chunk_rows:BLK + 2 * chunk_rows, :]
     else:
         (dq_ref, dk_acc, dv_acc, kt_ref, vt_ref) = rest
     score_scale = HD ** (-0.5)
@@ -127,8 +126,8 @@
     operands = [slot_index.reshape(-1), slot_valid.reshape(-1), kv, qd, corr]
     scratch = [pltpu.VMEM((KB * BLK, HD), jnp.bfloat16), pltpu.VMEM((KB * BLK, HD), jnp.bfloat16)]
     if final:
-        operands += list(previous)
-        out_shape = (jax.ShapeDtypeStruct((chunks, 3 * chunk_rows, HD), jnp.bfloat16),)
+        operands += list(previous[1:])
+        out_shape = (jax.ShapeDtypeStruct((chunks, BLK + 2 * chunk_rows, HD), jnp.bfloat16),)
         scratch += [pltpu.VMEM((block_count, BLK, HD), jnp.float32)] * 2
     else:
         out_shape = (dq_shape, acc_shape, acc_shape)
@@ -143,6 +142,26 @@
         scratch_shapes=scratch,
         compiler_params=pltpu.CompilerParams(vmem_limit_bytes=48 * 1024 * 1024),
     )(*operands)
+
+
+def assemble_kernel(first_ref, back_ref, dq_ref, dk_ref, dv_ref, *, local):
+    for h in range(first_ref.shape[0]):
+        cols = slice(h * HD, (h + 1) * HD)
+        dq_ref[0, 0:BLK, cols] = first_ref[h]
+        dq_ref[0, BLK:2 * BLK, cols] = back_ref[h, 0:BLK, :]
+        dk_ref[0, :, cols] = back_ref[h, BLK:BLK + local, :]
+        dv_ref[0, :, cols] = back_ref[h, BLK + local:BLK + 2 * local, :]
+
+
+def assemble(first, back, local):
+    vmem = pltpu.MemorySpace.VMEM
+    shape = jax.ShapeDtypeStruct((1, local, first.shape[0] * HD), jnp.bfloat16)
+    return pl.pallas_call(
+        functools.partial(assemble_kernel, local=local),
+        out_shape=(shape, shape, shape),
+        in_specs=[pl.BlockSpec(memory_space=vmem)] * 2,
+        out_specs=tuple(pl.BlockSpec(memory_space=vmem) for _ in range(3)),
+    )(first, back)
 
 
 def to_chunks(rows, chunks):
@@ -208,9 +227,10 @@
             parity,
         )
         previous = result
+        if parity == 0:
+            dq_first = lax.all_to_all(result[0], "ctx", split_axis=0, concat_axis=0, tiled=True)
     back = lax.all_to_all(result[0], "ctx", split_axis=0, concat_axis=0, tiled=True)
-    outs = [back[:, k * local:(k + 1) * local] for k in range(3)]
-    return tuple(o.transpose(1, 0, 2).reshape(1, local, chunks * HD) for o in outs)
+    return assemble(dq_first, back, local)
 
 
 def solution(mesh):

time: 270 us -> 263 us (0.974)
  blocking collectives: 78.8 us -> 67.1 us
  starting transfers between devices: 33.9 us -> 42.9 us
  local copies, waits for them, and re-layouts: 20.8 us -> 13.7 us
  Pallas kernels: 56 us -> 60.5 us
    all_to_all x1, blocking collectives: 78.8 us -> 67.1 us  [body(): lax.all_to_all(result[0], 'ctx', split_axis=0, concat_axis=0, tiled=True)]
    all_to_all x0 -> x1, starting transfers between devices: none -> 9.15 us  [body(): lax.all_to_all(result[0], 'ctx', split_axis=0, concat_axis=0, tiled=True)]
    pallas_call x0 -> x1, Pallas kernels: none -> 4.43 us  [assemble(): pl.pallas_call(functools.partial(assemble_kernel, local=local), out_shape...]
    transpose x4 -> x0, local copies, waits for them, and re-layouts: 4.16 us -> none  [body(): o.transpose(1, 0, 2).reshape(1, local, chunks * HD)]
    unnamed x31 -> x30, local copies, waits for them, and re-layouts: 12.1 us -> 8.2 us
  transfers between devices with their start and end apart: 7 -> 8, of which waited for: 4 -> 4; matrix products, arithmetic and copies ran while one was open for 3% -> 3% of each run, Pallas kernels for 10% -> 22%
where the time goes in v6:
time: 263 us; the launch traced here: 258 us
  blocking collectives  67.1 us (26%)
  waiting for transfers between devices  63.8 us (24%)
  Pallas kernels  60.5 us (23%)
  starting transfers between devices  42.9 us (16%)
  local copies, waits for them, and re-layouts  13.7 us (5%)
  other arithmetic  8.54 us (3%)
    all_to_all x1, blocking collectives, body(): lax.all_to_all(result[0], 'ctx', split_axis=0, concat_axis=0, tiled=True)  67.1 us
    pallas_call x2, Pallas kernels, head_part(): pl.pallas_call(kernel, out_shape=out_shape, in_specs=in_specs, out_specs=...  56.1 us
    all_to_all x1, waiting for transfers between devices, body(): kv = lax.all_to_all(kv, 'ctx', split_axis=0, concat_axis=0, tiled=True)  29.9 us
    all_to_all x2, waiting for transfers between devices, body(): qd = lax.all_to_all(qd, 'ctx', split_axis=0, concat_axis=0, tiled=True)  22.5 us
    all_to_all x2, starting transfers between devices, body(): qd = lax.all_to_all(qd, 'ctx', split_axis=0, concat_axis=0, tiled=True)  15.7 us
    all_to_all x1, starting transfers between devices, body(): kv = lax.all_to_all(kv, 'ctx', split_axis=0, concat_axis=0, tiled=True)  12 us
    ppermute x4, waiting for transfers between devices, passed_along(): return lax.ppermute(value, axis, pairs)  11.3 us
    all_to_all x1, starting transfers between devices, body(): lax.all_to_all(result[0], 'ctx', split_axis=0, concat_axis=0, tiled=True)  9.15 us
  transfers between devices with their start and end apart: 8, of which 4 were waited for; matrix products, arithmetic and copies ran while one was open for 3% of the time, Pallas kernels for 22%

profile of v6, /device:TPU:1, one launch (start us, length us, event | category | flops | bytes accessed | tf_op | source)
XLA Modules:
  0.0 258.1 jit_solution(12645668173781731470)
XLA Ops:
  0.6 1.8 multiply_bitcast_fusion
  2.8 0.6 reduce_sum.9
  4.0 1.8 copy_bitcast_fusion
  5.9 1.5 pad_maximum_fusion
  7.5 12.0 %all-to-all-start = ((bf16[32,264,128]{2,1,0:T(8,128)(2,1)}), bf16[32,264,128]{2,1,0:T(8,128)(2,1)S(1)}, u32[]{:S(2)}, u32[]{:S(2)}) async-start(bf16[32,264,128]{2,1,0:T(8,128)(2,1)} %pad_maximum_fusion), calls=%async_computation | async-start | bytes 4325376 | tf_op jit(solution)/shard_map/all_to_all | solution.py:213
  20.4 1.0 collective-permute-start
  22.1 2.0 collective-permute-done
  24.1 0.7 collective-permute-start.3
  24.9 1.3 copy.88
  26.1 3.2 %collective-permute-start.1 = (bf16[32,2,64,128]{3,2,1,0:T(8,128)(2,1)}, bf16[32,2,64,128]{3,2,1,0:T(8,128)(2,1)}, u32[]{:S(2)}, u32[]{:S(2)}) collective-permute-start(bf16[32,2,64,128]{3,2,1,0:T(8,128)(2,1)} %bitcast.44), channel_id=1, source_target_pairs={{0,224},{32,0},{64,32},{96,64},{128,96},{160,128},{192,160},{224,1... | collective-permute-start | bytes 3145736 | tf_op jit(solution)/shard_map/ppermute | solution.py:21
  29.4 9.3 %collective-permute-done.3 = bf16[32,2,64,128]{3,2,1,0:T(8,128)(2,1)S(1)} collective-permute-done((bf16[32,2,64,128]{3,2,1,0:T(8,128)(2,1)S(1)}, bf16[32,2,64,128]{3,2,1,0:T(8,128)(2,1)S(1)}, u32[]{:S(2)}, u32[]{:S(2)}) %collective-permute-start.3) | collective-permute-done | bytes 1048608 | tf_op jit(solution)/shard_map/ppermute | solution.py:21
  38.7 1.0 copy-done.10
  39.6 29.9 %all-to-all-done = bf16[32,264,128]{2,1,0:T(8,128)(2,1)S(1)} async-done(((bf16[32,264,128]{2,1,0:T(8,128)(2,1)}), bf16[32,264,128]{2,1,0:T(8,128)(2,1)S(1)}, u32[]{:S(2)}, u32[]{:S(2)}) %all-to-all-start) | async-done | bytes 2162720 | tf_op jit(solution)/shard_map/all_to_all | solution.py:213
  69.6 7.2 %all-to-all-start.1 = ((bf16[32,2,64,128]{3,2,1,0:T(8,128)(2,1)}), bf16[32,2,64,128]{3,2,1,0:T(8,128)(2,1)S(1)}, u32[]{:S(2)}, u32[]{:S(2)}) async-start(bf16[32,2,64,128]{3,2,1,0:T(8,128)(2,1)} %copy-done.10), calls=%async_computation.1 | async-start | bytes 2097152 | tf_op jit(solution)/shard_map/all_to_all | solution.py:223
  76.8 1.2 collective-permute-start.2
  78.4 0.6 slice.47
  79.2 22.5 %all-to-all-done.1.qd_ref = bf16[32,2,64,128]{3,2,1,0:T(8,128)(2,1)S(1)} async-done(((bf16[32,2,64,128]{3,2,1,0:T(8,128)(2,1)}), bf16[32,2,64,128]{3,2,1,0:T(8,128)(2,1)S(1)}, u32[]{:S(2)}, u32[]{:S(2)}) %all-to-all-start.1) | async-done | bytes 1048608 | tf_op jit(solution)/shard_map/all_to_all | solution.py:223
  101.7 8.4 %all-to-all-start.3 = ((bf16[32,2,64,128]{3,2,1,0:T(8,128)(2,1)}), bf16[32,2,64,128]{3,2,1,0:T(8,128)(2,1)}, u32[]{:S(2)}, u32[]{:S(2)}) async-start(bf16[32,2,64,128]{3,2,1,0:T(8,128)(2,1)} %collective-permute-done.1), calls=%async_computation.3 | async-start | bytes 2097152 | tf_op jit(solution)/shard_map/all_to_all | solution.py:223
  110.1 0.7 abs_compare_fusion.2
  111.1 0.7 abs_compare_fusion.1
  111.9 0.7 not_and_fusion
  112.9 1.3 copy-done.5
  114.2 2.0 copy.72.corr_ref
  116.2 26.8 %shard_map.103 = (bf16[32,64,128]{2,1,0:T(8,128)(2,1)S(1)}, f32[64,64,128]{2,1,0:T(8,128)S(1)}, f32[64,64,128]{2,1,0:T(8,128)S(1)}) custom-call(s32[640]{0:T(1024)S(1)} %min.22.slot_ref, s32[640]{0:T(1024)S(1)} %reshape.123.valid_ref, bf16[32,264,128]{2,1,0:T(8,128)(2,1)} %copy-done.5, bf16[32,2,64,128]{3,2,1,0:T(8,128)(2,1)S(1)} %all-to-all-done.1.qd_ref, ...), custom_call_target="tpu_custom_call" | custom-call | tf_op jit(solution)/shard_map/pallas_call | solution.py:137
  143.0 1.4 copy-done.1
  144.4 1.3 copy-done.3
  145.8 0.8 copy-done.4
  146.6 9.1 %all-to-all-start.2 = ((bf16[32,64,128]{2,1,0:T(8,128)(2,1)}), bf16[32,64,128]{2,1,0:T(8,128)(2,1)S(1)}, u32[]{:S(2)}, u32[]{:S(2)}) async-start(bf16[32,64,128]{2,1,0:T(8,128)(2,1)} %copy-done.4), calls=%async_computation.2 | async-start | bytes 1048576 | tf_op jit(solution)/shard_map/all_to_all | solution.py:231
  155.7 1.6 copy-done.2
  157.3 29.3 %shard_map.104 = bf16[32,320,128]{2,1,0:T(8,128)(2,1)} custom-call(s32[640]{0:T(1024)S(1)} %min.22.slot_ref, s32[640]{0:T(1024)S(1)} %reshape.123.valid_ref, bf16[32,264,128]{2,1,0:T(8,128)(2,1)} %copy-done.5, bf16[32,2,64,128]{3,2,1,0:T(8,128)(2,1)} %all-to-all-done.3.qd_ref, f32[4096,1]{1,0:T(8,128)S(1)} %copy-done, f32[64,64,128]{2,1,0:T(8,128)S(1)} %copy-done.2, ...), custom_call_target="tpu_custom_call" | custom-call | tf_op jit(solution)/shard_map/pallas_call | solution.py:137
  186.6 67.1 %all_to_all.25.back_ref = bf16[32,320,128]{2,1,0:T(8,128)(2,1)} all-to-all(bf16[32,320,128]{2,1,0:T(8,128)(2,1)} %shard_map.104), channel_id=1, replica_groups=mesh['pipe'=8,'ctx'=32] {'ctx'}, dimensions={0} | all-to-all | bytes 5242880 | tf_op jit(solution)/shard_map/all_to_all | solution.py:232
  253.7 4.4 %shard_map.105 = (bf16[1,128,4096]{2,1,0:T(8,128)(2,1)}, bf16[1,128,4096]{2,1,0:T(8,128)(2,1)}, bf16[1,128,4096]{2,1,0:T(8,128)(2,1)}) custom-call(bf16[32,64,128]{2,1,0:T(8,128)(2,1)} %copy-done.8, bf16[32,320,128]{2,1,0:T(8,128)(2,1)} %all_to_all.25.back_ref), custom_call_target="tpu_custom_call" | custom-call | tf_op jit(solution)/shard_map/pallas_call | solution.py:159
  (59 shorter events, 3.3 us)
Async XLA Ops:
  2.8 1.2 copy-start.11
  7.5 12.6 %copy-start.12 = (s32[1,1,64,3]{2,1,3,0:T(1,128)S(1)}, s32[1,1,64,3]{2,1,3,0:T(1,128)}, u32[]{:S(2)}) copy-start(s32[1,1,64,3]{2,1,3,0:T(1,128)} %param.13) | copy-start | bytes 2308
  7.5 12.9 %copy-start.13 = (s32[1,2]{1,0:T(1,128)S(1)}, s32[1,2]{1,0:T(1,128)}, u32[]{:S(2)}) copy-start(s32[1,2]{1,0:T(1,128)} %param.14) | copy-start | bytes 28
  7.5 13.9 %copy-start.6 = (bf16[1,128,4096]{2,1,0:T(8,128)(2,1)S(1)}, bf16[1,128,4096]{2,1,0:T(8,128)(2,1)}, u32[]{:S(2)}) copy-start(bf16[1,128,4096]{2,1,0:T(8,128)(2,1)} %param.12) | copy-start | bytes 3145732
  7.5 62.1 %all-to-all-start = ((bf16[32,264,128]{2,1,0:T(8,128)(2,1)}), bf16[32,264,128]{2,1,0:T(8,128)(2,1)S(1)}, u32[]{:S(2)}, u32[]{:S(2)}) async-start(bf16[32,264,128]{2,1,0:T(8,128)(2,1)} %pad_maximum_fusion), calls=%async_computation | async-start | bytes 4325376 | tf_op jit(solution)/shard_map/all_to_all | solution.py:213
  20.3 1.2 copy-start.9
  20.4 3.7 %collective-permute-start = (s32[195]{0:T(256)S(1)}, s32[195]{0:T(256)S(1)}, u32[]{:S(2)}, u32[]{:S(2)}) collective-permute-start(s32[195]{0:T(256)S(1)} %pad_add_fusion), channel_id=1, source_target_pairs={{0,224},{32,0},{64,32},{96,64},{128,96},{160,128},{192,160},{224,1... | collective-permute-start | bytes 2348 | tf_op jit(solution)/shard_map/ppermute | solution.py:21
  24.1 14.5 %collective-permute-start.3 = (bf16[32,2,64,128]{3,2,1,0:T(8,128)(2,1)S(1)}, bf16[32,2,64,128]{3,2,1,0:T(8,128)(2,1)S(1)}, u32[]{:S(2)}, u32[]{:S(2)}) collective-permute-start(bf16[32,2,64,128]{3,2,1,0:T(8,128)(2,1)S(1)} %bitcast.49), channel_id=1, source_target_pairs={{0,224},{32,0},{64,32},{96,64},{128,96},{160,128},{192,160},{224,1... | collective-permute-start | bytes 3145736 | tf_op jit(solution)/shard_map/ppermute | solution.py:21
  26.1 50.7 %collective-permute-start.1 = (bf16[32,2,64,128]{3,2,1,0:T(8,128)(2,1)}, bf16[32,2,64,128]{3,2,1,0:T(8,128)(2,1)}, u32[]{:S(2)}, u32[]{:S(2)}) collective-permute-start(bf16[32,2,64,128]{3,2,1,0:T(8,128)(2,1)} %bitcast.44), channel_id=1, source_target_pairs={{0,224},{32,0},{64,32},{96,64},{128,96},{160,128},{192,160},{224,1... | collective-permute-start | bytes 3145736 | tf_op jit(solution)/shard_map/ppermute | solution.py:21
  38.7 1.0 copy-start.10
  69.6 7.2 %copy-start.7 = (bf16[32,264,128]{2,1,0:T(8,128)(2,1)}, bf16[32,264,128]{2,1,0:T(8,128)(2,1)S(1)}, u32[]{:S(2)}) copy-start(bf16[32,264,128]{2,1,0:T(8,128)(2,1)S(1)} %all-to-all-done) | copy-start | bytes 6488068
  69.6 32.1 %all-to-all-start.1 = ((bf16[32,2,64,128]{3,2,1,0:T(8,128)(2,1)}), bf16[32,2,64,128]{3,2,1,0:T(8,128)(2,1)S(1)}, u32[]{:S(2)}, u32[]{:S(2)}) async-start(bf16[32,2,64,128]{3,2,1,0:T(8,128)(2,1)} %copy-done.10), calls=%async_computation.1 | async-start | bytes 2097152 | tf_op jit(solution)/shard_map/all_to_all | solution.py:223
  76.8 36.0 %collective-permute-start.2 = (bf16[32,264,128]{2,1,0:T(8,128)(2,1)}, bf16[32,264,128]{2,1,0:T(8,128)(2,1)S(1)}, u32[]{:S(2)}, u32[]{:S(2)}) collective-permute-start(bf16[32,264,128]{2,1,0:T(8,128)(2,1)} %copy-done.7), channel_id=1, source_target_pairs={{0,224},{32,0},{64,32},{96,64},{128,96},{160,128},{192,160},{224,1... | collective-permute-start | bytes 6488072 | tf_op jit(solution)/shard_map/ppermute | solution.py:21
  101.7 44.9 %all-to-all-start.3 = ((bf16[32,2,64,128]{3,2,1,0:T(8,128)(2,1)}), bf16[32,2,64,128]{3,2,1,0:T(8,128)(2,1)}, u32[]{:S(2)}, u32[]{:S(2)}) async-start(bf16[32,2,64,128]{3,2,1,0:T(8,128)(2,1)} %collective-permute-done.1), calls=%async_computation.3 | async-start | bytes 2097152 | tf_op jit(solution)/shard_map/all_to_all | solution.py:223
  112.8 1.3 copy-start.5
  116.2 39.5 %copy-start = (f32[4096,1]{1,0:T(8,128)S(1)}, f32[4096,1]{1,0:T(8,128)}, u32[]{:S(2)}) copy-start(f32[4096,1]{1,0:T(8,128)} %copy.72.corr_ref) | copy-start | bytes 49156
  143.0 1.4 copy-start.1
  144.4 1.3 copy-start.3
  145.8 0.8 copy-start.4
  146.6 40.0 %all-to-all-start.2 = ((bf16[32,64,128]{2,1,0:T(8,128)(2,1)}), bf16[32,64,128]{2,1,0:T(8,128)(2,1)S(1)}, u32[]{:S(2)}, u32[]{:S(2)}) async-start(bf16[32,64,128]{2,1,0:T(8,128)(2,1)} %copy-done.4), calls=%async_computation.2 | async-start | bytes 1048576 | tf_op jit(solution)/shard_map/all_to_all | solution.py:231
  155.7 1.6 copy-start.2
  186.6 67.1 %copy-start.8 = (bf16[32,64,128]{2,1,0:T(8,128)(2,1)}, bf16[32,64,128]{2,1,0:T(8,128)(2,1)S(1)}, u32[]{:S(2)}) copy-start(bf16[32,64,128]{2,1,0:T(8,128)(2,1)S(1)} %all-to-all-done.2.first_ref) | copy-start | bytes 1572868

commit v7 on v6

--- a/solution.py
+++ b/solution.py
@@ -55,7 +55,7 @@
     dv_acc[...] = jnp.zeros_like(dv_acc)
     lane_slot = lax.broadcasted_iota(jnp.int32, (1, KB * BLK), 1) // BLK
 
-    def one_block(t, carry):
+    def one_block(t, u):
         i = t * per_chunk + parity
         query = qd_ref[t, 0]
         grad = qd_ref[t, 1]
@@ -64,11 +64,11 @@
             kb = slot_ref[i * KB + j]
             kc = kb // per_chunk
             kr = pl.multiple_of((kb % per_chunk) * BLK, BLK)
-            kt_ref[pl.ds(j * BLK, BLK), :] = kv_ref[kc, pl.ds(kr, BLK), :]
-            vt_ref[pl.ds(j * BLK, BLK), :] = kv_ref[kc, pl.ds(chunk_rows + kr, BLK), :]
+            kt_ref[u, pl.ds(j * BLK, BLK), :] = kv_ref[kc, pl.ds(kr, BLK), :]
+            vt_ref[u, pl.ds(j * BLK, BLK), :] = kv_ref[kc, pl.ds(chunk_rows + kr, BLK), :]
             live = live | ((lane_slot == j) & (valid_ref[i * KB + j] != 0))
-        key_tiles = kt_ref[...]
-        value_tiles = vt_ref[...]
+        key_tiles = kt_ref[u]
+        value_tiles = vt_ref[u]
         scores = lax.dot_general(
             query, key_tiles, (((1,), (1,)), ((), ())), preferred_element_type=jnp.float32
         ) * score_scale
@@ -90,13 +90,22 @@
             attention.astype(jnp.bfloat16), grad, (((0,), (0,)), ((), ())),
             preferred_element_type=jnp.float32,
         )
+        return i, key_part, value_part
+
+    def scatter(i, key_part, value_part):
         for j in range(KB):
             kb = slot_ref[i * KB + j]
             dk_acc[kb] = dk_acc[kb] + key_part[j * BLK:(j + 1) * BLK]
             dv_acc[kb] = dv_acc[kb] + value_part[j * BLK:(j + 1) * BLK]
+
+    def two_blocks(t2, carry):
+        first = one_block(2 * t2, 0)
+        second = one_block(2 * t2 + 1, 1)
+        scatter(*first)
+        scatter(*second)
         return carry
 
-    lax.fori_loop(0, block_count // per_chunk, one_block, 0)
+    lax.fori_loop(0, block_count // per_chunk // 2, two_blocks, 0)
 
     if final:
         def one_chunk(c, carry):
@@ -124,7 +133,7 @@
         head_kernel, block_count=block_count, chunk_rows=chunk_rows, parity=parity, final=final
     )
     operands = [slot_index.reshape(-1), slot_valid.reshape(-1), kv, qd, corr]
-    scratch = [pltpu.VMEM((KB * BLK, HD), jnp.bfloat16), pltpu.VMEM((KB * BLK, HD), jnp.bfloat16)]
+    scratch = [pltpu.VMEM((2, KB * BLK, HD), jnp.bfloat16), pltpu.VMEM((2, KB * BLK, HD), jnp.bfloat16)]
     if final:
         operands += list(previous[1:])
         out_shape = (jax.ShapeDtypeStruct((chunks, BLK + 2 * chunk_rows, HD), jnp.bfloat16),)
@@ -214,14 +223,15 @@
     after = kv
     kv, _ = lax.optimization_barrier((kv, shipped[-1]))
     kv = passed_along(kv, "pipe", -1)
-    got = kv[:, 2 * local:2 * local + 3, :].astype(jnp.float32)
-    correction = ((got[:, 0] + got[:, 1]) + got[:, 2]).reshape(length, 1)
     slot_index, slot_valid = slot_table(random_list, global_list, head_radius, block_count)
     previous = None
     for parity in range(per_chunk):
         qd, _ = lax.optimization_barrier((shipped[parity], after))
         qd = lax.all_to_all(qd, "ctx", split_axis=0, concat_axis=0, tiled=True)
         after = qd
+        if parity == 0:
+            got = kv[:, 2 * local:2 * local + 3, :].astype(jnp.float32)
+            correction = ((got[:, 0] + got[:, 1]) + got[:, 2]).reshape(length, 1)
         result = head_part(
             kv, qd, correction, slot_index, slot_valid, previous, block_count, chunks, local,
             parity,

time: 263 us -> 256 us (0.973)
  Pallas kernels: 60.5 us -> 53.3 us
    pallas_call x2, Pallas kernels: 56.1 us -> 48.9 us  [head_part(): pl.pallas_call(kernel, out_shape=out_shape, in_specs=in_specs, out_specs=...]
  transfers between devices with their start and end apart: 8 -> 8, of which waited for: 4 -> 4; matrix products, arithmetic and copies ran while one was open for 3% -> 3% of each run, Pallas kernels for 22% -> 19%
where the time goes in v7:
time: 256 us; the launch traced here: 251 us
  blocking collectives  67.1 us (26%)
  waiting for transfers between devices  63.8 us (25%)
  Pallas kernels  53.3 us (21%)
  starting transfers between devices  42.9 us (17%)
  local copies, waits for them, and re-layouts  13.7 us (5%)
  other arithmetic  8.54 us (3%)
    all_to_all x1, blocking collectives, body(): lax.all_to_all(result[0], 'ctx', split_axis=0, concat_axis=0, tiled=True)  67.1 us
    pallas_call x2, Pallas kernels, head_part(): pl.pallas_call(kernel, out_shape=out_shape, in_specs=in_specs, out_specs=...  48.9 us
    all_to_all x1, waiting for transfers between devices, body(): kv = lax.all_to_all(kv, 'ctx', split_axis=0, concat_axis=0, tiled=True)  29.9 us
    all_to_all x2, waiting for transfers between devices, body(): qd = lax.all_to_all(qd, 'ctx', split_axis=0, concat_axis=0, tiled=True)  22.5 us
    all_to_all x2, starting transfers between devices, body(): qd = lax.all_to_all(qd, 'ctx', split_axis=0, concat_axis=0, tiled=True)  15.7 us
    all_to_all x1, starting transfers between devices, body(): kv = lax.all_to_all(kv, 'ctx', split_axis=0, concat_axis=0, tiled=True)  12 us
    ppermute x4, waiting for transfers between devices, passed_along(): return lax.ppermute(value, axis, pairs)  11.3 us
    all_to_all x1, starting transfers between devices, body(): lax.all_to_all(result[0], 'ctx', split_axis=0, concat_axis=0, tiled=True)  9.15 us
  transfers between devices with their start and end apart: 8, of which 4 were waited for; matrix products, arithmetic and copies ran while one was open for 3% of the time, Pallas kernels for 19%

profile of v7, /device:TPU:1, one launch (start us, length us, event | category | flops | bytes accessed | tf_op | source)
XLA Modules:
  0.0 250.9 jit_solution(12729163833692421562)
XLA Ops:
  0.6 1.8 multiply_bitcast_fusion
  2.8 0.6 reduce_sum.9
  4.0 1.8 copy_bitcast_fusion
  5.9 1.5 pad_maximum_fusion
  7.5 12.0 %all-to-all-start = ((bf16[32,264,128]{2,1,0:T(8,128)(2,1)}), bf16[32,264,128]{2,1,0:T(8,128)(2,1)S(1)}, u32[]{:S(2)}, u32[]{:S(2)}) async-start(bf16[32,264,128]{2,1,0:T(8,128)(2,1)} %pad_maximum_fusion), calls=%async_computation | async-start | bytes 4325376 | tf_op jit(solution)/shard_map/all_to_all | solution.py:222
  20.4 1.0 collective-permute-start
  22.1 2.0 collective-permute-done
  24.1 0.7 collective-permute-start.3
  24.9 1.3 copy.88
  26.1 3.2 %collective-permute-start.1 = (bf16[32,2,64,128]{3,2,1,0:T(8,128)(2,1)}, bf16[32,2,64,128]{3,2,1,0:T(8,128)(2,1)}, u32[]{:S(2)}, u32[]{:S(2)}) collective-permute-start(bf16[32,2,64,128]{3,2,1,0:T(8,128)(2,1)} %bitcast.44), channel_id=1, source_target_pairs={{0,224},{32,0},{64,32},{96,64},{128,96},{160,128},{192,160},{224,1... | collective-permute-start | bytes 3145736 | tf_op jit(solution)/shard_map/ppermute | solution.py:21
  29.4 9.3 %collective-permute-done.3 = bf16[32,2,64,128]{3,2,1,0:T(8,128)(2,1)S(1)} collective-permute-done((bf16[32,2,64,128]{3,2,1,0:T(8,128)(2,1)S(1)}, bf16[32,2,64,128]{3,2,1,0:T(8,128)(2,1)S(1)}, u32[]{:S(2)}, u32[]{:S(2)}) %collective-permute-start.3) | collective-permute-done | bytes 1048608 | tf_op jit(solution)/shard_map/ppermute | solution.py:21
  38.7 1.0 copy-done.10
  39.6 29.9 %all-to-all-done = bf16[32,264,128]{2,1,0:T(8,128)(2,1)S(1)} async-done(((bf16[32,264,128]{2,1,0:T(8,128)(2,1)}), bf16[32,264,128]{2,1,0:T(8,128)(2,1)S(1)}, u32[]{:S(2)}, u32[]{:S(2)}) %all-to-all-start) | async-done | bytes 2162720 | tf_op jit(solution)/shard_map/all_to_all | solution.py:222
  69.6 7.2 %all-to-all-start.1 = ((bf16[32,2,64,128]{3,2,1,0:T(8,128)(2,1)}), bf16[32,2,64,128]{3,2,1,0:T(8,128)(2,1)S(1)}, u32[]{:S(2)}, u32[]{:S(2)}) async-start(bf16[32,2,64,128]{3,2,1,0:T(8,128)(2,1)} %copy-done.10), calls=%async_computation.1 | async-start | bytes 2097152 | tf_op jit(solution)/shard_map/all_to_all | solution.py:230
  76.8 1.2 collective-permute-start.2
  78.4 0.6 slice.47
  79.2 22.5 %all-to-all-done.1.qd_ref = bf16[32,2,64,128]{3,2,1,0:T(8,128)(2,1)S(1)} async-done(((bf16[32,2,64,128]{3,2,1,0:T(8,128)(2,1)}), bf16[32,2,64,128]{3,2,1,0:T(8,128)(2,1)S(1)}, u32[]{:S(2)}, u32[]{:S(2)}) %all-to-all-start.1) | async-done | bytes 1048608 | tf_op jit(solution)/shard_map/all_to_all | solution.py:230
  101.7 8.4 %all-to-all-start.3 = ((bf16[32,2,64,128]{3,2,1,0:T(8,128)(2,1)}), bf16[32,2,64,128]{3,2,1,0:T(8,128)(2,1)}, u32[]{:S(2)}, u32[]{:S(2)}) async-start(bf16[32,2,64,128]{3,2,1,0:T(8,128)(2,1)} %collective-permute-done.1), calls=%async_computation.3 | async-start | bytes 2097152 | tf_op jit(solution)/shard_map/all_to_all | solution.py:230
  110.1 0.7 abs_compare_fusion.2
  111.1 0.7 abs_compare_fusion.1
  111.9 0.7 not_and_fusion
  112.9 1.3 copy-done.5
  114.2 2.0 copy.72.corr_ref
  116.2 23.3 %shard_map.103 = (bf16[32,64,128]{2,1,0:T(8,128)(2,1)S(1)}, f32[64,64,128]{2,1,0:T(8,128)S(1)}, f32[64,64,128]{2,1,0:T(8,128)S(1)}) custom-call(s32[640]{0:T(1024)S(1)} %min.22.slot_ref, s32[640]{0:T(1024)S(1)} %reshape.123.valid_ref, bf16[32,264,128]{2,1,0:T(8,128)(2,1)} %copy-done.5, bf16[32,2,64,128]{3,2,1,0:T(8,128)(2,1)S(1)} %all-to-all-done.1.qd_ref, ...), custom_call_target="tpu_custom_call" | custom-call | tf_op jit(solution)/shard_map/pallas_call | solution.py:146
  139.5 1.4 copy-done.1
  140.9 1.3 copy-done.3
  142.3 0.8 copy-done.4
  143.1 9.2 %all-to-all-start.2 = ((bf16[32,64,128]{2,1,0:T(8,128)(2,1)}), bf16[32,64,128]{2,1,0:T(8,128)(2,1)S(1)}, u32[]{:S(2)}, u32[]{:S(2)}) async-start(bf16[32,64,128]{2,1,0:T(8,128)(2,1)} %copy-done.4), calls=%async_computation.2 | async-start | bytes 1048576 | tf_op jit(solution)/shard_map/all_to_all | solution.py:241
  152.2 1.6 copy-done.2
  153.8 25.6 %shard_map.104 = bf16[32,320,128]{2,1,0:T(8,128)(2,1)} custom-call(s32[640]{0:T(1024)S(1)} %min.22.slot_ref, s32[640]{0:T(1024)S(1)} %reshape.123.valid_ref, bf16[32,264,128]{2,1,0:T(8,128)(2,1)} %copy-done.5, bf16[32,2,64,128]{3,2,1,0:T(8,128)(2,1)} %all-to-all-done.3.qd_ref, f32[4096,1]{1,0:T(8,128)S(1)} %copy-done, f32[64,64,128]{2,1,0:T(8,128)S(1)} %copy-done.2, ...), custom_call_target="tpu_custom_call" | custom-call | tf_op jit(solution)/shard_map/pallas_call | solution.py:146
  179.4 67.1 %all_to_all.25.back_ref = bf16[32,320,128]{2,1,0:T(8,128)(2,1)} all-to-all(bf16[32,320,128]{2,1,0:T(8,128)(2,1)} %shard_map.104), channel_id=1, replica_groups=mesh['pipe'=8,'ctx'=32] {'ctx'}, dimensions={0} | all-to-all | bytes 5242880 | tf_op jit(solution)/shard_map/all_to_all | solution.py:242
  246.5 4.4 %shard_map.105 = (bf16[1,128,4096]{2,1,0:T(8,128)(2,1)}, bf16[1,128,4096]{2,1,0:T(8,128)(2,1)}, bf16[1,128,4096]{2,1,0:T(8,128)(2,1)}) custom-call(bf16[32,64,128]{2,1,0:T(8,128)(2,1)} %copy-done.8, bf16[32,320,128]{2,1,0:T(8,128)(2,1)} %all_to_all.25.back_ref), custom_call_target="tpu_custom_call" | custom-call | tf_op jit(solution)/shard_map/pallas_call | solution.py:168
  (59 shorter events, 3.3 us)
Async XLA Ops:
  2.8 1.2 copy-start.11
  7.5 12.6 %copy-start.12 = (s32[1,1,64,3]{2,1,3,0:T(1,128)S(1)}, s32[1,1,64,3]{2,1,3,0:T(1,128)}, u32[]{:S(2)}) copy-start(s32[1,1,64,3]{2,1,3,0:T(1,128)} %param.13) | copy-start | bytes 2308
  7.5 12.9 %copy-start.13 = (s32[1,2]{1,0:T(1,128)S(1)}, s32[1,2]{1,0:T(1,128)}, u32[]{:S(2)}) copy-start(s32[1,2]{1,0:T(1,128)} %param.14) | copy-start | bytes 28
  7.5 13.9 %copy-start.6 = (bf16[1,128,4096]{2,1,0:T(8,128)(2,1)S(1)}, bf16[1,128,4096]{2,1,0:T(8,128)(2,1)}, u32[]{:S(2)}) copy-start(bf16[1,128,4096]{2,1,0:T(8,128)(2,1)} %param.12) | copy-start | bytes 3145732
  7.5 62.1 %all-to-all-start = ((bf16[32,264,128]{2,1,0:T(8,128)(2,1)}), bf16[32,264,128]{2,1,0:T(8,128)(2,1)S(1)}, u32[]{:S(2)}, u32[]{:S(2)}) async-start(bf16[32,264,128]{2,1,0:T(8,128)(2,1)} %pad_maximum_fusion), calls=%async_computation | async-start | bytes 4325376 | tf_op jit(solution)/shard_map/all_to_all | solution.py:222
  20.3 1.2 copy-start.9
  20.4 3.7 %collective-permute-start = (s32[195]{0:T(256)S(1)}, s32[195]{0:T(256)S(1)}, u32[]{:S(2)}, u32[]{:S(2)}) collective-permute-start(s32[195]{0:T(256)S(1)} %pad_add_fusion), channel_id=1, source_target_pairs={{0,224},{32,0},{64,32},{96,64},{128,96},{160,128},{192,160},{224,1... | collective-permute-start | bytes 2348 | tf_op jit(solution)/shard_map/ppermute | solution.py:21
  24.1 14.5 %collective-permute-start.3 = (bf16[32,2,64,128]{3,2,1,0:T(8,128)(2,1)S(1)}, bf16[32,2,64,128]{3,2,1,0:T(8,128)(2,1)S(1)}, u32[]{:S(2)}, u32[]{:S(2)}) collective-permute-start(bf16[32,2,64,128]{3,2,1,0:T(8,128)(2,1)S(1)} %bitcast.49), channel_id=1, source_target_pairs={{0,224},{32,0},{64,32},{96,64},{128,96},{160,128},{192,160},{224,1... | collective-permute-start | bytes 3145736 | tf_op jit(solution)/shard_map/ppermute | solution.py:21
  26.1 50.7 %collective-permute-start.1 = (bf16[32,2,64,128]{3,2,1,0:T(8,128)(2,1)}, bf16[32,2,64,128]{3,2,1,0:T(8,128)(2,1)}, u32[]{:S(2)}, u32[]{:S(2)}) collective-permute-start(bf16[32,2,64,128]{3,2,1,0:T(8,128)(2,1)} %bitcast.44), channel_id=1, source_target_pairs={{0,224},{32,0},{64,32},{96,64},{128,96},{160,128},{192,160},{224,1... | collective-permute-start | bytes 3145736 | tf_op jit(solution)/shard_map/ppermute | solution.py:21
  38.7 1.0 copy-start.10
  69.6 7.2 %copy-start.7 = (bf16[32,264,128]{2,1,0:T(8,128)(2,1)}, bf16[32,264,128]{2,1,0:T(8,128)(2,1)S(1)}, u32[]{:S(2)}) copy-start(bf16[32,264,128]{2,1,0:T(8,128)(2,1)S(1)} %all-to-all-done) | copy-start | bytes 6488068
  69.6 32.1 %all-to-all-start.1 = ((bf16[32,2,64,128]{3,2,1,0:T(8,128)(2,1)}), bf16[32,2,64,128]{3,2,1,0:T(8,128)(2,1)S(1)}, u32[]{:S(2)}, u32[]{:S(2)}) async-start(bf16[32,2,64,128]{3,2,1,0:T(8,128)(2,1)} %copy-done.10), calls=%async_computation.1 | async-start | bytes 2097152 | tf_op jit(solution)/shard_map/all_to_all | solution.py:230
  76.8 36.0 %collective-permute-start.2 = (bf16[32,264,128]{2,1,0:T(8,128)(2,1)}, bf16[32,264,128]{2,1,0:T(8,128)(2,1)S(1)}, u32[]{:S(2)}, u32[]{:S(2)}) collective-permute-start(bf16[32,264,128]{2,1,0:T(8,128)(2,1)} %copy-done.7), channel_id=1, source_target_pairs={{0,224},{32,0},{64,32},{96,64},{128,96},{160,128},{192,160},{224,1... | collective-permute-start | bytes 6488072 | tf_op jit(solution)/shard_map/ppermute | solution.py:21
  101.7 41.4 %all-to-all-start.3 = ((bf16[32,2,64,128]{3,2,1,0:T(8,128)(2,1)}), bf16[32,2,64,128]{3,2,1,0:T(8,128)(2,1)}, u32[]{:S(2)}, u32[]{:S(2)}) async-start(bf16[32,2,64,128]{3,2,1,0:T(8,128)(2,1)} %collective-permute-done.1), calls=%async_computation.3 | async-start | bytes 2097152 | tf_op jit(solution)/shard_map/all_to_all | solution.py:230
  112.8 1.3 copy-start.5
  116.2 36.0 %copy-start = (f32[4096,1]{1,0:T(8,128)S(1)}, f32[4096,1]{1,0:T(8,128)}, u32[]{:S(2)}) copy-start(f32[4096,1]{1,0:T(8,128)} %copy.72.corr_ref) | copy-start | bytes 49156
  139.5 1.4 copy-start.1
  140.9 1.3 copy-start.3
  142.3 0.8 copy-start.4
  143.1 36.3 %all-to-all-start.2 = ((bf16[32,64,128]{2,1,0:T(8,128)(2,1)}), bf16[32,64,128]{2,1,0:T(8,128)(2,1)S(1)}, u32[]{:S(2)}, u32[]{:S(2)}) async-start(bf16[32,64,128]{2,1,0:T(8,128)(2,1)} %copy-done.4), calls=%async_computation.2 | async-start | bytes 1048576 | tf_op jit(solution)/shard_map/all_to_all | solution.py:241
  152.2 1.6 copy-start.2
  179.4 67.1 %copy-start.8 = (bf16[32,64,128]{2,1,0:T(8,128)(2,1)}, bf16[32,64,128]{2,1,0:T(8,128)(2,1)S(1)}, u32[]{:S(2)}) copy-start(bf16[32,64,128]{2,1,0:T(8,128)(2,1)S(1)} %all-to-all-done.2.first_ref) | copy-start | bytes 1572868

commit v8 on v7

--- a/solution.py
+++ b/solution.py
@@ -13,6 +13,7 @@
 RMAX = 2
 NR = 3
 KB = 10
+STEP = 8
 
 
 def passed_along(value, axis, steps):
@@ -98,14 +99,13 @@
             dk_acc[kb] = dk_acc[kb] + key_part[j * BLK:(j + 1) * BLK]
             dv_acc[kb] = dv_acc[kb] + value_part[j * BLK:(j + 1) * BLK]
 
-    def two_blocks(t2, carry):
-        first = one_block(2 * t2, 0)
-        second = one_block(2 * t2 + 1, 1)
-        scatter(*first)
-        scatter(*second)
+    def some_blocks(t, carry):
+        parts = [one_block(STEP * t + u, u) for u in range(STEP)]
+        for part in parts:
+            scatter(*part)
         return carry
 
-    lax.fori_loop(0, block_count // per_chunk // 2, two_blocks, 0)
+    lax.fori_loop(0, block_count // per_chunk // STEP, some_blocks, 0)
 
     if final:
         def one_chunk(c, carry):
@@ -133,7 +133,10 @@
         head_kernel, block_count=block_count, chunk_rows=chunk_rows, parity=parity, final=final
     )
     operands = [slot_index.reshape(-1), slot_valid.reshape(-1), kv, qd, corr]
-    scratch = [pltpu.VMEM((2, KB * BLK, HD), jnp.bfloat16), pltpu.VMEM((2, KB * BLK, HD), jnp.bfloat16)]
+    scratch = [
+        pltpu.VMEM((STEP, KB * BLK, HD), jnp.bfloat16),
+        pltpu.VMEM((STEP, KB * BLK, HD), jnp.bfloat16),
+    ]
     if final:
         operands += list(previous[1:])
         out_shape = (jax.ShapeDtypeStruct((chunks, BLK + 2 * chunk_rows, HD), jnp.bfloat16),)

time: 256 us -> 250 us (0.977)
  Pallas kernels: 53.3 us -> 47.5 us
    pallas_call x2, Pallas kernels: 48.9 us -> 43 us  [head_part(): pl.pallas_call(kernel, out_shape=out_shape, in_specs=in_specs, out_specs=...]
  transfers between devices with their start and end apart: 8 -> 8, of which waited for: 4 -> 4; matrix products, arithmetic and copies ran while one was open for 3% -> 3% of each run, Pallas kernels for 19% -> 18%
where the time goes in v8:
time: 250 us; the launch traced here: 245 us
  blocking collectives  66.9 us (27%)
  waiting for transfers between devices  63.8 us (26%)
  Pallas kernels  47.5 us (19%)
  starting transfers between devices  43.1 us (17%)
  local copies, waits for them, and re-layouts  13.7 us (5%)
  other arithmetic  8.54 us (3%)
    all_to_all x1, blocking collectives, body(): lax.all_to_all(result[0], 'ctx', split_axis=0, concat_axis=0, tiled=True)  66.9 us
    pallas_call x2, Pallas kernels, head_part(): pl.pallas_call(kernel, out_shape=out_shape, in_specs=in_specs, out_specs=...  43 us
    all_to_all x1, waiting for transfers between devices, body(): kv = lax.all_to_all(kv, 'ctx', split_axis=0, concat_axis=0, tiled=True)  29.9 us
    all_to_all x2, waiting for transfers between devices, body(): qd = lax.all_to_all(qd, 'ctx', split_axis=0, concat_axis=0, tiled=True)  22.5 us
    all_to_all x2, starting transfers between devices, body(): qd = lax.all_to_all(qd, 'ctx', split_axis=0, concat_axis=0, tiled=True)  15.7 us
    all_to_all x1, starting transfers between devices, body(): kv = lax.all_to_all(kv, 'ctx', split_axis=0, concat_axis=0, tiled=True)  12 us
    ppermute x4, waiting for transfers between devices, passed_along(): return lax.ppermute(value, axis, pairs)  11.3 us
    all_to_all x1, starting transfers between devices, body(): lax.all_to_all(result[0], 'ctx', split_axis=0, concat_axis=0, tiled=True)  9.35 us
  transfers between devices with their start and end apart: 8, of which 4 were waited for; matrix products, arithmetic and copies ran while one was open for 3% of the time, Pallas kernels for 18%

profile of v8, /device:TPU:1, one launch (start us, length us, event | category | flops | bytes accessed | tf_op | source)
XLA Modules:
  0.0 245.1 jit_solution(580037070639178178)
XLA Ops:
  0.6 1.8 multiply_bitcast_fusion
  2.8 0.6 reduce_sum.9
  4.0 1.8 copy_bitcast_fusion
  5.9 1.5 pad_maximum_fusion
  7.5 12.0 %all-to-all-start = ((bf16[32,264,128]{2,1,0:T(8,128)(2,1)}), bf16[32,264,128]{2,1,0:T(8,128)(2,1)S(1)}, u32[]{:S(2)}, u32[]{:S(2)}) async-start(bf16[32,264,128]{2,1,0:T(8,128)(2,1)} %pad_maximum_fusion), calls=%async_computation | async-start | bytes 4325376 | tf_op jit(solution)/shard_map/all_to_all | solution.py:225
  20.4 1.0 collective-permute-start
  22.1 2.0 collective-permute-done
  24.1 0.7 collective-permute-start.3
  24.9 1.3 copy.88
  26.1 3.2 %collective-permute-start.1 = (bf16[32,2,64,128]{3,2,1,0:T(8,128)(2,1)}, bf16[32,2,64,128]{3,2,1,0:T(8,128)(2,1)}, u32[]{:S(2)}, u32[]{:S(2)}) collective-permute-start(bf16[32,2,64,128]{3,2,1,0:T(8,128)(2,1)} %bitcast.44), channel_id=1, source_target_pairs={{0,224},{32,0},{64,32},{96,64},{128,96},{160,128},{192,160},{224,1... | collective-permute-start | bytes 3145736 | tf_op jit(solution)/shard_map/ppermute | solution.py:22
  29.4 9.3 %collective-permute-done.3 = bf16[32,2,64,128]{3,2,1,0:T(8,128)(2,1)S(1)} collective-permute-done((bf16[32,2,64,128]{3,2,1,0:T(8,128)(2,1)S(1)}, bf16[32,2,64,128]{3,2,1,0:T(8,128)(2,1)S(1)}, u32[]{:S(2)}, u32[]{:S(2)}) %collective-permute-start.3) | collective-permute-done | bytes 1048608 | tf_op jit(solution)/shard_map/ppermute | solution.py:22
  38.7 1.0 copy-done.10
  39.6 29.9 %all-to-all-done = bf16[32,264,128]{2,1,0:T(8,128)(2,1)S(1)} async-done(((bf16[32,264,128]{2,1,0:T(8,128)(2,1)}), bf16[32,264,128]{2,1,0:T(8,128)(2,1)S(1)}, u32[]{:S(2)}, u32[]{:S(2)}) %all-to-all-start) | async-done | bytes 2162720 | tf_op jit(solution)/shard_map/all_to_all | solution.py:225
  69.6 7.2 %all-to-all-start.1 = ((bf16[32,2,64,128]{3,2,1,0:T(8,128)(2,1)}), bf16[32,2,64,128]{3,2,1,0:T(8,128)(2,1)S(1)}, u32[]{:S(2)}, u32[]{:S(2)}) async-start(bf16[32,2,64,128]{3,2,1,0:T(8,128)(2,1)} %copy-done.10), calls=%async_computation.1 | async-start | bytes 2097152 | tf_op jit(solution)/shard_map/all_to_all | solution.py:233
  76.8 1.2 collective-permute-start.2
  78.4 0.6 slice.47
  79.2 22.5 %all-to-all-done.1.qd_ref = bf16[32,2,64,128]{3,2,1,0:T(8,128)(2,1)S(1)} async-done(((bf16[32,2,64,128]{3,2,1,0:T(8,128)(2,1)}), bf16[32,2,64,128]{3,2,1,0:T(8,128)(2,1)S(1)}, u32[]{:S(2)}, u32[]{:S(2)}) %all-to-all-start.1) | async-done | bytes 1048608 | tf_op jit(solution)/shard_map/all_to_all | solution.py:233
  101.7 8.4 %all-to-all-start.3 = ((bf16[32,2,64,128]{3,2,1,0:T(8,128)(2,1)}), bf16[32,2,64,128]{3,2,1,0:T(8,128)(2,1)}, u32[]{:S(2)}, u32[]{:S(2)}) async-start(bf16[32,2,64,128]{3,2,1,0:T(8,128)(2,1)} %collective-permute-done.1), calls=%async_computation.3 | async-start | bytes 2097152 | tf_op jit(solution)/shard_map/all_to_all | solution.py:233
  110.1 0.7 abs_compare_fusion.2
  111.1 0.7 abs_compare_fusion.1
  111.9 0.7 not_and_fusion
  112.9 1.3 copy-done.5
  114.2 2.0 copy.72.corr_ref
  116.2 20.4 %shard_map.103 = (bf16[32,64,128]{2,1,0:T(8,128)(2,1)S(1)}, f32[64,64,128]{2,1,0:T(8,128)S(1)}, f32[64,64,128]{2,1,0:T(8,128)S(1)}) custom-call(s32[640]{0:T(1024)S(1)} %min.22.slot_ref, s32[640]{0:T(1024)S(1)} %reshape.123.valid_ref, bf16[32,264,128]{2,1,0:T(8,128)(2,1)} %copy-done.5, bf16[32,2,64,128]{3,2,1,0:T(8,128)(2,1)S(1)} %all-to-all-done.1.qd_ref, ...), custom_call_target="tpu_custom_call" | custom-call | tf_op jit(solution)/shard_map/pallas_call | solution.py:149
  136.6 1.4 copy-done.1
  138.0 1.3 copy-done.3
  139.4 0.8 copy-done.4
  140.2 9.4 %all-to-all-start.2 = ((bf16[32,64,128]{2,1,0:T(8,128)(2,1)}), bf16[32,64,128]{2,1,0:T(8,128)(2,1)S(1)}, u32[]{:S(2)}, u32[]{:S(2)}) async-start(bf16[32,64,128]{2,1,0:T(8,128)(2,1)} %copy-done.4), calls=%async_computation.2 | async-start | bytes 1048576 | tf_op jit(solution)/shard_map/all_to_all | solution.py:244
  149.6 1.6 copy-done.2
  151.1 22.6 %shard_map.104 = bf16[32,320,128]{2,1,0:T(8,128)(2,1)} custom-call(s32[640]{0:T(1024)S(1)} %min.22.slot_ref, s32[640]{0:T(1024)S(1)} %reshape.123.valid_ref, bf16[32,264,128]{2,1,0:T(8,128)(2,1)} %copy-done.5, bf16[32,2,64,128]{3,2,1,0:T(8,128)(2,1)} %all-to-all-done.3.qd_ref, f32[4096,1]{1,0:T(8,128)S(1)} %copy-done, f32[64,64,128]{2,1,0:T(8,128)S(1)} %copy-done.2, ...), custom_call_target="tpu_custom_call" | custom-call | tf_op jit(solution)/shard_map/pallas_call | solution.py:149
  173.8 66.9 %all_to_all.25.back_ref = bf16[32,320,128]{2,1,0:T(8,128)(2,1)} all-to-all(bf16[32,320,128]{2,1,0:T(8,128)(2,1)} %shard_map.104), channel_id=1, replica_groups=mesh['pipe'=8,'ctx'=32] {'ctx'}, dimensions={0} | all-to-all | bytes 5242880 | tf_op jit(solution)/shard_map/all_to_all | solution.py:245
  240.7 4.4 %shard_map.105 = (bf16[1,128,4096]{2,1,0:T(8,128)(2,1)}, bf16[1,128,4096]{2,1,0:T(8,128)(2,1)}, bf16[1,128,4096]{2,1,0:T(8,128)(2,1)}) custom-call(bf16[32,64,128]{2,1,0:T(8,128)(2,1)} %copy-done.8, bf16[32,320,128]{2,1,0:T(8,128)(2,1)} %all_to_all.25.back_ref), custom_call_target="tpu_custom_call" | custom-call | tf_op jit(solution)/shard_map/pallas_call | solution.py:171
  (59 shorter events, 3.3 us)
Async XLA Ops:
  2.8 1.2 copy-start.11
  7.5 12.6 %copy-start.12 = (s32[1,1,64,3]{2,1,3,0:T(1,128)S(1)}, s32[1,1,64,3]{2,1,3,0:T(1,128)}, u32[]{:S(2)}) copy-start(s32[1,1,64,3]{2,1,3,0:T(1,128)} %param.13) | copy-start | bytes 2308
  7.5 12.9 %copy-start.13 = (s32[1,2]{1,0:T(1,128)S(1)}, s32[1,2]{1,0:T(1,128)}, u32[]{:S(2)}) copy-start(s32[1,2]{1,0:T(1,128)} %param.14) | copy-start | bytes 28
  7.5 13.9 %copy-start.6 = (bf16[1,128,4096]{2,1,0:T(8,128)(2,1)S(1)}, bf16[1,128,4096]{2,1,0:T(8,128)(2,1)}, u32[]{:S(2)}) copy-start(bf16[1,128,4096]{2,1,0:T(8,128)(2,1)} %param.12) | copy-start | bytes 3145732
  7.5 62.1 %all-to-all-start = ((bf16[32,264,128]{2,1,0:T(8,128)(2,1)}), bf16[32,264,128]{2,1,0:T(8,128)(2,1)S(1)}, u32[]{:S(2)}, u32[]{:S(2)}) async-start(bf16[32,264,128]{2,1,0:T(8,128)(2,1)} %pad_maximum_fusion), calls=%async_computation | async-start | bytes 4325376 | tf_op jit(solution)/shard_map/all_to_all | solution.py:225
  20.3 1.2 copy-start.9
  20.4 3.7 %collective-permute-start = (s32[195]{0:T(256)S(1)}, s32[195]{0:T(256)S(1)}, u32[]{:S(2)}, u32[]{:S(2)}) collective-permute-start(s32[195]{0:T(256)S(1)} %pad_add_fusion), channel_id=1, source_target_pairs={{0,224},{32,0},{64,32},{96,64},{128,96},{160,128},{192,160},{224,1... | collective-permute-start | bytes 2348 | tf_op jit(solution)/shard_map/ppermute | solution.py:22
  24.1 14.5 %collective-permute-start.3 = (bf16[32,2,64,128]{3,2,1,0:T(8,128)(2,1)S(1)}, bf16[32,2,64,128]{3,2,1,0:T(8,128)(2,1)S(1)}, u32[]{:S(2)}, u32[]{:S(2)}) collective-permute-start(bf16[32,2,64,128]{3,2,1,0:T(8,128)(2,1)S(1)} %bitcast.49), channel_id=1, source_target_pairs={{0,224},{32,0},{64,32},{96,64},{128,96},{160,128},{192,160},{224,1... | collective-permute-start | bytes 3145736 | tf_op jit(solution)/shard_map/ppermute | solution.py:22
  26.1 50.7 %collective-permute-start.1 = (bf16[32,2,64,128]{3,2,1,0:T(8,128)(2,1)}, bf16[32,2,64,128]{3,2,1,0:T(8,128)(2,1)}, u32[]{:S(2)}, u32[]{:S(2)}) collective-permute-start(bf16[32,2,64,128]{3,2,1,0:T(8,128)(2,1)} %bitcast.44), channel_id=1, source_target_pairs={{0,224},{32,0},{64,32},{96,64},{128,96},{160,128},{192,160},{224,1... | collective-permute-start | bytes 3145736 | tf_op jit(solution)/shard_map/ppermute | solution.py:22
  38.7 1.0 copy-start.10
  69.6 7.2 %copy-start.7 = (bf16[32,264,128]{2,1,0:T(8,128)(2,1)}, bf16[32,264,128]{2,1,0:T(8,128)(2,1)S(1)}, u32[]{:S(2)}) copy-start(bf16[32,264,128]{2,1,0:T(8,128)(2,1)S(1)} %all-to-all-done) | copy-start | bytes 6488068
  69.6 32.1 %all-to-all-start.1 = ((bf16[32,2,64,128]{3,2,1,0:T(8,128)(2,1)}), bf16[32,2,64,128]{3,2,1,0:T(8,128)(2,1)S(1)}, u32[]{:S(2)}, u32[]{:S(2)}) async-start(bf16[32,2,64,128]{3,2,1,0:T(8,128)(2,1)} %copy-done.10), calls=%async_computation.1 | async-start | bytes 2097152 | tf_op jit(solution)/shard_map/all_to_all | solution.py:233
  76.8 36.0 %collective-permute-start.2 = (bf16[32,264,128]{2,1,0:T(8,128)(2,1)}, bf16[32,264,128]{2,1,0:T(8,128)(2,1)S(1)}, u32[]{:S(2)}, u32[]{:S(2)}) collective-permute-start(bf16[32,264,128]{2,1,0:T(8,128)(2,1)} %copy-done.7), channel_id=1, source_target_pairs={{0,224},{32,0},{64,32},{96,64},{128,96},{160,128},{192,160},{224,1... | collective-permute-start | bytes 6488072 | tf_op jit(solution)/shard_map/ppermute | solution.py:22
  101.7 38.5 %all-to-all-start.3 = ((bf16[32,2,64,128]{3,2,1,0:T(8,128)(2,1)}), bf16[32,2,64,128]{3,2,1,0:T(8,128)(2,1)}, u32[]{:S(2)}, u32[]{:S(2)}) async-start(bf16[32,2,64,128]{3,2,1,0:T(8,128)(2,1)} %collective-permute-done.1), calls=%async_computation.3 | async-start | bytes 2097152 | tf_op jit(solution)/shard_map/all_to_all | solution.py:233
  112.8 1.3 copy-start.5
  116.2 33.3 %copy-start = (f32[4096,1]{1,0:T(8,128)S(1)}, f32[4096,1]{1,0:T(8,128)}, u32[]{:S(2)}) copy-start(f32[4096,1]{1,0:T(8,128)} %copy.72.corr_ref) | copy-start | bytes 49156
  136.6 1.4 copy-start.1
  138.0 1.3 copy-start.3
  139.4 0.8 copy-start.4
  140.2 33.6 %all-to-all-start.2 = ((bf16[32,64,128]{2,1,0:T(8,128)(2,1)}), bf16[32,64,128]{2,1,0:T(8,128)(2,1)S(1)}, u32[]{:S(2)}, u32[]{:S(2)}) async-start(bf16[32,64,128]{2,1,0:T(8,128)(2,1)} %copy-done.4), calls=%async_computation.2 | async-start | bytes 1048576 | tf_op jit(solution)/shard_map/all_to_all | solution.py:244
  149.5 1.6 copy-start.2
  173.8 66.9 %copy-start.8 = (bf16[32,64,128]{2,1,0:T(8,128)(2,1)}, bf16[32,64,128]{2,1,0:T(8,128)(2,1)S(1)}, u32[]{:S(2)}) copy-start(bf16[32,64,128]{2,1,0:T(8,128)(2,1)S(1)} %all-to-all-done.2.first_ref) | copy-start | bytes 1572868

commit v9 on v8

--- a/solution.py
+++ b/solution.py
@@ -13,7 +13,7 @@
 RMAX = 2
 NR = 3
 KB = 10
-STEP = 8
+STEP = 16
 
 
 def passed_along(value, axis, steps):
@@ -58,8 +58,8 @@
 
     def one_block(t, u):
         i = t * per_chunk + parity
-        query = qd_ref[t, 0]
-        grad = qd_ref[t, 1]
+        query = qd_ref[t, 0:BLK, :]
+        grad = qd_ref[t, BLK:2 * BLK, :]
         live = jnp.zeros((1, KB * BLK), jnp.bool_)
         for j in range(KB):
             kb = slot_ref[i * KB + j]
@@ -206,12 +206,6 @@
     random_list = ints[:block_count * NR].reshape(block_count, NR)
     global_list = ints[block_count * NR:-1]
     head_radius = ints[-1]
-    shipped = []
-    for parity in range(per_chunk):
-        rows = slice(parity * BLK, (parity + 1) * BLK)
-        qd = to_chunks(jnp.stack([queries[0, rows], out_grad[0, rows]], axis=0), chunks)
-        qd, _ = lax.optimization_barrier((qd, ints))
-        shipped.append(passed_along(qd, "pipe", -1))
     correction = jnp.sum(
         (attn_out[0].astype(jnp.float32) * out_grad[0].astype(jnp.float32)).reshape(
             local, heads, HD
@@ -220,8 +214,16 @@
     )
     pieces = jnp.stack(split_pieces(correction.T, 3), axis=1)
     pieces = jnp.pad(pieces, ((0, 0), (0, 8 - pieces.shape[1]), (0, 0)))
+    shipped = []
+    for parity in range(per_chunk):
+        rows = slice(parity * BLK, (parity + 1) * BLK)
+        qd = to_chunks(jnp.stack([queries[0, rows], out_grad[0, rows]], axis=0), chunks)
+        qd = qd.reshape(chunks, 2 * BLK, HD)
+        if parity == 0:
+            qd = jnp.concatenate([qd, pieces], axis=1)
+        qd, _ = lax.optimization_barrier((qd, ints))
+        shipped.append(passed_along(qd, "pipe", -1))
     kv = to_chunks(jnp.stack([keys[0], values[0]], axis=0), chunks).reshape(chunks, 2 * local, HD)
-    kv = jnp.concatenate([kv, pieces], axis=1)
     kv = lax.all_to_all(kv, "ctx", split_axis=0, concat_axis=0, tiled=True)
     after = kv
     kv, _ = lax.optimization_barrier((kv, shipped[-1]))
@@ -233,7 +235,7 @@
         qd = lax.all_to_all(qd, "ctx", split_axis=0, concat_axis=0, tiled=True)
         after = qd
         if parity == 0:
-            got = kv[:, 2 * local:2 * local + 3, :].astype(jnp.float32)
+            got = qd[:, 2 * BLK:2 * BLK + 3, :].astype(jnp.float32)
             correction = ((got[:, 0] + got[:, 1]) + got[:, 2]).reshape(length, 1)
         result = head_part(
             kv, qd, correction, slot_index, slot_valid, previous, block_count, chunks, local,

time: 250 us -> 250 us (level)
  the two profiles are of different devices: /device:TPU:1 before, /device:TPU:57 now
where the time goes in v9:
time: 250 us; the launch traced here: 249 us
  waiting for transfers between devices  75.8 us (30%)
  blocking collectives  71.7 us (29%)
  Pallas kernels  46.7 us (19%)
  starting transfers between devices  35.4 us (14%)
  local copies, waits for them, and re-layouts  9.93 us (4%)
  other arithmetic  7.88 us (3%)
    all_to_all x1, blocking collectives, body(): lax.all_to_all(result[0], 'ctx', split_axis=0, concat_axis=0, tiled=True)  71.7 us
    pallas_call x2, Pallas kernels, head_part(): pl.pallas_call(kernel, out_shape=out_shape, in_specs=in_specs, out_specs=...  42.3 us
    ppermute x4, waiting for transfers between devices, passed_along(): return lax.ppermute(value, axis, pairs)  33.2 us
    all_to_all x1, waiting for transfers between devices, body(): kv = lax.all_to_all(kv, 'ctx', split_axis=0, concat_axis=0, tiled=True)  29.6 us
    all_to_all x2, waiting for transfers between devices, body(): qd = lax.all_to_all(qd, 'ctx', split_axis=0, concat_axis=0, tiled=True)  13 us
    all_to_all x2, starting transfers between devices, body(): qd = lax.all_to_all(qd, 'ctx', split_axis=0, concat_axis=0, tiled=True)  12.8 us
    all_to_all x1, starting transfers between devices, body(): kv = lax.all_to_all(kv, 'ctx', split_axis=0, concat_axis=0, tiled=True)  10.8 us
    all_to_all x1, starting transfers between devices, body(): lax.all_to_all(result[0], 'ctx', split_axis=0, concat_axis=0, tiled=True)  9.23 us
  transfers between devices with their start and end apart: 8, of which 5 were waited for; matrix products, arithmetic and copies ran while one was open for 5% of the time, Pallas kernels for 17%

profile of v9, /device:TPU:57, one launch (start us, length us, event | category | flops | bytes accessed | tf_op | source)
XLA Modules:
  0.0 248.9 jit_solution(6391834722444391203)
XLA Ops:
  1.3 0.8 copy.57
  2.2 0.7 pad_add_fusion
  2.9 0.7 collective-permute-start
  3.6 3.5 %copy_bitcast_fusion = bf16[2,128,32,128]{3,1,0,2:T(8,128)(2,1)} fusion(bf16[1,128,4096]{2,1,0:T(8,128)(2,1)} %param.10, bf16[1,128,4096]{2,1,0:T(8,128)(2,1)} %param.9), kind=kLoop, calls=%fused_computation | loop fusion | flops 1048576 | bytes 4194304 | tf_op jit(solution)/shard_map/reshape | solution.py:181
  7.1 10.8 %all-to-all-start = ((bf16[32,256,128]{2,1,0:T(8,128)(2,1)}), bf16[32,256,128]{2,1,0:T(8,128)(2,1)}, u32[]{:S(2)}, u32[]{:S(2)}) async-start(bf16[32,256,128]{2,1,0:T(8,128)(2,1)} %bitcast.4), calls=%async_computation | async-start | bytes 4194304 | tf_op jit(solution)/shard_map/all_to_all | solution.py:227
  18.2 0.4 copy.85
  18.5 0.6 reduce_sum.9
  19.6 0.8 copy-done.6
  20.7 0.3 copy.89
  21.1 0.8 collective-permute-start.3
  21.9 15.8 %collective-permute-done.3 = bf16[32,136,128]{2,1,0:T(8,128)(2,1)} collective-permute-done((bf16[32,136,128]{2,1,0:T(8,128)(2,1)S(1)}, bf16[32,136,128]{2,1,0:T(8,128)(2,1)}, u32[]{:S(2)}, u32[]{:S(2)}) %collective-permute-start.3) | collective-permute-done | bytes 1114144 | tf_op jit(solution)/shard_map/ppermute | solution.py:22
  37.7 29.6 %all-to-all-done = bf16[32,256,128]{2,1,0:T(8,128)(2,1)} async-done(((bf16[32,256,128]{2,1,0:T(8,128)(2,1)}), bf16[32,256,128]{2,1,0:T(8,128)(2,1)}, u32[]{:S(2)}, u32[]{:S(2)}) %all-to-all-start) | async-done | bytes 2097184 | tf_op jit(solution)/shard_map/all_to_all | solution.py:227
  67.3 7.2 %all-to-all-start.1 = ((bf16[32,136,128]{2,1,0:T(8,128)(2,1)}), bf16[32,136,128]{2,1,0:T(8,128)(2,1)S(1)}, u32[]{:S(2)}, u32[]{:S(2)}) async-start(bf16[32,136,128]{2,1,0:T(8,128)(2,1)} %collective-permute-done.3), calls=%async_computation.1 | async-start | bytes 2228224 | tf_op jit(solution)/shard_map/all_to_all | solution.py:235
  74.5 0.3 copy.90
  74.8 1.1 collective-permute-start.1
  76.3 0.6 slice.47
  77.1 13.5 %collective-permute-done.1 = bf16[32,128,128]{2,1,0:T(8,128)(2,1)} collective-permute-done((bf16[32,128,128]{2,1,0:T(8,128)(2,1)S(1)}, bf16[32,128,128]{2,1,0:T(8,128)(2,1)}, u32[]{:S(2)}, u32[]{:S(2)}) %collective-permute-start.1) | collective-permute-done | bytes 1048608 | tf_op jit(solution)/shard_map/ppermute | solution.py:22
  90.5 13.0 %all-to-all-done.1.qd_ref = bf16[32,136,128]{2,1,0:T(8,128)(2,1)S(1)} async-done(((bf16[32,136,128]{2,1,0:T(8,128)(2,1)}), bf16[32,136,128]{2,1,0:T(8,128)(2,1)S(1)}, u32[]{:S(2)}, u32[]{:S(2)}) %all-to-all-start.1) | async-done | bytes 1114144 | tf_op jit(solution)/shard_map/all_to_all | solution.py:235
  103.5 5.6 %all-to-all-start.3 = ((bf16[32,128,128]{2,1,0:T(8,128)(2,1)}), bf16[32,128,128]{2,1,0:T(8,128)(2,1)}, u32[]{:S(2)}, u32[]{:S(2)}) async-start(bf16[32,128,128]{2,1,0:T(8,128)(2,1)} %collective-permute-done.1), calls=%async_computation.3 | async-start | bytes 2097152 | tf_op jit(solution)/shard_map/all_to_all | solution.py:235
  109.1 0.7 abs_compare_fusion.2
  110.1 0.7 abs_compare_fusion.1
  110.9 0.7 not_and_fusion
  111.9 2.0 copy.74.corr_ref
  113.9 3.9 %collective-permute-done.2.kv_ref = bf16[32,256,128]{2,1,0:T(8,128)(2,1)} collective-permute-done((bf16[32,256,128]{2,1,0:T(8,128)(2,1)}, bf16[32,256,128]{2,1,0:T(8,128)(2,1)}, u32[]{:S(2)}, u32[]{:S(2)}) %collective-permute-start.2) | collective-permute-done | bytes 2097184 | tf_op jit(solution)/shard_map/ppermute | solution.py:22
  117.8 19.6 %shard_map.103 = (bf16[32,64,128]{2,1,0:T(8,128)(2,1)S(1)}, f32[64,64,128]{2,1,0:T(8,128)S(1)}, f32[64,64,128]{2,1,0:T(8,128)S(1)}) custom-call(s32[640]{0:T(1024)S(1)} %min.22.slot_ref, s32[640]{0:T(1024)S(1)} %reshape.131.valid_ref, bf16[32,256,128]{2,1,0:T(8,128)(2,1)} %collective-permute-done.2.kv_ref, bf16[32,136,128]{2,1,0:T(8,128)(2,1)S(1)} %all-to-all-done.1.qd_ref, ...), custom_call_target="tpu_custom_call" | custom-call | tf_op jit(solution)/shard_map/pallas_call | solution.py:149
  137.4 1.3 copy-done.1
  138.7 1.4 copy-done.2
  140.1 0.8 copy-done.3
  140.9 9.2 %all-to-all-start.2 = ((bf16[32,64,128]{2,1,0:T(8,128)(2,1)}), bf16[32,64,128]{2,1,0:T(8,128)(2,1)S(1)}, u32[]{:S(2)}, u32[]{:S(2)}) async-start(bf16[32,64,128]{2,1,0:T(8,128)(2,1)} %copy-done.3), calls=%async_computation.2 | async-start | bytes 1048576 | tf_op jit(solution)/shard_map/all_to_all | solution.py:246
  150.2 22.7 %shard_map.104 = bf16[32,320,128]{2,1,0:T(8,128)(2,1)} custom-call(s32[640]{0:T(1024)S(1)} %min.22.slot_ref, s32[640]{0:T(1024)S(1)} %reshape.131.valid_ref, bf16[32,256,128]{2,1,0:T(8,128)(2,1)} %collective-permute-done.2.kv_ref, bf16[32,128,128]{2,1,0:T(8,128)(2,1)} %all-to-all-done.3.qd_ref, f32[4096,1]{1,0:T(8,128)S(1)} %copy-done, ...), custom_call_target="tpu_custom_call" | custom-call | tf_op jit(solution)/shard_map/pallas_call | solution.py:149
  172.8 71.7 %all_to_all.25.back_ref = bf16[32,320,128]{2,1,0:T(8,128)(2,1)} all-to-all(bf16[32,320,128]{2,1,0:T(8,128)(2,1)} %shard_map.104), channel_id=1, replica_groups=mesh['pipe'=8,'ctx'=32] {'ctx'}, dimensions={0} | all-to-all | bytes 5242880 | tf_op jit(solution)/shard_map/all_to_all | solution.py:247
  244.5 4.4 %shard_map.105 = (bf16[1,128,4096]{2,1,0:T(8,128)(2,1)}, bf16[1,128,4096]{2,1,0:T(8,128)(2,1)}, bf16[1,128,4096]{2,1,0:T(8,128)(2,1)}) custom-call(bf16[32,64,128]{2,1,0:T(8,128)(2,1)} %copy-done.5, bf16[32,320,128]{2,1,0:T(8,128)(2,1)} %all_to_all.25.back_ref), custom_call_target="tpu_custom_call" | custom-call | tf_op jit(solution)/shard_map/pallas_call | solution.py:171
  (47 shorter events, 2.4 us)
Async XLA Ops:
  2.9 18.2 %collective-permute-start = (s32[195]{0:T(256)S(1)}, s32[195]{0:T(256)S(1)}, u32[]{:S(2)}, u32[]{:S(2)}) collective-permute-start(s32[195]{0:T(256)S(1)} %pad_add_fusion), channel_id=1, source_target_pairs={{0,224},{32,0},{64,32},{96,64},{128,96},{160,128},{192,160},{224,1... | collective-permute-start | bytes 2348 | tf_op jit(solution)/shard_map/ppermute | solution.py:22
  7.1 10.8 %copy-start.4 = (bf16[1,128,4096]{2,1,0:T(8,128)(2,1)S(1)}, bf16[1,128,4096]{2,1,0:T(8,128)(2,1)}, u32[]{:S(2)}) copy-start(bf16[1,128,4096]{2,1,0:T(8,128)(2,1)} %param.12) | copy-start | bytes 3145732
  7.1 10.8 %copy-start.7 = (bf16[1,128,4096]{2,1,0:T(8,128)(2,1)S(1)}, bf16[1,128,4096]{2,1,0:T(8,128)(2,1)}, u32[]{:S(2)}) copy-start(bf16[1,128,4096]{2,1,0:T(8,128)(2,1)} %param.11) | copy-start | bytes 3145732
  7.1 60.2 %all-to-all-start = ((bf16[32,256,128]{2,1,0:T(8,128)(2,1)}), bf16[32,256,128]{2,1,0:T(8,128)(2,1)}, u32[]{:S(2)}, u32[]{:S(2)}) async-start(bf16[32,256,128]{2,1,0:T(8,128)(2,1)} %bitcast.4), calls=%async_computation | async-start | bytes 4194304 | tf_op jit(solution)/shard_map/all_to_all | solution.py:227
  19.2 1.2 copy-start.6
  21.1 16.5 %collective-permute-start.3 = (bf16[32,136,128]{2,1,0:T(8,128)(2,1)S(1)}, bf16[32,136,128]{2,1,0:T(8,128)(2,1)}, u32[]{:S(2)}, u32[]{:S(2)}) collective-permute-start(bf16[32,136,128]{2,1,0:T(8,128)(2,1)S(1)} %pad_maximum_fusion), channel_id=1, source_target_pairs={{0,224},{32,0},{64,32},{96,64},{128,96},{160,128},{192,160},{224,1... | collective-permute-start | bytes 3342344 | tf_op jit(solution)/shard_map/ppermute | solution.py:22
  67.3 36.2 %all-to-all-start.1 = ((bf16[32,136,128]{2,1,0:T(8,128)(2,1)}), bf16[32,136,128]{2,1,0:T(8,128)(2,1)S(1)}, u32[]{:S(2)}, u32[]{:S(2)}) async-start(bf16[32,136,128]{2,1,0:T(8,128)(2,1)} %collective-permute-done.3), calls=%async_computation.1 | async-start | bytes 2228224 | tf_op jit(solution)/shard_map/all_to_all | solution.py:235
  74.8 15.7 %collective-permute-start.1 = (bf16[32,128,128]{2,1,0:T(8,128)(2,1)S(1)}, bf16[32,128,128]{2,1,0:T(8,128)(2,1)}, u32[]{:S(2)}, u32[]{:S(2)}) collective-permute-start(bf16[32,128,128]{2,1,0:T(8,128)(2,1)S(1)} %bitcast.49), channel_id=1, source_target_pairs={{0,224},{32,0},{64,32},{96,64},{128,96},{160,128},{192,160},{224,1... | collective-permute-start | bytes 3145736 | tf_op jit(solution)/shard_map/ppermute | solution.py:22
  90.5 27.3 %collective-permute-start.2 = (bf16[32,256,128]{2,1,0:T(8,128)(2,1)}, bf16[32,256,128]{2,1,0:T(8,128)(2,1)}, u32[]{:S(2)}, u32[]{:S(2)}) collective-permute-start(bf16[32,256,128]{2,1,0:T(8,128)(2,1)} %all-to-all-done), channel_id=1, source_target_pairs={{0,224},{32,0},{64,32},{96,64},{128,96},{160,128},{192,160},{224,1... | collective-permute-start | bytes 6291464 | tf_op jit(solution)/shard_map/ppermute | solution.py:22
  103.5 37.4 %all-to-all-start.3 = ((bf16[32,128,128]{2,1,0:T(8,128)(2,1)}), bf16[32,128,128]{2,1,0:T(8,128)(2,1)}, u32[]{:S(2)}, u32[]{:S(2)}) async-start(bf16[32,128,128]{2,1,0:T(8,128)(2,1)} %collective-permute-done.1), calls=%async_computation.3 | async-start | bytes 2097152 | tf_op jit(solution)/shard_map/all_to_all | solution.py:235
  113.9 36.3 %copy-start = (f32[4096,1]{1,0:T(8,128)S(1)}, f32[4096,1]{1,0:T(8,128)}, u32[]{:S(2)}) copy-start(f32[4096,1]{1,0:T(8,128)} %copy.74.corr_ref) | copy-start | bytes 49156
  137.4 1.3 copy-start.1
  138.7 1.4 copy-start.2
  140.1 0.8 copy-start.3
  140.9 31.9 %all-to-all-start.2 = ((bf16[32,64,128]{2,1,0:T(8,128)(2,1)}), bf16[32,64,128]{2,1,0:T(8,128)(2,1)S(1)}, u32[]{:S(2)}, u32[]{:S(2)}) async-start(bf16[32,64,128]{2,1,0:T(8,128)(2,1)} %copy-done.3), calls=%async_computation.2 | async-start | bytes 1048576 | tf_op jit(solution)/shard_map/all_to_all | solution.py:246
  172.8 71.7 %copy-start.5 = (bf16[32,64,128]{2,1,0:T(8,128)(2,1)}, bf16[32,64,128]{2,1,0:T(8,128)(2,1)S(1)}, u32[]{:S(2)}) copy-start(bf16[32,64,128]{2,1,0:T(8,128)(2,1)S(1)} %all-to-all-done.2.first_ref) | copy-start | bytes 1572868

commit v10 on v9

--- a/solution.py
+++ b/solution.py
@@ -166,13 +166,19 @@
 
 
 def assemble(first, back, local):
-    vmem = pltpu.MemorySpace.VMEM
-    shape = jax.ShapeDtypeStruct((1, local, first.shape[0] * HD), jnp.bfloat16)
+    heads = first.shape[0]
+    group = 8
+    shape = jax.ShapeDtypeStruct((1, local, heads * HD), jnp.bfloat16)
+    out_spec = pl.BlockSpec((1, local, group * HD), lambda g: (0, 0, g))
     return pl.pallas_call(
         functools.partial(assemble_kernel, local=local),
         out_shape=(shape, shape, shape),
-        in_specs=[pl.BlockSpec(memory_space=vmem)] * 2,
-        out_specs=tuple(pl.BlockSpec(memory_space=vmem) for _ in range(3)),
+        grid=(heads // group,),
+        in_specs=[
+            pl.BlockSpec((group,) + first.shape[1:], lambda g: (g, 0, 0)),
+            pl.BlockSpec((group,) + back.shape[1:], lambda g: (g, 0, 0)),
+        ],
+        out_specs=(out_spec, out_spec, out_spec),
     )(first, back)
 
 

time: 250 us -> 250 us (level)
  no operation moved by 1% of the time
where the time goes in v10:
time: 250 us; the launch traced here: 249 us
  waiting for transfers between devices  75.8 us (30%)
  blocking collectives  71.7 us (29%)
  Pallas kernels  46.8 us (19%)
  starting transfers between devices  35.4 us (14%)
  local copies, waits for them, and re-layouts  9.93 us (4%)
  other arithmetic  7.88 us (3%)
    all_to_all x1, blocking collectives, body(): lax.all_to_all(result[0], 'ctx', split_axis=0, concat_axis=0, tiled=True)  71.7 us
    pallas_call x2, Pallas kernels, head_part(): pl.pallas_call(kernel, out_shape=out_shape, in_specs=in_specs, out_specs=...  42.3 us
    ppermute x4, waiting for transfers between devices, passed_along(): return lax.ppermute(value, axis, pairs)  33.2 us
    all_to_all x1, waiting for transfers between devices, body(): kv = lax.all_to_all(kv, 'ctx', split_axis=0, concat_axis=0, tiled=True)  29.6 us
    all_to_all x2, waiting for transfers between devices, body(): qd = lax.all_to_all(qd, 'ctx', split_axis=0, concat_axis=0, tiled=True)  13 us
    all_to_all x2, starting transfers between devices, body(): qd = lax.all_to_all(qd, 'ctx', split_axis=0, concat_axis=0, tiled=True)  12.8 us
    all_to_all x1, starting transfers between devices, body(): kv = lax.all_to_all(kv, 'ctx', split_axis=0, concat_axis=0, tiled=True)  10.8 us
    all_to_all x1, starting transfers between devices, body(): lax.all_to_all(result[0], 'ctx', split_axis=0, concat_axis=0, tiled=True)  9.23 us
  transfers between devices with their start and end apart: 8, of which 5 were waited for; matrix products, arithmetic and copies ran while one was open for 5% of the time, Pallas kernels for 17%

profile of v10, /device:TPU:57, one launch (start us, length us, event | category | flops | bytes accessed | tf_op | source)
XLA Modules:
  0.0 249.0 jit_solution(17933220130479646109)
XLA Ops:
  1.3 0.8 copy.57
  2.2 0.7 pad_add_fusion
  2.9 0.7 collective-permute-start
  3.6 3.5 %copy_bitcast_fusion = bf16[2,128,32,128]{3,1,0,2:T(8,128)(2,1)} fusion(bf16[1,128,4096]{2,1,0:T(8,128)(2,1)} %param.10, bf16[1,128,4096]{2,1,0:T(8,128)(2,1)} %param.9), kind=kLoop, calls=%fused_computation | loop fusion | flops 1048576 | bytes 4194304 | tf_op jit(solution)/shard_map/reshape | solution.py:187
  7.1 10.8 %all-to-all-start = ((bf16[32,256,128]{2,1,0:T(8,128)(2,1)}), bf16[32,256,128]{2,1,0:T(8,128)(2,1)}, u32[]{:S(2)}, u32[]{:S(2)}) async-start(bf16[32,256,128]{2,1,0:T(8,128)(2,1)} %bitcast.4), calls=%async_computation | async-start | bytes 4194304 | tf_op jit(solution)/shard_map/all_to_all | solution.py:233
  18.2 0.4 copy.85
  18.5 0.6 reduce_sum.9
  19.6 0.8 copy-done.6
  20.7 0.3 copy.89
  21.1 0.8 collective-permute-start.3
  21.9 15.8 %collective-permute-done.3 = bf16[32,136,128]{2,1,0:T(8,128)(2,1)} collective-permute-done((bf16[32,136,128]{2,1,0:T(8,128)(2,1)S(1)}, bf16[32,136,128]{2,1,0:T(8,128)(2,1)}, u32[]{:S(2)}, u32[]{:S(2)}) %collective-permute-start.3) | collective-permute-done | bytes 1114144 | tf_op jit(solution)/shard_map/ppermute | solution.py:22
  37.7 29.6 %all-to-all-done = bf16[32,256,128]{2,1,0:T(8,128)(2,1)} async-done(((bf16[32,256,128]{2,1,0:T(8,128)(2,1)}), bf16[32,256,128]{2,1,0:T(8,128)(2,1)}, u32[]{:S(2)}, u32[]{:S(2)}) %all-to-all-start) | async-done | bytes 2097184 | tf_op jit(solution)/shard_map/all_to_all | solution.py:233
  67.3 7.2 %all-to-all-start.1 = ((bf16[32,136,128]{2,1,0:T(8,128)(2,1)}), bf16[32,136,128]{2,1,0:T(8,128)(2,1)S(1)}, u32[]{:S(2)}, u32[]{:S(2)}) async-start(bf16[32,136,128]{2,1,0:T(8,128)(2,1)} %collective-permute-done.3), calls=%async_computation.1 | async-start | bytes 2228224 | tf_op jit(solution)/shard_map/all_to_all | solution.py:241
  74.5 0.3 copy.90
  74.8 1.1 collective-permute-start.1
  76.3 0.6 slice.47
  77.1 13.5 %collective-permute-done.1 = bf16[32,128,128]{2,1,0:T(8,128)(2,1)} collective-permute-done((bf16[32,128,128]{2,1,0:T(8,128)(2,1)S(1)}, bf16[32,128,128]{2,1,0:T(8,128)(2,1)}, u32[]{:S(2)}, u32[]{:S(2)}) %collective-permute-start.1) | collective-permute-done | bytes 1048608 | tf_op jit(solution)/shard_map/ppermute | solution.py:22
  90.5 13.0 %all-to-all-done.1.qd_ref = bf16[32,136,128]{2,1,0:T(8,128)(2,1)S(1)} async-done(((bf16[32,136,128]{2,1,0:T(8,128)(2,1)}), bf16[32,136,128]{2,1,0:T(8,128)(2,1)S(1)}, u32[]{:S(2)}, u32[]{:S(2)}) %all-to-all-start.1) | async-done | bytes 1114144 | tf_op jit(solution)/shard_map/all_to_all | solution.py:241
  103.5 5.6 %all-to-all-start.3 = ((bf16[32,128,128]{2,1,0:T(8,128)(2,1)}), bf16[32,128,128]{2,1,0:T(8,128)(2,1)}, u32[]{:S(2)}, u32[]{:S(2)}) async-start(bf16[32,128,128]{2,1,0:T(8,128)(2,1)} %collective-permute-done.1), calls=%async_computation.3 | async-start | bytes 2097152 | tf_op jit(solution)/shard_map/all_to_all | solution.py:241
  109.1 0.7 abs_compare_fusion.2
  110.1 0.7 abs_compare_fusion.1
  110.9 0.7 not_and_fusion
  111.9 2.0 copy.74.corr_ref
  113.9 3.9 %collective-permute-done.2.kv_ref = bf16[32,256,128]{2,1,0:T(8,128)(2,1)} collective-permute-done((bf16[32,256,128]{2,1,0:T(8,128)(2,1)}, bf16[32,256,128]{2,1,0:T(8,128)(2,1)}, u32[]{:S(2)}, u32[]{:S(2)}) %collective-permute-start.2) | collective-permute-done | bytes 2097184 | tf_op jit(solution)/shard_map/ppermute | solution.py:22
  117.8 19.6 %shard_map.103 = (bf16[32,64,128]{2,1,0:T(8,128)(2,1)S(1)}, f32[64,64,128]{2,1,0:T(8,128)S(1)}, f32[64,64,128]{2,1,0:T(8,128)S(1)}) custom-call(s32[640]{0:T(1024)S(1)} %min.22.slot_ref, s32[640]{0:T(1024)S(1)} %reshape.131.valid_ref, bf16[32,256,128]{2,1,0:T(8,128)(2,1)} %collective-permute-done.2.kv_ref, bf16[32,136,128]{2,1,0:T(8,128)(2,1)S(1)} %all-to-all-done.1.qd_ref, ...), custom_call_target="tpu_custom_call" | custom-call | tf_op jit(solution)/shard_map/pallas_call | solution.py:149
  137.4 1.3 copy-done.1
  138.7 1.4 copy-done.2
  140.1 0.8 copy-done.3
  140.9 9.2 %all-to-all-start.2 = ((bf16[32,64,128]{2,1,0:T(8,128)(2,1)}), bf16[32,64,128]{2,1,0:T(8,128)(2,1)S(1)}, u32[]{:S(2)}, u32[]{:S(2)}) async-start(bf16[32,64,128]{2,1,0:T(8,128)(2,1)} %copy-done.3), calls=%async_computation.2 | async-start | bytes 1048576 | tf_op jit(solution)/shard_map/all_to_all | solution.py:252
  150.2 22.7 %shard_map.104 = bf16[32,320,128]{2,1,0:T(8,128)(2,1)} custom-call(s32[640]{0:T(1024)S(1)} %min.22.slot_ref, s32[640]{0:T(1024)S(1)} %reshape.131.valid_ref, bf16[32,256,128]{2,1,0:T(8,128)(2,1)} %collective-permute-done.2.kv_ref, bf16[32,128,128]{2,1,0:T(8,128)(2,1)} %all-to-all-done.3.qd_ref, f32[4096,1]{1,0:T(8,128)S(1)} %copy-done, ...), custom_call_target="tpu_custom_call" | custom-call | tf_op jit(solution)/shard_map/pallas_call | solution.py:149
  172.8 71.7 %all_to_all.25.back_ref = bf16[32,320,128]{2,1,0:T(8,128)(2,1)} all-to-all(bf16[32,320,128]{2,1,0:T(8,128)(2,1)} %shard_map.104), channel_id=1, replica_groups=mesh['pipe'=8,'ctx'=32] {'ctx'}, dimensions={0} | all-to-all | bytes 5242880 | tf_op jit(solution)/shard_map/all_to_all | solution.py:253
  244.5 4.5 %shard_map.105 = (bf16[1,128,4096]{2,1,0:T(8,128)(2,1)}, bf16[1,128,4096]{2,1,0:T(8,128)(2,1)}, bf16[1,128,4096]{2,1,0:T(8,128)(2,1)}) custom-call(bf16[32,64,128]{2,1,0:T(8,128)(2,1)} %copy-done.5, bf16[32,320,128]{2,1,0:T(8,128)(2,1)} %all_to_all.25.back_ref), custom_call_target="tpu_custom_call" | custom-call | tf_op jit(solution)/shard_map/pallas_call | solution.py:173
  (47 shorter events, 2.4 us)
Async XLA Ops:
  2.9 18.2 %collective-permute-start = (s32[195]{0:T(256)S(1)}, s32[195]{0:T(256)S(1)}, u32[]{:S(2)}, u32[]{:S(2)}) collective-permute-start(s32[195]{0:T(256)S(1)} %pad_add_fusion), channel_id=1, source_target_pairs={{0,224},{32,0},{64,32},{96,64},{128,96},{160,128},{192,160},{224,1... | collective-permute-start | bytes 2348 | tf_op jit(solution)/shard_map/ppermute | solution.py:22
  7.1 10.8 %copy-start.4 = (bf16[1,128,4096]{2,1,0:T(8,128)(2,1)S(1)}, bf16[1,128,4096]{2,1,0:T(8,128)(2,1)}, u32[]{:S(2)}) copy-start(bf16[1,128,4096]{2,1,0:T(8,128)(2,1)} %param.12) | copy-start | bytes 3145732
  7.1 10.8 %copy-start.7 = (bf16[1,128,4096]{2,1,0:T(8,128)(2,1)S(1)}, bf16[1,128,4096]{2,1,0:T(8,128)(2,1)}, u32[]{:S(2)}) copy-start(bf16[1,128,4096]{2,1,0:T(8,128)(2,1)} %param.11) | copy-start | bytes 3145732
  7.1 60.2 %all-to-all-start = ((bf16[32,256,128]{2,1,0:T(8,128)(2,1)}), bf16[32,256,128]{2,1,0:T(8,128)(2,1)}, u32[]{:S(2)}, u32[]{:S(2)}) async-start(bf16[32,256,128]{2,1,0:T(8,128)(2,1)} %bitcast.4), calls=%async_computation | async-start | bytes 4194304 | tf_op jit(solution)/shard_map/all_to_all | solution.py:233
  19.2 1.2 copy-start.6
  21.1 16.5 %collective-permute-start.3 = (bf16[32,136,128]{2,1,0:T(8,128)(2,1)S(1)}, bf16[32,136,128]{2,1,0:T(8,128)(2,1)}, u32[]{:S(2)}, u32[]{:S(2)}) collective-permute-start(bf16[32,136,128]{2,1,0:T(8,128)(2,1)S(1)} %pad_maximum_fusion), channel_id=1, source_target_pairs={{0,224},{32,0},{64,32},{96,64},{128,96},{160,128},{192,160},{224,1... | collective-permute-start | bytes 3342344 | tf_op jit(solution)/shard_map/ppermute | solution.py:22
  67.3 36.2 %all-to-all-start.1 = ((bf16[32,136,128]{2,1,0:T(8,128)(2,1)}), bf16[32,136,128]{2,1,0:T(8,128)(2,1)S(1)}, u32[]{:S(2)}, u32[]{:S(2)}) async-start(bf16[32,136,128]{2,1,0:T(8,128)(2,1)} %collective-permute-done.3), calls=%async_computation.1 | async-start | bytes 2228224 | tf_op jit(solution)/shard_map/all_to_all | solution.py:241
  74.8 15.7 %collective-permute-start.1 = (bf16[32,128,128]{2,1,0:T(8,128)(2,1)S(1)}, bf16[32,128,128]{2,1,0:T(8,128)(2,1)}, u32[]{:S(2)}, u32[]{:S(2)}) collective-permute-start(bf16[32,128,128]{2,1,0:T(8,128)(2,1)S(1)} %bitcast.49), channel_id=1, source_target_pairs={{0,224},{32,0},{64,32},{96,64},{128,96},{160,128},{192,160},{224,1... | collective-permute-start | bytes 3145736 | tf_op jit(solution)/shard_map/ppermute | solution.py:22
  90.5 27.3 %collective-permute-start.2 = (bf16[32,256,128]{2,1,0:T(8,128)(2,1)}, bf16[32,256,128]{2,1,0:T(8,128)(2,1)}, u32[]{:S(2)}, u32[]{:S(2)}) collective-permute-start(bf16[32,256,128]{2,1,0:T(8,128)(2,1)} %all-to-all-done), channel_id=1, source_target_pairs={{0,224},{32,0},{64,32},{96,64},{128,96},{160,128},{192,160},{224,1... | collective-permute-start | bytes 6291464 | tf_op jit(solution)/shard_map/ppermute | solution.py:22
  103.5 37.4 %all-to-all-start.3 = ((bf16[32,128,128]{2,1,0:T(8,128)(2,1)}), bf16[32,128,128]{2,1,0:T(8,128)(2,1)}, u32[]{:S(2)}, u32[]{:S(2)}) async-start(bf16[32,128,128]{2,1,0:T(8,128)(2,1)} %collective-permute-done.1), calls=%async_computation.3 | async-start | bytes 2097152 | tf_op jit(solution)/shard_map/all_to_all | solution.py:241
  113.9 36.3 %copy-start = (f32[4096,1]{1,0:T(8,128)S(1)}, f32[4096,1]{1,0:T(8,128)}, u32[]{:S(2)}) copy-start(f32[4096,1]{1,0:T(8,128)} %copy.74.corr_ref) | copy-start | bytes 49156
  137.4 1.3 copy-start.1
  138.7 1.4 copy-start.2
  140.1 0.8 copy-start.3
  140.9 31.9 %all-to-all-start.2 = ((bf16[32,64,128]{2,1,0:T(8,128)(2,1)}), bf16[32,64,128]{2,1,0:T(8,128)(2,1)S(1)}, u32[]{:S(2)}, u32[]{:S(2)}) async-start(bf16[32,64,128]{2,1,0:T(8,128)(2,1)} %copy-done.3), calls=%async_computation.2 | async-start | bytes 1048576 | tf_op jit(solution)/shard_map/all_to_all | solution.py:252
  172.8 71.7 %copy-start.5 = (bf16[32,64,128]{2,1,0:T(8,128)(2,1)}, bf16[32,64,128]{2,1,0:T(8,128)(2,1)S(1)}, u32[]{:S(2)}) copy-start(bf16[32,64,128]{2,1,0:T(8,128)(2,1)S(1)} %all-to-all-done.2.first_ref) | copy-start | bytes 1572868
